TPU v7x, 128 devices: a whole 4x4x4 slice. The times are simulated.
128 devices in a mesh: seg: 16 (over x_hi, z, core), chan: 8 (over y, x_lo).
Axes of the slice: x: 4 (x_hi: 2, x_lo: 2; x = x_hi * 2 + x_lo), y: 4, z: 4, core: 2. Of those that a mesh axis runs over, the one named last changes fastest.
Arguments:
- signal: bfloat16 [4096, 32768], P('chan', 'seg'), may hold values from -64 to 64
- spatial: float32 [4096, 64], P('chan'), may hold values from -0.09375 to 0.09375
- temporal: float32 [64, 256], replicated, may hold values from -5 to 5
- start_codes: float32 [64, 32768], P(None, 'seg'), may hold values from -1.2 to 1.2
- thresholds: float32 [64], replicated, may hold values from 0.05 to 0.3
- step_sizes: float32 [64], replicated, may hold values from 0.03 to 0.1
- breaks: int32 [16], replicated, may hold values from 0 to 32767, as said below
Outputs:
- final_codes: float32 [64, 32768], P(None, 'seg')
- space_atoms: float32 [4096, 64], P('chan')
- time_atoms: float32 [64, 256], replicated
Inputs may be any that keep to these rules, and one draw needn't show every extreme that they name: `breaks`: Increasing; one break lies in each of the 16 equal stretches of the window.
All inputs are finite; a program needn't handle non-finite values.
Results may differ from a plain program's by a relative error of at most 0.0058.
Values may be sent and summed in bfloat16 or wider, within the bound.
No kernel may reach another device: no remote copies, remote signals or barrier semaphores. Data moves between devices by JAX's collectives and lax.ppermute only.
A program may use at most 128 MiB of HBM per device.

v0:
```python
import jax
import jax.numpy as jnp
from jax import lax
from jax.sharding import PartitionSpec as P

ITERS = 10
OUTER = 2


epsilon = 1e-06
highest = lax.Precision.HIGHEST


def passed_along(value, axis, steps):
    count = lax.axis_size(axis)
    leading, last = (max(0, -steps), min(count, count - steps))
    return lax.ppermute(value, axis, [(source, source + steps) for source in range(leading, last)])


def skewed(padded, row_total):
    atoms_here, period = padded.shape
    repeated = jnp.broadcast_to(padded[:, None, :], (atoms_here, row_total, period))
    flattened = repeated.reshape(atoms_here, row_total * period)[:, : row_total * (period - 1)]
    return flattened.reshape(atoms_here, row_total, period - 1)[:, :, :row_total]


def toeplitz(kernel_taps, block_width):
    atoms_here, tap_count = kernel_taps.shape
    zero_pad = jnp.zeros((atoms_here, block_width), kernel_taps.dtype)
    padded = jnp.concatenate([zero_pad, kernel_taps, zero_pad], axis=1)
    matrices = []
    for offset in range(tap_count // block_width + 1):
        earlier = padded[:, offset * block_width : (offset + 1) * block_width]
        current = padded[:, (offset + 1) * block_width : (offset + 2) * block_width]
        matrices.append(skewed(jnp.concatenate([current, earlier], axis=1), block_width))
    return matrices


def convolve_blocks(matrices, code_rows, before, block_width):
    atoms_here, seg_len = code_rows.shape
    block_count = seg_len // block_width
    lag_blocks = len(matrices) - 1
    extended = jnp.concatenate([before, code_rows], axis=1).reshape(
        atoms_here, block_count + lag_blocks, block_width
    )
    summed = jnp.zeros((atoms_here, block_count, block_width), jnp.float32)
    for offset, matrix in enumerate(matrices):
        window = extended[:, lag_blocks - offset : lag_blocks - offset + block_count]
        summed = summed + jnp.einsum(
            "kbm,kmi->kbi", window, matrix, preferred_element_type=jnp.float32, precision=highest
        )
    return summed.reshape(atoms_here, seg_len)


def correlate_blocks(matrices, residual_b, after_rim, block_width):
    atoms_here, seg_len = residual_b.shape
    block_count = seg_len // block_width
    extended = jnp.concatenate([residual_b, after_rim], axis=1).reshape(
        atoms_here, block_count + len(matrices) - 1, block_width
    )
    summed = jnp.zeros((atoms_here, block_count, block_width), jnp.float32)
    for offset, matrix in enumerate(matrices):
        window = extended[:, offset : offset + block_count]
        summed = summed + jnp.einsum(
            "kbi,kmi->kbm", window, matrix, preferred_element_type=jnp.float32, precision=highest
        )
    return summed.reshape(atoms_here, seg_len)


def reconstruct(matrices, latent_rows, block_width, tap_count):
    latent_b = latent_rows.astype(jnp.bfloat16)
    before = passed_along(latent_b[:, latent_b.shape[1] - tap_count :], "seg", 1)
    return (convolve_blocks(matrices, latent_b, before, block_width), before)


def on_device(signal, spatial, temporal, start_codes, thresholds, step_sizes, breaks):
    chan_rows, seg_len = signal.shape
    atoms_all, tap_count = temporal.shape
    block_width = 128
    positions = lax.axis_index("seg") * seg_len + lax.iota(jnp.int32, seg_len)
    crosses = (positions[None, :] < breaks[:, None]) & (
        breaks[:, None] < positions[None, :] + tap_count
    )
    allowed = jnp.where(jnp.any(crosses, axis=0), 0.0, 1.0).astype(jnp.float32)
    raw_start = lax.psum(jnp.dot(spatial.T, spatial, precision=highest), "chan")
    scaling = 1.0 / jnp.sqrt(jnp.diag(raw_start) + epsilon)
    space_loc = spatial * scaling[None, :]
    gram_matrix = raw_start * scaling[:, None] * scaling[None, :]
    kernel = temporal / jnp.sqrt(jnp.sum(temporal * temporal, axis=1, keepdims=True) + epsilon)
    latent = start_codes
    rows_share = chan_rows // lax.axis_size("seg")
    for sweep_index in range(OUTER):
        space_b = space_loc.astype(jnp.bfloat16)
        kernel_b = kernel.astype(jnp.bfloat16)
        projected = lax.psum(jnp.dot(space_b.T, signal, preferred_element_type=jnp.float32), "chan")
        own_gram = gram_matrix
        own_latent = latent

        def mix_atoms(rebuilt_part):
            return jnp.dot(own_gram, rebuilt_part, precision=highest)

        matrices = toeplitz(kernel_b, block_width)
        step_col = step_sizes[:, None]
        limit_col = (step_sizes * thresholds)[:, None]

        def shrink_step(iteration, current):
            rebuilt, before_now = reconstruct(matrices, current, block_width, tap_count)
            residual = projected - mix_atoms(rebuilt)
            residual_b = residual.astype(jnp.bfloat16)
            after_rim = passed_along(residual_b[:, :tap_count], "seg", -1)
            descent = correlate_blocks(matrices, residual_b, after_rim, block_width)
            stepped = current + step_col * descent
            return (
                allowed[None, :]
                * jnp.sign(stepped)
                * jnp.maximum(jnp.abs(stepped) - limit_col, 0.0)
            )

        own_latent = lax.fori_loop(0, ITERS, shrink_step, own_latent)
        rebuilt, before = reconstruct(matrices, own_latent, block_width, tap_count)
        latent = own_latent
        latent_b = latent.astype(jnp.bfloat16)
        rebuilt_b = rebuilt.astype(jnp.bfloat16)
        stats_rows = lax.psum_scatter(
            jnp.dot(signal, rebuilt_b.T, preferred_element_type=jnp.float32),
            "seg",
            scatter_dimension=0,
            tiled=True,
        )
        others = projected - jnp.dot(
            gram_matrix - jnp.diag(jnp.diag(gram_matrix)), rebuilt, precision=highest
        )

        def convolve_kernel(kernel_wide):
            return convolve_blocks(
                toeplitz(kernel_wide, block_width),
                latent_b.astype(jnp.float32),
                before.astype(jnp.float32),
                block_width,
            )

        primal, pullback = jax.vjp(convolve_kernel, kernel)
        (taps_part,) = pullback(others)
        cross_gram, raw_kernel = lax.psum(
            (jnp.dot(rebuilt, rebuilt.T, precision=highest), taps_part), "seg"
        )
        seg_first = lax.axis_index("seg") * rows_share
        own_space = lax.dynamic_slice_in_dim(space_loc, seg_first, rows_share, 0)
        raw_rows = stats_rows - jnp.dot(
            own_space, cross_gram - jnp.diag(jnp.diag(cross_gram)), precision=highest
        )
        squares = lax.psum(jnp.sum(raw_rows * raw_rows, axis=0), ("seg", "chan"))
        new_rows = raw_rows / jnp.sqrt(squares + epsilon)[None, :]
        space_loc = lax.all_gather(new_rows, "seg", axis=0, tiled=True)
        if sweep_index + 1 < OUTER:
            gram_matrix = lax.psum(jnp.dot(space_loc.T, space_loc, precision=highest), "chan")
        kernel = raw_kernel / jnp.sqrt(
            jnp.sum(raw_kernel * raw_kernel, axis=1, keepdims=True) + epsilon
        )
    return (latent, space_loc, kernel)


def solution(mesh):
    placed = (P("chan", "seg"), P("chan", None), P(), P(None, "seg"), P(), P(), P())
    return jax.shard_map(
        on_device,
        mesh=mesh,
        in_specs=placed,
        out_specs=(P(None, "seg"), P("chan", None), P()),
        check_vma=False,
    )
```

profile of v0, /device:TPU:4, one launch (start us, length us, event | category | flops | bytes accessed | tf_op | source)
XLA Modules:
  0.0 1486.9 jit_solution(3020994345920446049)
XLA Ops:
  8.6 34.3 %psum.70 = f32[64,64]{1,0:T(8,128)S(1)} all-reduce(f32[64,64]{1,0:T(8,128)S(1)} %fusion.98), channel_id=1, replica_groups=mesh['seg'=16,'chan'=8] {'chan'}, use_global_device_ids=true, to_apply=%region_1.2 | all-reduce | flops 4096 | bytes 32768 | tf_op jit(solution)/shard_map/psum | solution.py:85
  51.5 16.3 %reshape.190 = bf16[64,128,255]{2,1,0:T(8,128)(2,1)} reshape(bf16[64,32640]{1,0:T(8,128)(2,1)} %slice.200) | data formatting | bytes 8355840 | tf_op jit(solution)/shard_map/reshape | solution.py:24
  76.2 15.8 %reshape.192 = bf16[64,128,255]{2,1,0:T(8,128)(2,1)} reshape(bf16[64,32640]{1,0:T(8,128)(2,1)} %slice.204) | data formatting | bytes 8355840 | tf_op jit(solution)/shard_map/reshape | solution.py:24
  100.3 16.0 %reshape.194 = bf16[64,128,255]{2,1,0:T(8,128)(2,1)} reshape(bf16[64,32640]{1,0:T(8,128)(2,1)} %slice.206) | data formatting | bytes 8355840 | tf_op jit(solution)/shard_map/reshape | solution.py:24
  121.3 263.8 %while.20 = (s32[]{:T(128)}, f32[64,2048]{1,0:T(8,128)S(1)}, f32[2048]{0:T(1024)S(1)}, f32[64,1]{0,1:T(1,128)S(1)}, bf16[64,128,128]{2,1,0:T(8,128)(2,1)}, /*ind...) while((s32[]{:T(128)}, f32[64,2048]{1,0:T(8,128)S(1)}, ...), condition=%wide.region_5.6_spmd, body=%wide.region_4.5_spmd.sunk | while | flops 305135616 | bytes 44720912 | solution.py:119
  123.3 6.9 collective-permute-done
  149.7 6.9 collective-permute-done
  176.1 6.9 collective-permute-done
  202.5 6.9 collective-permute-done
  228.9 6.9 collective-permute-done
  255.2 6.9 collective-permute-done
  281.6 6.9 collective-permute-done
  308.0 6.9 collective-permute-done
  334.4 6.9 collective-permute-done
  360.8 6.9 collective-permute-done
  388.0 6.1 collective-permute-done.4
  404.0 3.6 fusion.44
  407.7 3.4 fusion.52
  411.8 4.3 pad.84
  416.1 9.3 reshape.203
  425.4 4.0 pad.85
  434.1 4.3 pad.80
  438.5 9.6 reshape.201
  448.1 4.0 pad.81
  456.9 4.3 pad.76
  461.2 9.3 reshape.199
  470.4 4.0 pad.77
  480.8 65.1 %psum.73 = f32[64,64]{1,0:T(8,128)S(1)} all-reduce(f32[64,64]{1,0:T(8,128)S(1)} %convolution_bitcast_fusion.5), channel_id=1, replica_groups=mesh['seg'=16,'chan'=8] {'seg'}, use_global_device_ids=true, to_apply=%region_12.13 | all-reduce | flops 4096 | bytes 32768 | tf_op jit(solution)/shard_map/psum | solution.py:144
  546.8 55.0 %all-reduce.33.cloned.1.call-done = f32[64,256]{1,0:T(8,128)} async-done(((f32[64,256]{1,0:T(8,128)}), f32[64,256]{1,0:T(8,128)}) %all-reduce.33.cloned.1.call-update) | async-done | bytes 65552 | tf_op jit(solution)/shard_map/psum | solution.py:144
  608.9 15.8 %reshape.206 = bf16[64,128,255]{2,1,0:T(8,128)(2,1)} reshape(bf16[64,32640]{1,0:T(8,128)(2,1)} %slice.211) | data formatting | bytes 8355840 | tf_op jit(solution)/shard_map/reshape | solution.py:24
  628.0 44.8 %reduce-scatter.7.cloned.1.call-done = f32[32,64]{1,0:T(8,128)} async-done(((f32[512,64]{1,0:T(8,128)}), f32[32,64]{1,0:T(8,128)}) %reduce-scatter.7.cloned.1.call-update) | async-done | bytes 8208 | tf_op jit(solution)/shard_map/reduce_scatter | solution.py:124
  673.8 63.9 %psum.74 = f32[64]{0:T(128)S(1)} all-reduce(f32[64]{0:T(128)S(1)} %get-tuple-element.179), channel_id=1, replica_groups=mesh['seg'=16,'chan'=8] {'seg','chan'}, use_global_device_ids=true, to_apply=%region_14.15 | all-reduce | flops 64 | bytes 512 | tf_op jit(solution)/shard_map/psum | solution.py:152
  737.7 21.3 %all_gather.6 = f32[512,64]{1,0:T(8,128)S(1)} all-gather(f32[32,64]{1,0:T(8,128)S(1)} %broadcast_divide_fusion.2), channel_id=1, replica_groups=mesh['seg'=16,'chan'=8] {'seg'}, dimensions={0}, use_global_device_ids=true | all-gather | bytes 139264 | tf_op jit(solution)/shard_map/all_gather | solution.py:154
  765.6 16.0 %reshape.208 = bf16[64,128,255]{2,1,0:T(8,128)(2,1)} reshape(bf16[64,32640]{1,0:T(8,128)(2,1)} %slice.215) | data formatting | bytes 8355840 | tf_op jit(solution)/shard_map/reshape | solution.py:24
  789.8 15.8 %reshape.210 = bf16[64,128,255]{2,1,0:T(8,128)(2,1)} reshape(bf16[64,32640]{1,0:T(8,128)(2,1)} %slice.217) | data formatting | bytes 8355840 | tf_op jit(solution)/shard_map/reshape | solution.py:24
  809.5 33.6 %psum.75 = f32[64,64]{1,0:T(8,128)S(1)} all-reduce(f32[64,64]{1,0:T(8,128)S(1)} %fusion.99), channel_id=1, replica_groups=mesh['seg'=16,'chan'=8] {'chan'}, use_global_device_ids=true, to_apply=%region_15.16 | all-reduce | flops 4096 | bytes 32768 | tf_op jit(solution)/shard_map/psum | solution.py:156
  843.0 263.8 %while.21 = (s32[]{:T(128)}, f32[64,2048]{1,0:T(8,128)S(1)}, f32[2048]{0:T(1024)S(1)}, f32[64,1]{0,1:T(1,128)S(1)}, bf16[64,128,128]{2,1,0:T(8,128)(2,1)}, /*ind...) while((s32[]{:T(128)}, f32[64,2048]{1,0:T(8,128)S(1)}, ...), condition=%wide.region_18.19_spmd, body=%wide.region_17.18_spmd.sunk | while | flops 305135616 | bytes 44720912 | solution.py:119
  845.0 6.9 collective-permute-done.2
  871.4 6.9 collective-permute-done.2
  897.8 6.9 collective-permute-done.2
  924.2 6.9 collective-permute-done.2
  950.6 6.9 collective-permute-done.2
  977.0 6.9 collective-permute-done.2
  1003.3 6.9 collective-permute-done.2
  1029.7 6.9 collective-permute-done.2
  1056.1 6.9 collective-permute-done.2
  1082.5 6.9 collective-permute-done.2
  1109.7 6.1 collective-permute-done.5
  1126.6 3.6 fusion.37
  1130.2 3.4 fusion.34
  1133.6 4.3 pad.96
  1137.9 9.3 reshape.219
  1147.2 4.0 pad.97
  1155.9 4.3 pad.92
  1160.2 9.4 reshape.217
  1169.7 4.0 pad.93
  1178.4 4.3 pad.88
  1182.8 9.3 reshape.215
  1192.0 4.0 pad.89
  1202.4 65.0 %psum.77 = f32[64,64]{1,0:T(8,128)S(1)} all-reduce(f32[64,64]{1,0:T(8,128)S(1)} %convolution_bitcast_fusion.4), channel_id=1, replica_groups=mesh['seg'=16,'chan'=8] {'seg'}, use_global_device_ids=true, to_apply=%region_20.21 | all-reduce | flops 4096 | bytes 32768 | tf_op jit(solution)/shard_map/psum | solution.py:144
  1268.2 54.5 %all-reduce.37.cloned.1.call-done = f32[64,256]{1,0:T(8,128)} async-done(((f32[64,256]{1,0:T(8,128)}), f32[64,256]{1,0:T(8,128)}) %all-reduce.37.cloned.1.call-update) | async-done | bytes 65552 | tf_op jit(solution)/shard_map/psum | solution.py:144
  1325.2 67.6 %reduce-scatter.9.cloned.1.call-done = f32[32,64]{1,0:T(8,128)} async-done(((f32[512,64]{1,0:T(8,128)}), f32[32,64]{1,0:T(8,128)}) %reduce-scatter.9.cloned.1.call-update) | async-done | bytes 8208 | tf_op jit(solution)/shard_map/reduce_scatter | solution.py:124
  1393.8 63.9 %psum.78 = f32[64]{0:T(128)S(1)} all-reduce(f32[64]{0:T(128)S(1)} %get-tuple-element.181), channel_id=1, replica_groups=mesh['seg'=16,'chan'=8] {'seg','chan'}, use_global_device_ids=true, to_apply=%region_22.23 | all-reduce | flops 64 | bytes 512 | tf_op jit(solution)/shard_map/psum | solution.py:152
  1457.7 21.3 %all_gather.7 = f32[512,64]{1,0:T(8,128)S(1)} all-gather(f32[32,64]{1,0:T(8,128)S(1)} %broadcast_divide_fusion.1), channel_id=1, replica_groups=mesh['seg'=16,'chan'=8] {'seg'}, dimensions={0}, use_global_device_ids=true | all-gather | bytes 139264 | tf_op jit(solution)/shard_map/all_gather | solution.py:154
  (651 shorter events, 512.3 us)
Async XLA Ops:
  7.2 37.6 %copy-start = (bf16[512,2048]{1,0:T(8,128)(2,1)S(1)}, bf16[512,2048]{1,0:T(8,128)(2,1)}, u32[]{:S(2)}) copy-start(bf16[512,2048]{1,0:T(8,128)(2,1)} %param.11) | copy-start | bytes 6291460
  7.2 39.1 %copy-start.27 = (pred[256]{0:T(512)(128)(4,1)S(1)}, pred[256]{0:T(512)(128)(4,1)}, u32[]{:S(2)}) copy-start(pred[256]{0:T(512)(128)(4,1)} %constant.51.clone.1) | copy-start | bytes 772
  7.2 39.0 %copy-start.23 = (f32[64,256]{1,0:T(8,128)S(1)}, f32[64,256]{1,0:T(8,128)}, u32[]{:S(2)}) copy-start(f32[64,256]{1,0:T(8,128)} %param.13) | copy-start | bytes 196612
  7.2 114.1 %all-reduce.31.cloned.1.call-start = ((), (), s32[]{:S(2)}) async-start(), calls=%async_computation.2 | async-start | bytes 1048576 | tf_op jit(solution)/shard_map/psum | solution.py:95
  46.1 555.8 %all-reduce.33.cloned.1.call-start = ((), (), s32[]{:S(2)}) async-start(), calls=%async_computation.3 | async-start | bytes 131072 | tf_op jit(solution)/shard_map/psum | solution.py:144
  121.4 8.8 collective-permute-start
  136.6 3.5 collective-permute-start.1
  140.3 5.7 copy-start.4
  147.8 8.9 collective-permute-start
  163.0 3.5 collective-permute-start.1
  174.2 8.9 collective-permute-start
  189.3 3.5 collective-permute-start.1
  200.5 8.9 collective-permute-start
  215.7 3.5 collective-permute-start.1
  219.4 5.7 copy-start.4
  226.9 8.9 collective-permute-start
  242.1 3.5 collective-permute-start.1
  253.3 8.9 collective-permute-start
  268.5 3.5 collective-permute-start.1
  272.2 5.7 copy-start.4
  279.7 8.9 collective-permute-start
  294.9 3.5 collective-permute-start.1
  298.6 5.7 copy-start.4
  306.1 8.9 collective-permute-start
  321.3 3.5 collective-permute-start.1
  332.5 8.9 collective-permute-start
  347.7 3.5 collective-permute-start.1
  358.9 8.9 collective-permute-start
  374.0 3.5 collective-permute-start.1
  385.2 15.4 %copy-start.25 = (f32[64,1]{0,1:T(1,128)}, f32[64,1]{0,1:T(1,128)S(1)}, u32[]{:S(2)}) copy-start(f32[64,1]{0,1:T(1,128)S(1)} %get-tuple-element.409) | copy-start | bytes 772
  385.2 8.9 collective-permute-start.4
  401.3 9.8 copy-start.19
  479.2 193.5 %reduce-scatter.7.cloned.1.call-start = ((), (), s32[]{:S(2)}) async-start(), calls=%async_computation.6 | async-start | bytes 278528 | tf_op jit(solution)/shard_map/reduce_scatter | solution.py:124
  546.8 296.3 %all-reduce.35.cloned.1.call-start = ((), (), s32[]{:S(2)}) async-start(), calls=%async_computation.4 | async-start | bytes 1048576 | tf_op jit(solution)/shard_map/psum | solution.py:95
  759.0 49.9 %copy-start.21 = (f32[512,64]{1,0:T(8,128)}, f32[512,64]{1,0:T(8,128)S(1)}, u32[]{:S(2)}) copy-start(f32[512,64]{1,0:T(8,128)S(1)} %all_gather.6) | copy-start | bytes 393220
  760.3 562.4 %all-reduce.37.cloned.1.call-start = ((), (), s32[]{:S(2)}) async-start(), calls=%async_computation.5 | async-start | bytes 131072 | tf_op jit(solution)/shard_map/psum | solution.py:144
  805.7 37.4 %copy-start.26 = (f32[64,1]{0,1:T(1,128)S(1)}, f32[64,1]{0,1:T(1,128)}, u32[]{:S(2)}) copy-start(f32[64,1]{0,1:T(1,128)} %copy-done.25) | copy-start | bytes 772
  843.1 8.8 collective-permute-start.2
  858.3 3.5 collective-permute-start.3
  862.0 5.7 copy-start.6
  869.5 8.9 collective-permute-start.2
  884.7 3.5 collective-permute-start.3
  895.9 8.9 collective-permute-start.2
  911.1 3.5 collective-permute-start.3
  914.8 5.7 copy-start.6
  922.3 8.9 collective-permute-start.2
  937.4 3.5 collective-permute-start.3
  941.1 5.7 copy-start.6
  948.6 8.9 collective-permute-start.2
  963.8 3.5 collective-permute-start.3
  975.0 8.9 collective-permute-start.2
  990.2 3.5 collective-permute-start.3
  1001.4 8.9 collective-permute-start.2
  1016.6 3.5 collective-permute-start.3
  1027.8 8.9 collective-permute-start.2
  1043.0 3.5 collective-permute-start.3
  1054.2 8.9 collective-permute-start.2
  1069.4 3.5 collective-permute-start.3
  1080.6 8.9 collective-permute-start.2
  1095.8 3.5 collective-permute-start.3
  1099.5 5.7 copy-start.6
  1106.9 15.5 %copy-start.1 = (f32[64,2048]{1,0:T(8,128)}, f32[64,2048]{1,0:T(8,128)S(1)}, u32[]{:S(2)}) copy-start(f32[64,2048]{1,0:T(8,128)S(1)} %get-tuple-element.112) | copy-start | bytes 1572868
  1107.0 8.9 collective-permute-start.5
  1200.8 192.0 %reduce-scatter.9.cloned.1.call-start = ((), (), s32[]{:S(2)}) async-start(), calls=%async_computation.7 | async-start | bytes 278528 | tf_op jit(solution)/shard_map/reduce_scatter | solution.py:124
  (68 other events, 323.4 us)
Sparse Core Ops, SparseCore 0:
  46.2 75.1 all-reduce.30
  479.3 122.4 all-reduce.32
  606.1 66.5 reduce-scatter.6
  760.5 73.7 all-reduce.34
  1200.9 121.7 all-reduce.36
  1326.2 66.5 reduce-scatter.8
where the time goes:
time: 1500 us; the launch traced here: 1490 us
  waiting for transfers between devices  406 us (27%)
  blocking collectives  368 us (25%)
  matrix products  300 us (20%)
  local copies, waits for them, and re-layouts  286 us (19%)
  starting transfers between devices  80.9 us (5%)
  other arithmetic  28.6 us (2%)
  between operations  15.1 us (1%)
    ppermute x42, waiting for transfers between devices, passed_along(): lax.ppermute(value, axis, [(source, source + steps) for source in range(l...  182 us
    reshape x12, local copies, waits for them, and re-layouts, skewed(): flattened.reshape(atoms_here, row_total, period - 1)[:, :, :row_total]  152 us
    dot_general x60, matrix products, correlate_blocks(): jnp.einsum('kbi,kmi->kbm', window, matrix, preferred_element_type=jnp.flo...  139 us
    dot_general x72, matrix products, convolve_blocks(): jnp.einsum('kbm,kmi->kbi', window, matrix, preferred_element_type=jnp.flo...  135 us
    psum x2, blocking collectives, on_device(): lax.psum((jnp.dot(rebuilt, rebuilt.T, precision=highest), taps_part), 'seg')  130 us
    psum x2, blocking collectives, on_device(): squares = lax.psum(jnp.sum(raw_rows * raw_rows, axis=0), ('seg', 'chan'))  128 us
    reduce_scatter x2, waiting for transfers between devices, on_device(): lax.psum_scatter(jnp.dot(signal, rebuilt_b.T, preferred_element_type=jnp....  112 us
    psum x2, waiting for transfers between devices, on_device(): lax.psum((jnp.dot(rebuilt, rebuilt.T, precision=highest), taps_part), 'seg')  110 us
  transfers between devices with their start and end apart: 48, of which 47 were waited for; matrix products, arithmetic and copies ran while one was open for 11% of the time, Pallas kernels for 0%

commit v1 on v0

v1 whole, which is shorter than its diff:
```python
import jax
import jax.numpy as jnp
from jax import lax
from jax.sharding import PartitionSpec as P

ITERS = 10
OUTER = 2


epsilon = 1e-06
highest = lax.Precision.HIGHEST


def passed_along(value, axis, steps):
    count = lax.axis_size(axis)
    leading, last = (max(0, -steps), min(count, count - steps))
    return lax.ppermute(value, axis, [(source, source + steps) for source in range(leading, last)])


def butterfly_sum(value, axis):
    count = lax.axis_size(axis)
    distance = 1
    while distance < count:
        partner = lax.ppermute(value, axis, [(i, i ^ distance) for i in range(count)])
        value = value + partner
        distance *= 2
    return value


def one_hot_skew(block_width, tap_span):
    shape = (tap_span, block_width, block_width)
    d = lax.broadcasted_iota(jnp.int32, shape, 0)
    m = lax.broadcasted_iota(jnp.int32, shape, 1)
    i = lax.broadcasted_iota(jnp.int32, shape, 2)
    hit = d == i - m + (block_width - 1)
    return jnp.where(hit, 1.0, 0.0).astype(jnp.bfloat16).reshape(tap_span, block_width * block_width)


def toeplitz(kernel_taps, block_width, skew):
    atoms_here, tap_count = kernel_taps.shape
    zero_pad = jnp.zeros((atoms_here, block_width), kernel_taps.dtype)
    padded = jnp.concatenate([zero_pad, kernel_taps, zero_pad, zero_pad], axis=1)
    lag_blocks = tap_count // block_width
    tap_span = 2 * block_width
    bands = jnp.concatenate(
        [padded[:, off * block_width + 1 : off * block_width + 1 + tap_span] for off in range(lag_blocks + 1)],
        axis=0,
    )
    flat = jnp.dot(bands, skew, preferred_element_type=jnp.float32).astype(kernel_taps.dtype)
    flat = flat.reshape(lag_blocks + 1, atoms_here, block_width, block_width)
    return [flat[off] for off in range(lag_blocks + 1)]


def lag_sums(code_ext, others, block_width, tap_count, skew):
    atoms_here, seg_len = others.shape
    block_count = seg_len // block_width
    lag_blocks = tap_count // block_width
    extended = code_ext.reshape(atoms_here, block_count + lag_blocks, block_width)
    others_blocks = others.reshape(atoms_here, block_count, block_width)
    grads = []
    for offset in range(lag_blocks + 1):
        window = extended[:, lag_blocks - offset : lag_blocks - offset + block_count]
        grads.append(
            jnp.einsum(
                "kbm,kbi->kmi", window, others_blocks, preferred_element_type=jnp.float32, precision=highest
            )
        )
    stacked = jnp.concatenate(grads, axis=0).reshape((lag_blocks + 1) * atoms_here, block_width * block_width)
    bands = jnp.dot(stacked, skew.astype(jnp.float32).T, precision=highest)
    bands = bands.reshape(lag_blocks + 1, atoms_here, 2 * block_width)
    total = jnp.zeros((atoms_here, tap_count + 3 * block_width), jnp.float32)
    for offset in range(lag_blocks + 1):
        start = offset * block_width + 1
        total = total.at[:, start : start + 2 * block_width].add(bands[offset])
    return total[:, block_width : block_width + tap_count]


def convolve_blocks(matrices, code_rows, before, block_width):
    atoms_here, seg_len = code_rows.shape
    block_count = seg_len // block_width
    lag_blocks = len(matrices) - 1
    extended = jnp.concatenate([before, code_rows], axis=1).reshape(
        atoms_here, block_count + lag_blocks, block_width
    )
    summed = jnp.zeros((atoms_here, block_count, block_width), jnp.float32)
    for offset, matrix in enumerate(matrices):
        window = extended[:, lag_blocks - offset : lag_blocks - offset + block_count]
        summed = summed + jnp.einsum(
            "kbm,kmi->kbi", window, matrix, preferred_element_type=jnp.float32, precision=highest
        )
    return summed.reshape(atoms_here, seg_len)


def correlate_blocks(matrices, residual_b, after_rim, block_width):
    atoms_here, seg_len = residual_b.shape
    block_count = seg_len // block_width
    extended = jnp.concatenate([residual_b, after_rim], axis=1).reshape(
        atoms_here, block_count + len(matrices) - 1, block_width
    )
    summed = jnp.zeros((atoms_here, block_count, block_width), jnp.float32)
    for offset, matrix in enumerate(matrices):
        window = extended[:, offset : offset + block_count]
        summed = summed + jnp.einsum(
            "kbi,kmi->kbm", window, matrix, preferred_element_type=jnp.float32, precision=highest
        )
    return summed.reshape(atoms_here, seg_len)


def reconstruct(matrices, latent_rows, block_width, tap_count):
    latent_b = latent_rows.astype(jnp.bfloat16)
    before = passed_along(latent_b[:, latent_b.shape[1] - tap_count :], "seg", 1)
    return (convolve_blocks(matrices, latent_b, before, block_width), before, latent_b)


def on_device(signal, spatial, temporal, start_codes, thresholds, step_sizes, breaks):
    chan_rows, seg_len = signal.shape
    atoms_all, tap_count = temporal.shape
    block_width = 128
    skew = one_hot_skew(block_width, 2 * block_width)
    positions = lax.axis_index("seg") * seg_len + lax.iota(jnp.int32, seg_len)
    crosses = (positions[None, :] < breaks[:, None]) & (
        breaks[:, None] < positions[None, :] + tap_count
    )
    allowed = jnp.where(jnp.any(crosses, axis=0), 0.0, 1.0).astype(jnp.float32)
    raw_start = butterfly_sum(jnp.dot(spatial.T, spatial, precision=highest), "chan")
    scaling = 1.0 / jnp.sqrt(jnp.diag(raw_start) + epsilon)
    space_loc = spatial * scaling[None, :]
    gram_matrix = raw_start * scaling[:, None] * scaling[None, :]
    kernel = temporal / jnp.sqrt(jnp.sum(temporal * temporal, axis=1, keepdims=True) + epsilon)
    latent = start_codes
    for sweep_index in range(OUTER):
        space_b = space_loc.astype(jnp.bfloat16)
        kernel_b = kernel.astype(jnp.bfloat16)
        projected = butterfly_sum(
            jnp.dot(space_b.T, signal, preferred_element_type=jnp.float32), "chan"
        )
        own_gram = gram_matrix

        def mix_atoms(rebuilt_part):
            return jnp.dot(own_gram, rebuilt_part, precision=highest)

        matrices = toeplitz(kernel_b, block_width, skew)
        step_col = step_sizes[:, None]
        limit_col = (step_sizes * thresholds)[:, None]

        def shrink_step(iteration, current):
            rebuilt, _, _ = reconstruct(matrices, current, block_width, tap_count)
            residual = projected - mix_atoms(rebuilt)
            residual_b = residual.astype(jnp.bfloat16)
            after_rim = passed_along(residual_b[:, :tap_count], "seg", -1)
            descent = correlate_blocks(matrices, residual_b, after_rim, block_width)
            stepped = current + step_col * descent
            return (
                allowed[None, :]
                * jnp.sign(stepped)
                * jnp.maximum(jnp.abs(stepped) - limit_col, 0.0)
            )

        latent = lax.fori_loop(0, ITERS, shrink_step, latent)
        rebuilt, before, latent_b = reconstruct(matrices, latent, block_width, tap_count)
        rebuilt_b = rebuilt.astype(jnp.bfloat16)
        row_part = jnp.dot(signal, rebuilt_b.T, preferred_element_type=jnp.float32)
        others = projected - jnp.dot(
            gram_matrix - jnp.diag(jnp.diag(gram_matrix)), rebuilt, precision=highest
        )
        code_ext = jnp.concatenate([before, latent_b], axis=1)
        taps_part = lag_sums(code_ext, others, block_width, tap_count, skew)
        cross_part = jnp.dot(rebuilt, rebuilt.T, precision=highest)
        joined = butterfly_sum(jnp.concatenate([row_part, cross_part, taps_part.T], axis=0), "seg")
        stats_rows = joined[:chan_rows]
        cross_gram = joined[chan_rows : chan_rows + atoms_all]
        raw_kernel = joined[chan_rows + atoms_all :].T
        raw_rows = stats_rows - jnp.dot(
            space_loc, cross_gram - jnp.diag(jnp.diag(cross_gram)), precision=highest
        )
        raw_gram = butterfly_sum(jnp.dot(raw_rows.T, raw_rows, precision=highest), "chan")
        scaling = 1.0 / jnp.sqrt(jnp.diag(raw_gram) + epsilon)
        space_loc = raw_rows * scaling[None, :]
        gram_matrix = raw_gram * scaling[:, None] * scaling[None, :]
        kernel = raw_kernel / jnp.sqrt(
            jnp.sum(raw_kernel * raw_kernel, axis=1, keepdims=True) + epsilon
        )
    return (latent, space_loc, kernel)


def solution(mesh):
    placed = (P("chan", "seg"), P("chan", None), P(), P(None, "seg"), P(), P(), P())
    return jax.shard_map(
        on_device,
        mesh=mesh,
        in_specs=placed,
        out_specs=(P(None, "seg"), P("chan", None), P()),
        check_vma=False,
    )
```

time: 1500 us -> 842 us (0.56)
  blocking collectives: 368 us -> 0 us
  local copies, waits for them, and re-layouts: 286 us -> 40.2 us
  waiting for transfers between devices: 406 us -> 310 us
  matrix products: 300 us -> 335 us
  starting transfers between devices: 80.9 us -> 109 us
    psum x6 -> x0, blocking collectives: 326 us -> none  [the longest x2 130 us: on_device(): lax.psum((jnp.dot(rebuilt, rebuilt.T, precision=highest), taps_part), 'seg')]
    reshape x12 -> x0, local copies, waits for them, and re-layouts: 152 us -> none  [skewed(): flattened.reshape(atoms_here, row_total, period - 1)[:, :, :row_total]]
    ppermute x0 -> x23, waiting for transfers between devices: none -> 130 us  [butterfly_sum(): lax.ppermute(value, axis, [(i, i ^ distance) for i in range(count)])]
    reduce_scatter x2 -> x0, waiting for transfers between devices: 112 us -> none  [on_device(): lax.psum_scatter(jnp.dot(signal, rebuilt_b.T, preferred_element_type=jnp....]
    psum x4 -> x0, waiting for transfers between devices: 111 us -> none  [the longest x2 110 us: on_device(): lax.psum((jnp.dot(rebuilt, rebuilt.T, precision=highest), taps_part), 'seg')]
    dot_general x8 -> x19, matrix products: 6.94 us -> 59.7 us  [the longest x2 36.8 us: lag_sums(): bands = jnp.dot(stacked, skew.astype(jnp.float32).T, precision=highest)]
    pad x12 -> x0, local copies, waits for them, and re-layouts: 50.1 us -> none  [the longest x6 25.9 us: skewed(): flattened.reshape(atoms_here, row_total, period - 1)[:, :, :row_total]]
    all_gather x2 -> x0, blocking collectives: 42.6 us -> none  [on_device(): space_loc = lax.all_gather(new_rows, 'seg', axis=0, tiled=True)]
  transfers between devices with their start and end apart: 48 -> 65, of which waited for: 47 -> 64; matrix products, arithmetic and copies ran while one was open for 11% -> 4% of each run, Pallas kernels for 0% -> 0%
where the time goes in v1:
time: 842 us; the launch traced here: 831 us
  matrix products  335 us (40%)
  waiting for transfers between devices  310 us (37%)
  starting transfers between devices  109 us (13%)
  local copies, waits for them, and re-layouts  40.2 us (5%)
  other arithmetic  32.8 us (4%)
    ppermute x42, waiting for transfers between devices, passed_along(): lax.ppermute(value, axis, [(source, source + steps) for source in range(l...  180 us
    dot_general x60, matrix products, correlate_blocks(): jnp.einsum('kbi,kmi->kbm', window, matrix, preferred_element_type=jnp.flo...  139 us
    ppermute x23, waiting for transfers between devices, butterfly_sum(): lax.ppermute(value, axis, [(i, i ^ distance) for i in range(count)])  130 us
    dot_general x66, matrix products, convolve_blocks(): jnp.einsum('kbm,kmi->kbi', window, matrix, preferred_element_type=jnp.flo...  117 us
    ppermute x42, starting transfers between devices, passed_along(): lax.ppermute(value, axis, [(source, source + steps) for source in range(l...  81 us
    dot_general x2, matrix products, lag_sums(): bands = jnp.dot(stacked, skew.astype(jnp.float32).T, precision=highest)  36.8 us
    ppermute x23, starting transfers between devices, butterfly_sum(): lax.ppermute(value, axis, [(i, i ^ distance) for i in range(count)])  28.3 us
    unnamed x54, local copies, waits for them, and re-layouts  19.4 us
  transfers between devices with their start and end apart: 65, of which 64 were waited for; matrix products, arithmetic and copies ran while one was open for 4% of the time, Pallas kernels for 0%

profile of v1, /device:TPU:4, one launch (start us, length us, event | category | flops | bytes accessed | tf_op | source)
XLA Modules:
  0.0 830.8 jit_solution(11177856804214538211)
XLA Ops:
  9.9 3.2 collective-permute-start.6
  20.8 7.4 collective-permute-done.7
  32.7 3.7 copy.88
  41.4 3.0 collective-permute-start.9
  44.6 7.6 collective-permute-done.9
  53.0 264.1 %while.26 = (s32[]{:T(128)}, f32[64,2048]{1,0:T(8,128)S(1)}, f32[2048]{0:T(1024)S(1)}, f32[64,1]{0,1:T(1,128)S(1)}, bf16[64,128,128]{2,1,0:T(8,128)(2,1)}, /*ind...) while((s32[]{:T(128)}, f32[64,2048]{1,0:T(8,128)S(1)}, ...), condition=%wide.region_3.4_spmd, body=%wide.region_2.3_spmd.sunk | while | flops 305135616 | bytes 44720912 | solution.py:159
  55.0 6.9 collective-permute-done
  72.0 2.9 fusion.226
  81.4 6.9 collective-permute-done
  98.4 2.9 fusion.226
  107.8 6.9 collective-permute-done
  124.8 2.9 fusion.226
  134.2 6.9 collective-permute-done
  151.2 2.9 fusion.226
  160.6 6.9 collective-permute-done
  177.6 2.9 fusion.226
  187.1 6.9 collective-permute-done
  204.0 2.9 fusion.226
  213.5 6.9 collective-permute-done
  230.4 2.9 fusion.226
  239.9 6.9 collective-permute-done
  256.9 2.9 fusion.226
  266.3 6.9 collective-permute-done
  283.3 2.9 fusion.226
  292.7 6.9 collective-permute-done
  309.7 2.9 fusion.226
  322.1 3.9 collective-permute-done.10
  342.5 18.5 %fusion.44 = f32[192,256]{0,1:T(8,128)S(1)} fusion(f32[192,128,128]{2,1,0:T(8,128)S(1)} %pad_maximum_fusion.4), kind=kOutput, calls=%fused_computation.91 | convolution fusion | flops 9684647936 | bytes 12779520 | tf_op jit(solution)/shard_map/dot_general | solution.py:69
  372.5 11.8 %collective-permute-done.12 = f32[832,64]{1,0:T(8,128)S(1)} collective-permute-done((f32[832,64]{1,0:T(8,128)S(1)}, f32[832,64]{1,0:T(8,128)S(1)}, u32[]{:S(2)}, u32[]{:S(2)}) %collective-permute-start.12) | collective-permute-done | bytes 213024 | tf_op jit(solution)/shard_map/ppermute | solution.py:24
  384.5 12.5 %collective-permute-done.13 = f32[832,64]{1,0:T(8,128)S(1)} collective-permute-done((f32[832,64]{1,0:T(8,128)S(1)}, f32[832,64]{1,0:T(8,128)S(1)}, u32[]{:S(2)}, u32[]{:S(2)}) %collective-permute-start.13) | collective-permute-done | bytes 213024 | tf_op jit(solution)/shard_map/ppermute | solution.py:24
  397.2 11.6 %collective-permute-done.14 = f32[832,64]{1,0:T(8,128)S(1)} collective-permute-done((f32[832,64]{1,0:T(8,128)S(1)}, f32[832,64]{1,0:T(8,128)S(1)}, u32[]{:S(2)}, u32[]{:S(2)}) %collective-permute-start.14) | collective-permute-done | bytes 213024 | tf_op jit(solution)/shard_map/ppermute | solution.py:24
  413.7 2.9 collective-permute-done.15
  417.3 3.3 collective-permute-done.16
  429.4 7.2 collective-permute-done.18
  439.3 10.7 %collective-permute-done.19 = f32[64,2048]{1,0:T(8,128)S(1)} collective-permute-done((f32[64,2048]{1,0:T(8,128)S(1)}, f32[64,2048]{1,0:T(8,128)S(1)}, u32[]{:S(2)}, u32[]{:S(2)}) %collective-permute-start.19) | collective-permute-done | bytes 524320 | tf_op jit(solution)/shard_map/ppermute | solution.py:24
  450.1 4.6 collective-permute-start.20
  462.7 264.0 %while.27 = (s32[]{:T(128)}, f32[64,2048]{1,0:T(8,128)S(1)}, f32[2048]{0:T(1024)S(1)}, f32[64,1]{0,1:T(1,128)S(1)}, bf16[64,128,128]{2,1,0:T(8,128)(2,1)}, /*ind...) while((s32[]{:T(128)}, f32[64,2048]{1,0:T(8,128)S(1)}, ...), condition=%wide.region_9.10_spmd, body=%wide.region_8.9_spmd.sunk | while | flops 305135616 | bytes 44720912 | solution.py:159
  464.7 6.9 collective-permute-done.2
  481.7 2.9 fusion.243
  491.1 6.9 collective-permute-done.2
  508.1 2.9 fusion.243
  517.5 6.9 collective-permute-done.2
  534.5 2.9 fusion.243
  543.9 6.9 collective-permute-done.2
  560.9 2.9 fusion.243
  570.3 6.9 collective-permute-done.2
  587.3 2.9 fusion.243
  596.7 6.9 collective-permute-done.2
  613.7 2.9 fusion.243
  623.1 6.9 collective-permute-done.2
  640.1 2.9 fusion.243
  649.6 6.9 collective-permute-done.2
  666.5 2.9 fusion.243
  676.0 6.9 collective-permute-done.2
  692.9 2.9 fusion.243
  702.4 6.9 collective-permute-done.2
  719.3 2.9 fusion.243
  729.8 5.9 collective-permute-done.21
  751.8 18.3 %fusion.47 = f32[192,256]{0,1:T(8,128)S(1)} fusion(f32[192,128,128]{2,1,0:T(8,128)S(1)} %pad_maximum_fusion.5), kind=kOutput, calls=%fused_computation.92 | convolution fusion | flops 9684647936 | bytes 12779520 | tf_op jit(solution)/shard_map/dot_general | solution.py:69
  777.3 11.8 %collective-permute-done.23 = f32[832,64]{1,0:T(8,128)S(1)} collective-permute-done((f32[832,64]{1,0:T(8,128)S(1)}, f32[832,64]{1,0:T(8,128)S(1)}, u32[]{:S(2)}, u32[]{:S(2)}) %collective-permute-start.23) | collective-permute-done | bytes 213024 | tf_op jit(solution)/shard_map/ppermute | solution.py:24
  789.3 12.5 %collective-permute-done.24 = f32[832,64]{1,0:T(8,128)S(1)} collective-permute-done((f32[832,64]{1,0:T(8,128)S(1)}, f32[832,64]{1,0:T(8,128)S(1)}, u32[]{:S(2)}, u32[]{:S(2)}) %collective-permute-start.24) | collective-permute-done | bytes 213024 | tf_op jit(solution)/shard_map/ppermute | solution.py:24
  802.0 11.6 %collective-permute-done.25 = f32[832,64]{1,0:T(8,128)S(1)} collective-permute-done((f32[832,64]{1,0:T(8,128)S(1)}, f32[832,64]{1,0:T(8,128)S(1)}, u32[]{:S(2)}, u32[]{:S(2)}) %collective-permute-start.25) | collective-permute-done | bytes 213024 | tf_op jit(solution)/shard_map/ppermute | solution.py:24
  819.7 3.9 collective-permute-done.27
  823.6 3.4 collective-permute-start.28
  (655 shorter events, 450.7 us)
Async XLA Ops:
  2.0 4.0 collective-permute-start.4
  6.0 3.9 collective-permute-start.5
  9.9 5.4 collective-permute-start.6
  17.6 10.5 %collective-permute-start.7 = (f32[64,2048]{1,0:T(8,128)S(1)}, f32[64,2048]{1,0:T(8,128)S(1)}, u32[]{:S(2)}, u32[]{:S(2)}) collective-permute-start(f32[64,2048]{1,0:T(8,128)S(1)} %fusion.97), channel_id=1, source_target_pairs={{0,1},{1,0},{2,3},{3,2},{4,5},{5,4},{6,7},{7,6},{8,9},{9,8},{10,11... | collective-permute-start | bytes 1572872 | tf_op jit(solution)/shard_map/ppermute | solution.py:24
  28.2 12.1 %collective-permute-start.8 = (f32[64,2048]{1,0:T(8,128)S(1)}, f32[64,2048]{1,0:T(8,128)}, u32[]{:S(2)}, u32[]{:S(2)}) collective-permute-start(f32[64,2048]{1,0:T(8,128)S(1)} %add.295), channel_id=1, source_target_pairs={{0,2},{1,3},{2,0},{3,1},{4,6},{5,7},{6,4},{7,5},{8,10},{9,11},{10,... | collective-permute-start | bytes 1572872 | tf_op jit(solution)/shard_map/ppermute | solution.py:24
  41.4 10.8 %collective-permute-start.9 = (f32[64,2048]{1,0:T(8,128)S(1)}, f32[64,2048]{1,0:T(8,128)S(1)}, u32[]{:S(2)}, u32[]{:S(2)}) collective-permute-start(f32[64,2048]{1,0:T(8,128)S(1)} %add.296), channel_id=1, source_target_pairs={{0,4},{1,5},{2,6},{3,7},{4,0},{5,1},{6,2},{7,3},{8,12},{9,13},{10,... | collective-permute-start | bytes 1572872 | tf_op jit(solution)/shard_map/ppermute | solution.py:24
  53.1 8.8 %collective-permute-start = (bf16[64,256]{1,0:T(8,128)(2,1)S(1)}, bf16[64,256]{1,0:T(8,128)(2,1)S(1)}, u32[]{:S(2)}, u32[]{:S(2)}) collective-permute-start(bf16[64,256]{1,0:T(8,128)(2,1)S(1)} %slice.490), channel_id=1, source_target_pairs={{0,8},{8,16},{16,24},{24,32},{32,40},{40,48},{48,56},{56,64},{64,7... | collective-permute-start | bytes 98312 | tf_op jit(solution)/shard_map/while/body/eval_jaxpr/ppermute | solution.py:17
  68.3 3.5 collective-permute-start.1
  79.5 8.9 %collective-permute-start = (bf16[64,256]{1,0:T(8,128)(2,1)S(1)}, bf16[64,256]{1,0:T(8,128)(2,1)S(1)}, u32[]{:S(2)}, u32[]{:S(2)}) collective-permute-start(bf16[64,256]{1,0:T(8,128)(2,1)S(1)} %slice.490), channel_id=1, source_target_pairs={{0,8},{8,16},{16,24},{24,32},{32,40},{40,48},{48,56},{56,64},{64,7... | collective-permute-start | bytes 98312 | tf_op jit(solution)/shard_map/while/body/eval_jaxpr/ppermute | solution.py:17
  94.7 3.5 collective-permute-start.1
  105.9 8.9 %collective-permute-start = (bf16[64,256]{1,0:T(8,128)(2,1)S(1)}, bf16[64,256]{1,0:T(8,128)(2,1)S(1)}, u32[]{:S(2)}, u32[]{:S(2)}) collective-permute-start(bf16[64,256]{1,0:T(8,128)(2,1)S(1)} %slice.490), channel_id=1, source_target_pairs={{0,8},{8,16},{16,24},{24,32},{32,40},{40,48},{48,56},{56,64},{64,7... | collective-permute-start | bytes 98312 | tf_op jit(solution)/shard_map/while/body/eval_jaxpr/ppermute | solution.py:17
  121.1 3.5 collective-permute-start.1
  132.3 8.9 %collective-permute-start = (bf16[64,256]{1,0:T(8,128)(2,1)S(1)}, bf16[64,256]{1,0:T(8,128)(2,1)S(1)}, u32[]{:S(2)}, u32[]{:S(2)}) collective-permute-start(bf16[64,256]{1,0:T(8,128)(2,1)S(1)} %slice.490), channel_id=1, source_target_pairs={{0,8},{8,16},{16,24},{24,32},{32,40},{40,48},{48,56},{56,64},{64,7... | collective-permute-start | bytes 98312 | tf_op jit(solution)/shard_map/while/body/eval_jaxpr/ppermute | solution.py:17
  147.5 3.5 collective-permute-start.1
  158.7 8.9 %collective-permute-start = (bf16[64,256]{1,0:T(8,128)(2,1)S(1)}, bf16[64,256]{1,0:T(8,128)(2,1)S(1)}, u32[]{:S(2)}, u32[]{:S(2)}) collective-permute-start(bf16[64,256]{1,0:T(8,128)(2,1)S(1)} %slice.490), channel_id=1, source_target_pairs={{0,8},{8,16},{16,24},{24,32},{32,40},{40,48},{48,56},{56,64},{64,7... | collective-permute-start | bytes 98312 | tf_op jit(solution)/shard_map/while/body/eval_jaxpr/ppermute | solution.py:17
  173.9 3.5 collective-permute-start.1
  185.1 8.9 %collective-permute-start = (bf16[64,256]{1,0:T(8,128)(2,1)S(1)}, bf16[64,256]{1,0:T(8,128)(2,1)S(1)}, u32[]{:S(2)}, u32[]{:S(2)}) collective-permute-start(bf16[64,256]{1,0:T(8,128)(2,1)S(1)} %slice.490), channel_id=1, source_target_pairs={{0,8},{8,16},{16,24},{24,32},{32,40},{40,48},{48,56},{56,64},{64,7... | collective-permute-start | bytes 98312 | tf_op jit(solution)/shard_map/while/body/eval_jaxpr/ppermute | solution.py:17
  200.3 3.5 collective-permute-start.1
  211.5 8.9 %collective-permute-start = (bf16[64,256]{1,0:T(8,128)(2,1)S(1)}, bf16[64,256]{1,0:T(8,128)(2,1)S(1)}, u32[]{:S(2)}, u32[]{:S(2)}) collective-permute-start(bf16[64,256]{1,0:T(8,128)(2,1)S(1)} %slice.490), channel_id=1, source_target_pairs={{0,8},{8,16},{16,24},{24,32},{32,40},{40,48},{48,56},{56,64},{64,7... | collective-permute-start | bytes 98312 | tf_op jit(solution)/shard_map/while/body/eval_jaxpr/ppermute | solution.py:17
  226.7 3.5 collective-permute-start.1
  237.9 8.9 %collective-permute-start = (bf16[64,256]{1,0:T(8,128)(2,1)S(1)}, bf16[64,256]{1,0:T(8,128)(2,1)S(1)}, u32[]{:S(2)}, u32[]{:S(2)}) collective-permute-start(bf16[64,256]{1,0:T(8,128)(2,1)S(1)} %slice.490), channel_id=1, source_target_pairs={{0,8},{8,16},{16,24},{24,32},{32,40},{40,48},{48,56},{56,64},{64,7... | collective-permute-start | bytes 98312 | tf_op jit(solution)/shard_map/while/body/eval_jaxpr/ppermute | solution.py:17
  253.1 3.5 collective-permute-start.1
  264.4 8.9 %collective-permute-start = (bf16[64,256]{1,0:T(8,128)(2,1)S(1)}, bf16[64,256]{1,0:T(8,128)(2,1)S(1)}, u32[]{:S(2)}, u32[]{:S(2)}) collective-permute-start(bf16[64,256]{1,0:T(8,128)(2,1)S(1)} %slice.490), channel_id=1, source_target_pairs={{0,8},{8,16},{16,24},{24,32},{32,40},{40,48},{48,56},{56,64},{64,7... | collective-permute-start | bytes 98312 | tf_op jit(solution)/shard_map/while/body/eval_jaxpr/ppermute | solution.py:17
  279.5 3.5 collective-permute-start.1
  290.8 8.9 %collective-permute-start = (bf16[64,256]{1,0:T(8,128)(2,1)S(1)}, bf16[64,256]{1,0:T(8,128)(2,1)S(1)}, u32[]{:S(2)}, u32[]{:S(2)}) collective-permute-start(bf16[64,256]{1,0:T(8,128)(2,1)S(1)} %slice.490), channel_id=1, source_target_pairs={{0,8},{8,16},{16,24},{24,32},{32,40},{40,48},{48,56},{56,64},{64,7... | collective-permute-start | bytes 98312 | tf_op jit(solution)/shard_map/while/body/eval_jaxpr/ppermute | solution.py:17
  306.0 3.5 collective-permute-start.1
  317.2 8.9 %collective-permute-start.10 = (bf16[64,256]{1,0:T(8,128)(2,1)S(1)}, bf16[64,256]{1,0:T(8,128)(2,1)S(1)}, u32[]{:S(2)}, u32[]{:S(2)}) collective-permute-start(bf16[64,256]{1,0:T(8,128)(2,1)S(1)} %slice.353), channel_id=1, source_target_pairs={{0,8},{8,16},{16,24},{24,32},{32,40},{40,48},{48,56},{56,64},{64,7... | collective-permute-start | bytes 98312 | tf_op jit(solution)/shard_map/ppermute | solution.py:17
  369.8 1.8 collective-permute-start.11
  372.4 11.9 %collective-permute-start.12 = (f32[832,64]{1,0:T(8,128)S(1)}, f32[832,64]{1,0:T(8,128)S(1)}, u32[]{:S(2)}, u32[]{:S(2)}) collective-permute-start(f32[832,64]{1,0:T(8,128)S(1)} %fusion.136), channel_id=1, source_target_pairs={{0,16},{8,24},{16,0},{24,8},{32,48},{40,56},{48,32},{56,40},{64,80... | collective-permute-start | bytes 638984 | tf_op jit(solution)/shard_map/ppermute | solution.py:24
  384.4 12.6 %collective-permute-start.13 = (f32[832,64]{1,0:T(8,128)S(1)}, f32[832,64]{1,0:T(8,128)S(1)}, u32[]{:S(2)}, u32[]{:S(2)}) collective-permute-start(f32[832,64]{1,0:T(8,128)S(1)} %add.305), channel_id=1, source_target_pairs={{0,32},{8,40},{16,48},{24,56},{32,0},{40,8},{48,16},{56,24},{64,96... | collective-permute-start | bytes 638984 | tf_op jit(solution)/shard_map/ppermute | solution.py:24
  397.1 11.7 %collective-permute-start.14 = (f32[832,64]{1,0:T(8,128)S(1)}, f32[832,64]{1,0:T(8,128)S(1)}, u32[]{:S(2)}, u32[]{:S(2)}) collective-permute-start(f32[832,64]{1,0:T(8,128)S(1)} %add.306), channel_id=1, source_target_pairs={{0,64},{8,72},{16,80},{24,88},{32,96},{40,104},{48,112},{56,120},{... | collective-permute-start | bytes 638984 | tf_op jit(solution)/shard_map/ppermute | solution.py:24
  412.7 4.0 collective-permute-start.15
  416.7 3.9 collective-permute-start.16
  420.6 5.4 collective-permute-start.17
  427.3 9.3 %collective-permute-start.18 = (f32[64,2048]{1,0:T(8,128)S(1)}, f32[64,2048]{1,0:T(8,128)S(1)}, u32[]{:S(2)}, u32[]{:S(2)}) collective-permute-start(f32[64,2048]{1,0:T(8,128)S(1)} %fusion.80), channel_id=1, source_target_pairs={{0,1},{1,0},{2,3},{3,2},{4,5},{5,4},{6,7},{7,6},{8,9},{9,8},{10,11... | collective-permute-start | bytes 1572872 | tf_op jit(solution)/shard_map/ppermute | solution.py:24
  436.7 13.3 %collective-permute-start.19 = (f32[64,2048]{1,0:T(8,128)S(1)}, f32[64,2048]{1,0:T(8,128)S(1)}, u32[]{:S(2)}, u32[]{:S(2)}) collective-permute-start(f32[64,2048]{1,0:T(8,128)S(1)} %add.313), channel_id=1, source_target_pairs={{0,2},{1,3},{2,0},{3,1},{4,6},{5,7},{6,4},{7,5},{8,10},{9,11},{10,... | collective-permute-start | bytes 1572872 | tf_op jit(solution)/shard_map/ppermute | solution.py:24
  450.1 11.8 %collective-permute-start.20 = (f32[64,2048]{1,0:T(8,128)S(1)}, f32[64,2048]{1,0:T(8,128)S(1)}, u32[]{:S(2)}, u32[]{:S(2)}) collective-permute-start(f32[64,2048]{1,0:T(8,128)S(1)} %add.314), channel_id=1, source_target_pairs={{0,4},{1,5},{2,6},{3,7},{4,0},{5,1},{6,2},{7,3},{8,12},{9,13},{10,... | collective-permute-start | bytes 1572872 | tf_op jit(solution)/shard_map/ppermute | solution.py:24
  462.8 8.8 %collective-permute-start.2 = (bf16[64,256]{1,0:T(8,128)(2,1)S(1)}, bf16[64,256]{1,0:T(8,128)(2,1)S(1)}, u32[]{:S(2)}, u32[]{:S(2)}) collective-permute-start(bf16[64,256]{1,0:T(8,128)(2,1)S(1)} %slice.498), channel_id=1, source_target_pairs={{0,8},{8,16},{16,24},{24,32},{32,40},{40,48},{48,56},{56,64},{64,7... | collective-permute-start | bytes 98312 | tf_op jit(solution)/shard_map/while/body/eval_jaxpr/ppermute | solution.py:17
  478.0 3.5 collective-permute-start.3
  489.2 8.9 %collective-permute-start.2 = (bf16[64,256]{1,0:T(8,128)(2,1)S(1)}, bf16[64,256]{1,0:T(8,128)(2,1)S(1)}, u32[]{:S(2)}, u32[]{:S(2)}) collective-permute-start(bf16[64,256]{1,0:T(8,128)(2,1)S(1)} %slice.498), channel_id=1, source_target_pairs={{0,8},{8,16},{16,24},{24,32},{32,40},{40,48},{48,56},{56,64},{64,7... | collective-permute-start | bytes 98312 | tf_op jit(solution)/shard_map/while/body/eval_jaxpr/ppermute | solution.py:17
  504.4 3.5 collective-permute-start.3
  515.6 8.9 %collective-permute-start.2 = (bf16[64,256]{1,0:T(8,128)(2,1)S(1)}, bf16[64,256]{1,0:T(8,128)(2,1)S(1)}, u32[]{:S(2)}, u32[]{:S(2)}) collective-permute-start(bf16[64,256]{1,0:T(8,128)(2,1)S(1)} %slice.498), channel_id=1, source_target_pairs={{0,8},{8,16},{16,24},{24,32},{32,40},{40,48},{48,56},{56,64},{64,7... | collective-permute-start | bytes 98312 | tf_op jit(solution)/shard_map/while/body/eval_jaxpr/ppermute | solution.py:17
  530.8 3.5 collective-permute-start.3
  542.0 8.9 %collective-permute-start.2 = (bf16[64,256]{1,0:T(8,128)(2,1)S(1)}, bf16[64,256]{1,0:T(8,128)(2,1)S(1)}, u32[]{:S(2)}, u32[]{:S(2)}) collective-permute-start(bf16[64,256]{1,0:T(8,128)(2,1)S(1)} %slice.498), channel_id=1, source_target_pairs={{0,8},{8,16},{16,24},{24,32},{32,40},{40,48},{48,56},{56,64},{64,7... | collective-permute-start | bytes 98312 | tf_op jit(solution)/shard_map/while/body/eval_jaxpr/ppermute | solution.py:17
  557.2 3.5 collective-permute-start.3
  568.4 8.9 %collective-permute-start.2 = (bf16[64,256]{1,0:T(8,128)(2,1)S(1)}, bf16[64,256]{1,0:T(8,128)(2,1)S(1)}, u32[]{:S(2)}, u32[]{:S(2)}) collective-permute-start(bf16[64,256]{1,0:T(8,128)(2,1)S(1)} %slice.498), channel_id=1, source_target_pairs={{0,8},{8,16},{16,24},{24,32},{32,40},{40,48},{48,56},{56,64},{64,7... | collective-permute-start | bytes 98312 | tf_op jit(solution)/shard_map/while/body/eval_jaxpr/ppermute | solution.py:17
  583.6 3.5 collective-permute-start.3
  594.8 8.9 %collective-permute-start.2 = (bf16[64,256]{1,0:T(8,128)(2,1)S(1)}, bf16[64,256]{1,0:T(8,128)(2,1)S(1)}, u32[]{:S(2)}, u32[]{:S(2)}) collective-permute-start(bf16[64,256]{1,0:T(8,128)(2,1)S(1)} %slice.498), channel_id=1, source_target_pairs={{0,8},{8,16},{16,24},{24,32},{32,40},{40,48},{48,56},{56,64},{64,7... | collective-permute-start | bytes 98312 | tf_op jit(solution)/shard_map/while/body/eval_jaxpr/ppermute | solution.py:17
  610.0 3.5 collective-permute-start.3
  621.2 8.9 %collective-permute-start.2 = (bf16[64,256]{1,0:T(8,128)(2,1)S(1)}, bf16[64,256]{1,0:T(8,128)(2,1)S(1)}, u32[]{:S(2)}, u32[]{:S(2)}) collective-permute-start(bf16[64,256]{1,0:T(8,128)(2,1)S(1)} %slice.498), channel_id=1, source_target_pairs={{0,8},{8,16},{16,24},{24,32},{32,40},{40,48},{48,56},{56,64},{64,7... | collective-permute-start | bytes 98312 | tf_op jit(solution)/shard_map/while/body/eval_jaxpr/ppermute | solution.py:17
  636.4 3.5 collective-permute-start.3
  647.6 8.9 %collective-permute-start.2 = (bf16[64,256]{1,0:T(8,128)(2,1)S(1)}, bf16[64,256]{1,0:T(8,128)(2,1)S(1)}, u32[]{:S(2)}, u32[]{:S(2)}) collective-permute-start(bf16[64,256]{1,0:T(8,128)(2,1)S(1)} %slice.498), channel_id=1, source_target_pairs={{0,8},{8,16},{16,24},{24,32},{32,40},{40,48},{48,56},{56,64},{64,7... | collective-permute-start | bytes 98312 | tf_op jit(solution)/shard_map/while/body/eval_jaxpr/ppermute | solution.py:17
  662.8 3.5 collective-permute-start.3
  674.0 8.9 %collective-permute-start.2 = (bf16[64,256]{1,0:T(8,128)(2,1)S(1)}, bf16[64,256]{1,0:T(8,128)(2,1)S(1)}, u32[]{:S(2)}, u32[]{:S(2)}) collective-permute-start(bf16[64,256]{1,0:T(8,128)(2,1)S(1)} %slice.498), channel_id=1, source_target_pairs={{0,8},{8,16},{16,24},{24,32},{32,40},{40,48},{48,56},{56,64},{64,7... | collective-permute-start | bytes 98312 | tf_op jit(solution)/shard_map/while/body/eval_jaxpr/ppermute | solution.py:17
  689.2 3.5 collective-permute-start.3
  700.4 8.9 %collective-permute-start.2 = (bf16[64,256]{1,0:T(8,128)(2,1)S(1)}, bf16[64,256]{1,0:T(8,128)(2,1)S(1)}, u32[]{:S(2)}, u32[]{:S(2)}) collective-permute-start(bf16[64,256]{1,0:T(8,128)(2,1)S(1)} %slice.498), channel_id=1, source_target_pairs={{0,8},{8,16},{16,24},{24,32},{32,40},{40,48},{48,56},{56,64},{64,7... | collective-permute-start | bytes 98312 | tf_op jit(solution)/shard_map/while/body/eval_jaxpr/ppermute | solution.py:17
  715.6 3.5 collective-permute-start.3
  726.9 8.9 %collective-permute-start.21 = (bf16[64,256]{1,0:T(8,128)(2,1)S(1)}, bf16[64,256]{1,0:T(8,128)(2,1)S(1)}, u32[]{:S(2)}, u32[]{:S(2)}) collective-permute-start(bf16[64,256]{1,0:T(8,128)(2,1)S(1)} %slice.368), channel_id=1, source_target_pairs={{0,8},{8,16},{16,24},{24,32},{32,40},{40,48},{48,56},{56,64},{64,7... | collective-permute-start | bytes 98312 | tf_op jit(solution)/shard_map/ppermute | solution.py:17
  777.3 11.9 %collective-permute-start.23 = (f32[832,64]{1,0:T(8,128)S(1)}, f32[832,64]{1,0:T(8,128)S(1)}, u32[]{:S(2)}, u32[]{:S(2)}) collective-permute-start(f32[832,64]{1,0:T(8,128)S(1)} %fusion.135), channel_id=1, source_target_pairs={{0,16},{8,24},{16,0},{24,8},{32,48},{40,56},{48,32},{56,40},{64,80... | collective-permute-start | bytes 638984 | tf_op jit(solution)/shard_map/ppermute | solution.py:24
  789.3 12.6 %collective-permute-start.24 = (f32[832,64]{1,0:T(8,128)S(1)}, f32[832,64]{1,0:T(8,128)S(1)}, u32[]{:S(2)}, u32[]{:S(2)}) collective-permute-start(f32[832,64]{1,0:T(8,128)S(1)} %add.321), channel_id=1, source_target_pairs={{0,32},{8,40},{16,48},{24,56},{32,0},{40,8},{48,16},{56,24},{64,96... | collective-permute-start | bytes 638984 | tf_op jit(solution)/shard_map/ppermute | solution.py:24
  801.9 11.7 %collective-permute-start.25 = (f32[832,64]{1,0:T(8,128)S(1)}, f32[832,64]{1,0:T(8,128)S(1)}, u32[]{:S(2)}, u32[]{:S(2)}) collective-permute-start(f32[832,64]{1,0:T(8,128)S(1)} %add.322), channel_id=1, source_target_pairs={{0,64},{8,72},{16,80},{24,88},{32,96},{40,104},{48,112},{56,120},{... | collective-permute-start | bytes 638984 | tf_op jit(solution)/shard_map/ppermute | solution.py:24
  815.5 4.0 collective-permute-start.26
  819.5 4.0 collective-permute-start.27
  823.6 5.4 collective-permute-start.28
  (82 other events, 626.8 us)

commit v2 on v1

--- a/solution.py
+++ b/solution.py
@@ -5,6 +5,8 @@
 
 ITERS = 10
 OUTER = 2
+CHUNK = 5
+GHOST_BLOCKS = 10
 
 
 epsilon = 1e-06
@@ -15,6 +17,13 @@
     count = lax.axis_size(axis)
     leading, last = (max(0, -steps), min(count, count - steps))
     return lax.ppermute(value, axis, [(source, source + steps) for source in range(leading, last)])
+
+
+def widened(rows, ghost):
+    seg_len = rows.shape[1]
+    from_left = passed_along(rows[:, seg_len - ghost :], "seg", 1)
+    from_right = passed_along(rows[:, :ghost], "seg", -1)
+    return jnp.concatenate([from_left, rows, from_right], axis=1)
 
 
 def butterfly_sum(value, axis):
@@ -117,11 +126,16 @@
     atoms_all, tap_count = temporal.shape
     block_width = 128
     skew = one_hot_skew(block_width, 2 * block_width)
-    positions = lax.axis_index("seg") * seg_len + lax.iota(jnp.int32, seg_len)
-    crosses = (positions[None, :] < breaks[:, None]) & (
-        breaks[:, None] < positions[None, :] + tap_count
-    )
-    allowed = jnp.where(jnp.any(crosses, axis=0), 0.0, 1.0).astype(jnp.float32)
+    ghost = GHOST_BLOCKS * block_width
+    wide_positions = lax.axis_index("seg") * seg_len - ghost + lax.iota(jnp.int32, seg_len + 2 * ghost)
+    wide_crosses = (wide_positions[None, :] < breaks[:, None]) & (
+        breaks[:, None] < wide_positions[None, :] + tap_count
+    )
+    inside = jnp.where(
+        (wide_positions >= 0) & (wide_positions < seg_len * lax.axis_size("seg")), 1.0, 0.0
+    ).astype(jnp.float32)
+    allowed_wide = inside * jnp.where(jnp.any(wide_crosses, axis=0), 0.0, 1.0).astype(jnp.float32)
+    zero_rim = jnp.zeros((atoms_all, tap_count), jnp.bfloat16)
     raw_start = butterfly_sum(jnp.dot(spatial.T, spatial, precision=highest), "chan")
     scaling = 1.0 / jnp.sqrt(jnp.diag(raw_start) + epsilon)
     space_loc = spatial * scaling[None, :]
@@ -143,20 +157,22 @@
         step_col = step_sizes[:, None]
         limit_col = (step_sizes * thresholds)[:, None]
 
+        projected_wide = widened(projected, ghost)
+
         def shrink_step(iteration, current):
-            rebuilt, _, _ = reconstruct(matrices, current, block_width, tap_count)
-            residual = projected - mix_atoms(rebuilt)
-            residual_b = residual.astype(jnp.bfloat16)
-            after_rim = passed_along(residual_b[:, :tap_count], "seg", -1)
-            descent = correlate_blocks(matrices, residual_b, after_rim, block_width)
+            rebuilt = convolve_blocks(matrices, current.astype(jnp.bfloat16), zero_rim, block_width)
+            residual = (projected_wide - mix_atoms(rebuilt)) * inside[None, :]
+            descent = correlate_blocks(matrices, residual.astype(jnp.bfloat16), zero_rim, block_width)
             stepped = current + step_col * descent
             return (
-                allowed[None, :]
+                allowed_wide[None, :]
                 * jnp.sign(stepped)
                 * jnp.maximum(jnp.abs(stepped) - limit_col, 0.0)
             )
 
-        latent = lax.fori_loop(0, ITERS, shrink_step, latent)
+        for chunk in range(ITERS // CHUNK):
+            wide = lax.fori_loop(0, CHUNK, shrink_step, widened(latent, ghost))
+            latent = wide[:, ghost : ghost + seg_len]
         rebuilt, before, latent_b = reconstruct(matrices, latent, block_width, tap_count)
         rebuilt_b = rebuilt.astype(jnp.bfloat16)
         row_part = jnp.dot(signal, rebuilt_b.T, preferred_element_type=jnp.float32)

time: 842 us -> 758 us (0.900)
  waiting for transfers between devices: 310 us -> 163 us
  other arithmetic: 32.8 us -> 112 us
  local copies, waits for them, and re-layouts: 40.2 us -> 88.4 us
  matrix products: 335 us -> 300 us
  starting transfers between devices: 109 us -> 79.8 us
    ppermute x42 -> x14, waiting for transfers between devices: 180 us -> 23.6 us  [passed_along(): lax.ppermute(value, axis, [(source, source + steps) for source in range(l...]
    mul x20 -> x21, other arithmetic: 9.4 us -> 59.4 us  [the longest x20 59.4 us: shrink_step(): allowed_wide[None, :] * jnp.sign(stepped)]
    dot_general x66, matrix products: 117 us -> 84.4 us  [convolve_blocks(): jnp.einsum('kbm,kmi->kbi', window, matrix, preferred_element_type=jnp.flo...]
    while x120 -> x200, local copies, waits for them, and re-layouts: 0.27 us -> 29.2 us
    convert_element_type x0 -> x20, other arithmetic: none -> 26.6 us  [shrink_step(): current.astype(jnp.bfloat16)]
    ppermute x42 -> x14, starting transfers between devices: 81 us -> 60.4 us  [passed_along(): lax.ppermute(value, axis, [(source, source + steps) for source in range(l...]
    dot_general x20, matrix products: 15.4 us -> 27.6 us  [mix_atoms(): return jnp.dot(own_gram, rebuilt_part, precision=highest)]
    slice x20 -> x10, local copies, waits for them, and re-layouts: 0.13 us -> 11.9 us  [the longest x6 7.63 us: widened(): from_left = passed_along(rows[:, seg_len - ghost:], 'seg', 1)]
  transfers between devices with their start and end apart: 65 -> 37, of which waited for: 64 -> 30; matrix products, arithmetic and copies ran while one was open for 4% -> 5% of each run, Pallas kernels for 0% -> 0%
where the time goes in v2:
time: 758 us; the launch traced here: 748 us
  matrix products  300 us (40%)
  waiting for transfers between devices  163 us (22%)
  other arithmetic  112 us (15%)
  local copies, waits for them, and re-layouts  88.4 us (12%)
  starting transfers between devices  79.8 us (11%)
    ppermute x23, waiting for transfers between devices, butterfly_sum(): lax.ppermute(value, axis, [(i, i ^ distance) for i in range(count)])  140 us
    dot_general x60, matrix products, correlate_blocks(): jnp.einsum('kbi,kmi->kbm', window, matrix, preferred_element_type=jnp.flo...  127 us
    dot_general x66, matrix products, convolve_blocks(): jnp.einsum('kbm,kmi->kbi', window, matrix, preferred_element_type=jnp.flo...  84.4 us
    ppermute x14, starting transfers between devices, passed_along(): lax.ppermute(value, axis, [(source, source + steps) for source in range(l...  60.4 us
    mul x20, other arithmetic, shrink_step(): allowed_wide[None, :] * jnp.sign(stepped)  59.4 us
    dot_general x2, matrix products, lag_sums(): bands = jnp.dot(stacked, skew.astype(jnp.float32).T, precision=highest)  36.7 us
    while x200, local copies, waits for them, and re-layouts  29.2 us
    dot_general x20, matrix products, mix_atoms(): return jnp.dot(own_gram, rebuilt_part, precision=highest)  27.6 us
  transfers between devices with their start and end apart: 37, of which 30 were waited for; matrix products, arithmetic and copies ran while one was open for 5% of the time, Pallas kernels for 0%

profile of v2, /device:TPU:4, one launch (start us, length us, event | category | flops | bytes accessed | tf_op | source)
XLA Modules:
  0.0 747.8 jit_solution(15643965463968984813)
XLA Ops:
  7.3 7.3 collective-permute-start.1
  18.8 3.2 collective-permute-start.4
  28.4 6.5 collective-permute-done.5
  39.5 3.6 copy.92
  47.1 3.0 collective-permute-start.7
  50.4 7.5 %collective-permute-done.7 = f32[64,2048]{1,0:T(8,128)S(1)} collective-permute-done((f32[64,2048]{1,0:T(8,128)S(1)}, f32[64,2048]{1,0:T(8,128)S(1)}, u32[]{:S(2)}, u32[]{:S(2)}) %collective-permute-start.7) | collective-permute-done | bytes 524320 | tf_op jit(solution)/shard_map/ppermute | solution.py:33
  59.9 7.5 %collective-permute-start.9 = (f32[64,1280]{1,0:T(8,128)S(1)}, f32[64,1280]{1,0:T(8,128)S(1)}, u32[]{:S(2)}, u32[]{:S(2)}) collective-permute-start(f32[64,1280]{1,0:T(8,128)S(1)} %get-tuple-element.521), channel_id=1, source_target_pairs={{8,0},{16,8},{24,16},{32,24},{40,32},{48,40},{56,48},{64,56},{72,6... | collective-permute-start | bytes 983048 | tf_op jit(solution)/shard_map/ppermute | solution.py:19
  73.0 91.7 %while.50 = (s32[]{:T(128)}, f32[64,4608]{1,0:T(8,128)}, f32[4608]{0:T(1024)S(1)}, f32[64,1]{0,1:T(1,128)S(1)}, bf16[64,128,128]{2,1,0:T(8,128)(2,1)}, /*index=5...) while((s32[]{:T(128)}, f32[64,4608]{1,0:T(8,128)}, ...), condition=%wide.region_3.4_spmd.clone, body=%wide.region_2.3_spmd.clone.sunk | while | flops 684218880 | bytes 79633168 | solution.py:174
  81.9 3.2 fusion.344
  88.3 3.0 maximum_multiply_fusion.8
  100.2 3.2 fusion.344
  106.7 3.0 maximum_multiply_fusion.8
  118.6 3.3 fusion.344
  125.0 3.0 maximum_multiply_fusion.8
  136.9 3.2 fusion.344
  143.3 3.0 maximum_multiply_fusion.8
  155.2 3.3 fusion.344
  161.7 3.0 maximum_multiply_fusion.8
  168.4 8.0 %collective-permute-start.11 = (f32[64,1280]{1,0:T(8,128)S(1)}, f32[64,1280]{1,0:T(8,128)}, u32[]{:S(2)}, u32[]{:S(2)}) collective-permute-start(f32[64,1280]{1,0:T(8,128)S(1)} %get-tuple-element.517), channel_id=1, source_target_pairs={{8,0},{16,8},{24,16},{32,24},{40,32},{48,40},{56,48},{64,56},{72,6... | collective-permute-start | bytes 983048 | tf_op jit(solution)/shard_map/ppermute | solution.py:19
  182.6 91.7 %while.51 = (s32[]{:T(128)}, f32[64,4608]{1,0:T(8,128)}, f32[4608]{0:T(1024)S(1)}, f32[64,1]{0,1:T(1,128)S(1)}, bf16[64,128,128]{2,1,0:T(8,128)(2,1)}, /*index=5...) while((s32[]{:T(128)}, f32[64,4608]{1,0:T(8,128)}, ...), condition=%wide.region_5.6_spmd.clone, body=%wide.region_4.5_spmd.clone.sunk | while | flops 684218880 | bytes 79633168 | solution.py:174
  191.5 3.2 fusion.362
  197.9 3.0 maximum_multiply_fusion.9
  209.8 3.3 fusion.362
  216.3 3.0 maximum_multiply_fusion.9
  228.2 3.2 fusion.362
  234.6 3.0 maximum_multiply_fusion.9
  246.5 3.3 fusion.362
  252.9 3.0 maximum_multiply_fusion.9
  264.8 3.2 fusion.362
  271.3 3.0 maximum_multiply_fusion.9
  280.3 4.2 collective-permute-done.14
  300.0 18.5 %fusion.98 = f32[192,256]{0,1:T(8,128)S(1)} fusion(f32[192,128,128]{2,1,0:T(8,128)S(1)} %pad_maximum_fusion), kind=kOutput, calls=%fused_computation.161 | convolution fusion | flops 9684647936 | bytes 12779520 | tf_op jit(solution)/shard_map/dot_general | solution.py:78
  324.3 11.8 %collective-permute-done.16 = f32[832,64]{1,0:T(8,128)S(1)} collective-permute-done((f32[832,64]{1,0:T(8,128)S(1)}, f32[832,64]{1,0:T(8,128)S(1)}, u32[]{:S(2)}, u32[]{:S(2)}) %collective-permute-start.16) | collective-permute-done | bytes 213024 | tf_op jit(solution)/shard_map/ppermute | solution.py:33
  336.4 12.5 %collective-permute-done.17 = f32[832,64]{1,0:T(8,128)S(1)} collective-permute-done((f32[832,64]{1,0:T(8,128)S(1)}, f32[832,64]{1,0:T(8,128)S(1)}, u32[]{:S(2)}, u32[]{:S(2)}) %collective-permute-start.17) | collective-permute-done | bytes 213024 | tf_op jit(solution)/shard_map/ppermute | solution.py:33
  349.0 11.6 %collective-permute-done.18 = f32[832,64]{1,0:T(8,128)S(1)} collective-permute-done((f32[832,64]{1,0:T(8,128)S(1)}, f32[832,64]{1,0:T(8,128)S(1)}, u32[]{:S(2)}, u32[]{:S(2)}) %collective-permute-start.18) | collective-permute-done | bytes 213024 | tf_op jit(solution)/shard_map/ppermute | solution.py:33
  363.7 3.1 collective-permute-done.19
  367.2 3.5 collective-permute-done.20
  378.4 7.3 collective-permute-start.13
  395.2 5.0 collective-permute-done.22
  400.6 14.3 %collective-permute-done.23 = f32[64,2048]{1,0:T(8,128)S(1)} collective-permute-done((f32[64,2048]{1,0:T(8,128)S(1)}, f32[64,2048]{1,0:T(8,128)S(1)}, u32[]{:S(2)}, u32[]{:S(2)}) %collective-permute-start.23) | collective-permute-done | bytes 524320 | tf_op jit(solution)/shard_map/ppermute | solution.py:33
  417.4 8.7 %collective-permute-done.24 = f32[64,2048]{1,0:T(8,128)S(1)} collective-permute-done((f32[64,2048]{1,0:T(8,128)S(1)}, f32[64,2048]{1,0:T(8,128)S(1)}, u32[]{:S(2)}, u32[]{:S(2)}) %collective-permute-start.24) | collective-permute-done | bytes 524320 | tf_op jit(solution)/shard_map/ppermute | solution.py:33
  428.1 7.3 collective-permute-start.26
  443.0 91.4 %while.52 = (s32[]{:T(128)}, f32[64,4608]{1,0:T(8,128)}, f32[4608]{0:T(1024)S(1)}, f32[64,1]{0,1:T(1,128)S(1)}, bf16[64,128,128]{2,1,0:T(8,128)(2,1)}, /*index=5...) while((s32[]{:T(128)}, f32[64,4608]{1,0:T(8,128)}, ...), condition=%wide.region_11.12_spmd.clone, body=%wide.region_10.11_spmd.clone.sunk | while | flops 684218880 | bytes 79633168 | solution.py:174
  451.9 3.2 fusion.380
  470.2 3.2 fusion.380
  488.5 3.2 fusion.380
  494.9 2.9 maximum_multiply_fusion.10
  506.8 3.2 fusion.380
  525.1 3.2 fusion.380
  538.2 7.4 collective-permute-start.28
  552.1 91.4 %while.53 = (s32[]{:T(128)}, f32[64,4608]{1,0:T(8,128)}, f32[4608]{0:T(1024)S(1)}, f32[64,1]{0,1:T(1,128)S(1)}, bf16[64,128,128]{2,1,0:T(8,128)(2,1)}, /*index=5...) while((s32[]{:T(128)}, f32[64,4608]{1,0:T(8,128)}, ...), condition=%wide.region_13.14_spmd.clone, body=%wide.region_12.13_spmd.clone.sunk | while | flops 684218880 | bytes 79633168 | solution.py:174
  561.0 3.2 fusion.398
  579.3 3.2 fusion.398
  597.6 3.2 fusion.398
  615.9 3.2 fusion.398
  622.3 2.9 maximum_multiply_fusion.11
  634.1 3.2 fusion.398
  648.4 6.2 collective-permute-done.29
  670.3 18.3 %fusion.101 = f32[192,256]{0,1:T(8,128)S(1)} fusion(f32[192,128,128]{2,1,0:T(8,128)S(1)} %pad_maximum_fusion.1), kind=kOutput, calls=%fused_computation.162 | convolution fusion | flops 9684647936 | bytes 12779520 | tf_op jit(solution)/shard_map/dot_general | solution.py:78
  694.4 11.8 %collective-permute-done.31 = f32[832,64]{1,0:T(8,128)S(1)} collective-permute-done((f32[832,64]{1,0:T(8,128)S(1)}, f32[832,64]{1,0:T(8,128)S(1)}, u32[]{:S(2)}, u32[]{:S(2)}) %collective-permute-start.31) | collective-permute-done | bytes 213024 | tf_op jit(solution)/shard_map/ppermute | solution.py:33
  706.4 12.5 %collective-permute-done.32 = f32[832,64]{1,0:T(8,128)S(1)} collective-permute-done((f32[832,64]{1,0:T(8,128)S(1)}, f32[832,64]{1,0:T(8,128)S(1)}, u32[]{:S(2)}, u32[]{:S(2)}) %collective-permute-start.32) | collective-permute-done | bytes 213024 | tf_op jit(solution)/shard_map/ppermute | solution.py:33
  719.1 11.6 %collective-permute-done.33 = f32[832,64]{1,0:T(8,128)S(1)} collective-permute-done((f32[832,64]{1,0:T(8,128)S(1)}, f32[832,64]{1,0:T(8,128)S(1)}, u32[]{:S(2)}, u32[]{:S(2)}) %collective-permute-start.33) | collective-permute-done | bytes 213024 | tf_op jit(solution)/shard_map/ppermute | solution.py:33
  736.6 3.9 collective-permute-done.35
  741.3 4.7 collective-permute-done.36
  (690 shorter events, 412.1 us)
Async XLA Ops:
  0.6 24.4 %copy-start = (bf16[512,2048]{1,0:T(8,128)(2,1)S(1)}, bf16[512,2048]{1,0:T(8,128)(2,1)}, u32[]{:S(2)}) copy-start(bf16[512,2048]{1,0:T(8,128)(2,1)} %param.27) | copy-start | bytes 6291460
  0.6 13.9 %copy-start.38 = (f32[64,256]{1,0:T(8,128)S(1)}, f32[64,256]{1,0:T(8,128)}, u32[]{:S(2)}) copy-start(f32[64,256]{1,0:T(8,128)} %param.29) | copy-start | bytes 196612
  2.0 23.0 %copy-start.34 = (f32[512,64]{0,1:T(8,128)S(1)}, f32[512,64]{0,1:T(8,128)}, u32[]{:S(2)}) copy-start(f32[512,64]{0,1:T(8,128)} %param.28) | copy-start | bytes 393220
  2.1 12.7 %collective-permute-start.2 = (f32[64,64]{1,0:T(8,128)S(1)}, f32[64,64]{1,0:T(8,128)S(1)}, u32[]{:S(2)}, u32[]{:S(2)}) collective-permute-start(f32[64,64]{1,0:T(8,128)S(1)} %fusion.202), channel_id=1, source_target_pairs={{0,1},{1,0},{2,3},{3,2},{4,5},{5,4},{6,7},{7,6},{8,9},{9,8},{10,11... | collective-permute-start | bytes 49160 | tf_op jit(solution)/shard_map/ppermute | solution.py:33
  5.4 62.1 %collective-permute-start = (f32[64,1280]{1,0:T(8,128)}, f32[64,1280]{1,0:T(8,128)}, u32[]{:S(2)}, u32[]{:S(2)}) collective-permute-start(f32[64,1280]{1,0:T(8,128)} %get-tuple-element.522), channel_id=1, source_target_pairs={{0,8},{8,16},{16,24},{24,32},{32,40},{40,48},{48,56},{56,64},{64,7... | collective-permute-start | bytes 983048 | tf_op jit(solution)/shard_map/ppermute | solution.py:19
  7.3 60.2 %collective-permute-start.1 = (f32[64,1280]{1,0:T(8,128)}, f32[64,1280]{1,0:T(8,128)}, u32[]{:S(2)}, u32[]{:S(2)}) collective-permute-start(f32[64,1280]{1,0:T(8,128)} %get-tuple-element.523), channel_id=1, source_target_pairs={{8,0},{16,8},{24,16},{32,24},{40,32},{48,40},{56,48},{64,56},{72,6... | collective-permute-start | bytes 983048 | tf_op jit(solution)/shard_map/ppermute | solution.py:19
  14.8 11.7 %copy-start.40 = (s32[16384]{0:T(1024)}, s32[16384]{0:T(1024)S(1)}, u32[]{:S(2)}) copy-start(s32[16384]{0:T(1024)S(1)} %add_bitcast_fusion) | copy-start | bytes 196612
  14.8 4.0 collective-permute-start.3
  18.8 5.4 collective-permute-start.4
  25.1 25.2 %copy-start.42 = (f32[64]{0:T(128)}, f32[64]{0:T(128)S(1)}, u32[]{:S(2)}) copy-start(f32[64]{0:T(128)S(1)} %add_rsqrt_fusion.2) | copy-start | bytes 772
  25.6 9.3 %collective-permute-start.5 = (f32[64,2048]{1,0:T(8,128)S(1)}, f32[64,2048]{1,0:T(8,128)S(1)}, u32[]{:S(2)}, u32[]{:S(2)}) collective-permute-start(f32[64,2048]{1,0:T(8,128)S(1)} %fusion.151), channel_id=1, source_target_pairs={{0,1},{1,0},{2,3},{3,2},{4,5},{5,4},{6,7},{7,6},{8,9},{9,8},{10,11... | collective-permute-start | bytes 1572872 | tf_op jit(solution)/shard_map/ppermute | solution.py:33
  34.9 12.1 %collective-permute-start.6 = (f32[64,2048]{1,0:T(8,128)S(1)}, f32[64,2048]{1,0:T(8,128)S(1)}, u32[]{:S(2)}, u32[]{:S(2)}) collective-permute-start(f32[64,2048]{1,0:T(8,128)S(1)} %add.348), channel_id=1, source_target_pairs={{0,2},{1,3},{2,0},{3,1},{4,6},{5,7},{6,4},{7,5},{8,10},{9,11},{10,... | collective-permute-start | bytes 1572872 | tf_op jit(solution)/shard_map/ppermute | solution.py:33
  39.5 3.6 copy-start.30
  47.1 10.8 %collective-permute-start.7 = (f32[64,2048]{1,0:T(8,128)S(1)}, f32[64,2048]{1,0:T(8,128)S(1)}, u32[]{:S(2)}, u32[]{:S(2)}) collective-permute-start(f32[64,2048]{1,0:T(8,128)S(1)} %add.349), channel_id=1, source_target_pairs={{0,4},{1,5},{2,6},{3,7},{4,0},{5,1},{6,2},{7,3},{8,12},{9,13},{10,... | collective-permute-start | bytes 1572872 | tf_op jit(solution)/shard_map/ppermute | solution.py:33
  50.4 17.2 %copy-start.33 = (f32[64,2048]{1,0:T(8,128)S(1)}, f32[64,2048]{1,0:T(8,128)}, u32[]{:S(2)}) copy-start(f32[64,2048]{1,0:T(8,128)} %param.30) | copy-start | bytes 1572868
  57.9 13.8 %copy-start.27 = (f32[64,2048]{1,0:T(8,128)}, f32[64,2048]{1,0:T(8,128)S(1)}, u32[]{:S(2)}) copy-start(f32[64,2048]{1,0:T(8,128)S(1)} %add.350) | copy-start | bytes 1572868
  58.0 12.0 %collective-permute-start.8 = (f32[64,1280]{1,0:T(8,128)S(1)}, f32[64,1280]{1,0:T(8,128)S(1)}, u32[]{:S(2)}, u32[]{:S(2)}) collective-permute-start(f32[64,1280]{1,0:T(8,128)S(1)} %get-tuple-element.520), channel_id=1, source_target_pairs={{0,8},{8,16},{16,24},{24,32},{32,40},{40,48},{48,56},{56,64},{64,7... | collective-permute-start | bytes 983048 | tf_op jit(solution)/shard_map/ppermute | solution.py:19
  59.9 11.8 %collective-permute-start.9 = (f32[64,1280]{1,0:T(8,128)S(1)}, f32[64,1280]{1,0:T(8,128)S(1)}, u32[]{:S(2)}, u32[]{:S(2)}) collective-permute-start(f32[64,1280]{1,0:T(8,128)S(1)} %get-tuple-element.521), channel_id=1, source_target_pairs={{8,0},{16,8},{24,16},{32,24},{40,32},{48,40},{56,48},{64,56},{72,6... | collective-permute-start | bytes 983048 | tf_op jit(solution)/shard_map/ppermute | solution.py:19
  81.9 3.3 copy-start.9
  118.5 3.3 copy-start.9
  155.2 3.3 copy-start.9
  166.5 12.4 %collective-permute-start.10 = (f32[64,1280]{1,0:T(8,128)}, f32[64,1280]{1,0:T(8,128)S(1)}, u32[]{:S(2)}, u32[]{:S(2)}) collective-permute-start(f32[64,1280]{1,0:T(8,128)} %get-tuple-element.516), channel_id=1, source_target_pairs={{0,8},{8,16},{16,24},{24,32},{32,40},{40,48},{48,56},{56,64},{64,7... | collective-permute-start | bytes 983048 | tf_op jit(solution)/shard_map/ppermute | solution.py:19
  168.4 12.0 %collective-permute-start.11 = (f32[64,1280]{1,0:T(8,128)S(1)}, f32[64,1280]{1,0:T(8,128)}, u32[]{:S(2)}, u32[]{:S(2)}) collective-permute-start(f32[64,1280]{1,0:T(8,128)S(1)} %get-tuple-element.517), channel_id=1, source_target_pairs={{8,0},{16,8},{24,16},{32,24},{40,32},{48,40},{56,48},{64,56},{72,6... | collective-permute-start | bytes 983048 | tf_op jit(solution)/shard_map/ppermute | solution.py:19
  191.5 3.3 copy-start.11
  209.8 3.3 copy-start.11
  246.5 3.3 copy-start.11
  275.4 9.1 %collective-permute-start.14 = (bf16[64,256]{1,0:T(8,128)(2,1)S(1)}, bf16[64,256]{1,0:T(8,128)(2,1)S(1)}, u32[]{:S(2)}, u32[]{:S(2)}) collective-permute-start(bf16[64,256]{1,0:T(8,128)(2,1)S(1)} %slice.481), channel_id=1, source_target_pairs={{0,8},{8,16},{16,24},{24,32},{32,40},{40,48},{48,56},{56,64},{64,7... | collective-permute-start | bytes 98312 | tf_op jit(solution)/shard_map/ppermute | solution.py:19
  322.3 1.8 collective-permute-start.15
  324.2 11.9 %collective-permute-start.16 = (f32[832,64]{1,0:T(8,128)S(1)}, f32[832,64]{1,0:T(8,128)S(1)}, u32[]{:S(2)}, u32[]{:S(2)}) collective-permute-start(f32[832,64]{1,0:T(8,128)S(1)} %fusion.194), channel_id=1, source_target_pairs={{0,16},{8,24},{16,0},{24,8},{32,48},{40,56},{48,32},{56,40},{64,80... | collective-permute-start | bytes 638984 | tf_op jit(solution)/shard_map/ppermute | solution.py:33
  336.2 25.3 %copy-start.35 = (f32[512,64]{0,1:T(8,128)S(1)}, f32[512,64]{0,1:T(8,128)}, u32[]{:S(2)}) copy-start(f32[512,64]{0,1:T(8,128)} %param.28) | copy-start | bytes 393220
  336.2 25.3 %copy-start.43 = (f32[64]{0:T(128)S(1)}, f32[64]{0:T(128)}, u32[]{:S(2)}) copy-start(f32[64]{0:T(128)} %copy-done.42) | copy-start | bytes 772
  336.3 12.6 %collective-permute-start.17 = (f32[832,64]{1,0:T(8,128)S(1)}, f32[832,64]{1,0:T(8,128)S(1)}, u32[]{:S(2)}, u32[]{:S(2)}) collective-permute-start(f32[832,64]{1,0:T(8,128)S(1)} %add.358), channel_id=1, source_target_pairs={{0,32},{8,40},{16,48},{24,56},{32,0},{40,8},{48,16},{56,24},{64,96... | collective-permute-start | bytes 638984 | tf_op jit(solution)/shard_map/ppermute | solution.py:33
  348.9 11.7 %collective-permute-start.18 = (f32[832,64]{1,0:T(8,128)S(1)}, f32[832,64]{1,0:T(8,128)S(1)}, u32[]{:S(2)}, u32[]{:S(2)}) collective-permute-start(f32[832,64]{1,0:T(8,128)S(1)} %add.359), channel_id=1, source_target_pairs={{0,64},{8,72},{16,80},{24,88},{32,96},{40,104},{48,112},{56,120},{... | collective-permute-start | bytes 638984 | tf_op jit(solution)/shard_map/ppermute | solution.py:33
  360.7 12.9 %copy-start.36 = (f32[832,64]{1,0:T(8,128)}, f32[832,64]{1,0:T(8,128)S(1)}, u32[]{:S(2)}) copy-start(f32[832,64]{1,0:T(8,128)S(1)} %add.360) | copy-start | bytes 638980
  362.2 24.4 %copy-start.31 = (f32[512,64]{1,0:T(8,128)}, f32[512,64]{1,0:T(8,128)S(1)}, u32[]{:S(2)}) copy-start(f32[512,64]{1,0:T(8,128)S(1)} %slice_subtract_fusion.1) | copy-start | bytes 393220
  362.8 4.0 collective-permute-start.19
  366.8 3.9 collective-permute-start.20
  370.7 15.0 %collective-permute-start.21 = (f32[64,64]{1,0:T(8,128)S(1)}, f32[64,64]{1,0:T(8,128)S(1)}, u32[]{:S(2)}, u32[]{:S(2)}) collective-permute-start(f32[64,64]{1,0:T(8,128)S(1)} %add.363), channel_id=1, source_target_pairs={{0,4},{1,5},{2,6},{3,7},{4,0},{5,1},{6,2},{7,3},{8,12},{9,13},{10,... | collective-permute-start | bytes 49160 | tf_op jit(solution)/shard_map/ppermute | solution.py:33
  376.5 13.9 %collective-permute-start.12 = (f32[64,1280]{1,0:T(8,128)}, f32[64,1280]{1,0:T(8,128)}, u32[]{:S(2)}, u32[]{:S(2)}) collective-permute-start(f32[64,1280]{1,0:T(8,128)} %get-tuple-element.514), channel_id=1, source_target_pairs={{0,8},{8,16},{16,24},{24,32},{32,40},{40,48},{48,56},{56,64},{64,7... | collective-permute-start | bytes 983048 | tf_op jit(solution)/shard_map/ppermute | solution.py:19
  378.4 14.5 %collective-permute-start.13 = (f32[64,1280]{1,0:T(8,128)S(1)}, f32[64,1280]{1,0:T(8,128)}, u32[]{:S(2)}, u32[]{:S(2)}) collective-permute-start(f32[64,1280]{1,0:T(8,128)S(1)} %get-tuple-element.515), channel_id=1, source_target_pairs={{8,0},{16,8},{24,16},{32,24},{40,32},{48,40},{56,48},{64,56},{72,6... | collective-permute-start | bytes 983048 | tf_op jit(solution)/shard_map/ppermute | solution.py:19
  386.5 55.2 %copy-start.44 = (f32[64]{0:T(128)}, f32[64]{0:T(128)S(1)}, u32[]{:S(2)}) copy-start(f32[64]{0:T(128)S(1)} %add_rsqrt_fusion.1) | copy-start | bytes 772
  387.1 8.1 %copy-start.37 = (f32[832,64]{1,0:T(8,128)S(1)}, f32[832,64]{1,0:T(8,128)}, u32[]{:S(2)}) copy-start(f32[832,64]{1,0:T(8,128)} %copy-done.36) | copy-start | bytes 638980
  387.1 13.1 %collective-permute-start.22 = (f32[64,2048]{1,0:T(8,128)S(1)}, f32[64,2048]{1,0:T(8,128)S(1)}, u32[]{:S(2)}, u32[]{:S(2)}) collective-permute-start(f32[64,2048]{1,0:T(8,128)S(1)} %fusion.134), channel_id=1, source_target_pairs={{0,1},{1,0},{2,3},{3,2},{4,5},{5,4},{6,7},{7,6},{8,9},{9,8},{10,11... | collective-permute-start | bytes 1572872 | tf_op jit(solution)/shard_map/ppermute | solution.py:33
  400.3 15.1 %copy-start.41 = (s32[16384]{0:T(1024)S(1)}, s32[16384]{0:T(1024)}, u32[]{:S(2)}) copy-start(s32[16384]{0:T(1024)} %copy-done.40) | copy-start | bytes 196612
  400.3 14.6 %collective-permute-start.23 = (f32[64,2048]{1,0:T(8,128)S(1)}, f32[64,2048]{1,0:T(8,128)S(1)}, u32[]{:S(2)}, u32[]{:S(2)}) collective-permute-start(f32[64,2048]{1,0:T(8,128)S(1)} %add.366), channel_id=1, source_target_pairs={{0,2},{1,3},{2,0},{3,1},{4,6},{5,7},{6,4},{7,5},{8,10},{9,11},{10,... | collective-permute-start | bytes 1572872 | tf_op jit(solution)/shard_map/ppermute | solution.py:33
  414.9 11.2 %collective-permute-start.24 = (f32[64,2048]{1,0:T(8,128)S(1)}, f32[64,2048]{1,0:T(8,128)S(1)}, u32[]{:S(2)}, u32[]{:S(2)}) collective-permute-start(f32[64,2048]{1,0:T(8,128)S(1)} %add.367), channel_id=1, source_target_pairs={{0,4},{1,5},{2,6},{3,7},{4,0},{5,1},{6,2},{7,3},{8,12},{9,13},{10,... | collective-permute-start | bytes 1572872 | tf_op jit(solution)/shard_map/ppermute | solution.py:33
  426.1 15.7 %copy-start.25 = (f32[64,2048]{1,0:T(8,128)}, f32[64,2048]{1,0:T(8,128)S(1)}, u32[]{:S(2)}) copy-start(f32[64,2048]{1,0:T(8,128)S(1)} %add.368) | copy-start | bytes 1572868
  426.2 15.6 %collective-permute-start.25 = (f32[64,1280]{1,0:T(8,128)S(1)}, f32[64,1280]{1,0:T(8,128)S(1)}, u32[]{:S(2)}, u32[]{:S(2)}) collective-permute-start(f32[64,1280]{1,0:T(8,128)S(1)} %get-tuple-element.518), channel_id=1, source_target_pairs={{0,8},{8,16},{16,24},{24,32},{32,40},{40,48},{48,56},{56,64},{64,7... | collective-permute-start | bytes 983048 | tf_op jit(solution)/shard_map/ppermute | solution.py:19
  428.1 13.7 %collective-permute-start.26 = (f32[64,1280]{1,0:T(8,128)S(1)}, f32[64,1280]{1,0:T(8,128)S(1)}, u32[]{:S(2)}, u32[]{:S(2)}) collective-permute-start(f32[64,1280]{1,0:T(8,128)S(1)} %get-tuple-element.519), channel_id=1, source_target_pairs={{8,0},{16,8},{24,16},{32,24},{40,32},{48,40},{56,48},{64,56},{72,6... | collective-permute-start | bytes 983048 | tf_op jit(solution)/shard_map/ppermute | solution.py:19
  470.2 3.3 copy-start.18
  488.5 3.3 copy-start.18
  536.3 12.2 %collective-permute-start.27 = (f32[64,1280]{1,0:T(8,128)}, f32[64,1280]{1,0:T(8,128)S(1)}, u32[]{:S(2)}, u32[]{:S(2)}) collective-permute-start(f32[64,1280]{1,0:T(8,128)} %get-tuple-element.512), channel_id=1, source_target_pairs={{0,8},{8,16},{16,24},{24,32},{32,40},{40,48},{48,56},{56,64},{64,7... | collective-permute-start | bytes 983048 | tf_op jit(solution)/shard_map/ppermute | solution.py:19
  538.2 11.8 %collective-permute-start.28 = (f32[64,1280]{1,0:T(8,128)S(1)}, f32[64,1280]{1,0:T(8,128)}, u32[]{:S(2)}, u32[]{:S(2)}) collective-permute-start(f32[64,1280]{1,0:T(8,128)S(1)} %get-tuple-element.513), channel_id=1, source_target_pairs={{8,0},{16,8},{24,16},{32,24},{40,32},{48,40},{56,48},{64,56},{72,6... | collective-permute-start | bytes 983048 | tf_op jit(solution)/shard_map/ppermute | solution.py:19
  597.6 3.3 copy-start.20
  645.4 9.1 %collective-permute-start.29 = (bf16[64,256]{1,0:T(8,128)(2,1)S(1)}, bf16[64,256]{1,0:T(8,128)(2,1)S(1)}, u32[]{:S(2)}, u32[]{:S(2)}) collective-permute-start(bf16[64,256]{1,0:T(8,128)(2,1)S(1)} %slice.498), channel_id=1, source_target_pairs={{0,8},{8,16},{16,24},{24,32},{32,40},{40,48},{48,56},{56,64},{64,7... | collective-permute-start | bytes 98312 | tf_op jit(solution)/shard_map/ppermute | solution.py:19
  692.4 1.8 collective-permute-start.30
  694.3 11.9 %collective-permute-start.31 = (f32[832,64]{1,0:T(8,128)S(1)}, f32[832,64]{1,0:T(8,128)S(1)}, u32[]{:S(2)}, u32[]{:S(2)}) collective-permute-start(f32[832,64]{1,0:T(8,128)S(1)} %fusion.193), channel_id=1, source_target_pairs={{0,16},{8,24},{16,0},{24,8},{32,48},{40,56},{48,32},{56,40},{64,80... | collective-permute-start | bytes 638984 | tf_op jit(solution)/shard_map/ppermute | solution.py:33
  706.3 25.2 %copy-start.32 = (f32[512,64]{1,0:T(8,128)S(1)}, f32[512,64]{1,0:T(8,128)}, u32[]{:S(2)}) copy-start(f32[512,64]{1,0:T(8,128)} %copy-done.31) | copy-start | bytes 393220
  706.3 25.2 %copy-start.45 = (f32[64]{0:T(128)S(1)}, f32[64]{0:T(128)}, u32[]{:S(2)}) copy-start(f32[64]{0:T(128)} %copy-done.44) | copy-start | bytes 772
  706.3 12.6 %collective-permute-start.32 = (f32[832,64]{1,0:T(8,128)S(1)}, f32[832,64]{1,0:T(8,128)S(1)}, u32[]{:S(2)}, u32[]{:S(2)}) collective-permute-start(f32[832,64]{1,0:T(8,128)S(1)} %add.374), channel_id=1, source_target_pairs={{0,32},{8,40},{16,48},{24,56},{32,0},{40,8},{48,16},{56,24},{64,96... | collective-permute-start | bytes 638984 | tf_op jit(solution)/shard_map/ppermute | solution.py:33
  719.0 11.7 %collective-permute-start.33 = (f32[832,64]{1,0:T(8,128)S(1)}, f32[832,64]{1,0:T(8,128)S(1)}, u32[]{:S(2)}, u32[]{:S(2)}) collective-permute-start(f32[832,64]{1,0:T(8,128)S(1)} %add.375), channel_id=1, source_target_pairs={{0,64},{8,72},{16,80},{24,88},{32,96},{40,104},{48,112},{56,120},{... | collective-permute-start | bytes 638984 | tf_op jit(solution)/shard_map/ppermute | solution.py:33
  732.6 4.0 collective-permute-start.34
  736.6 3.9 collective-permute-start.35
  740.5 5.4 collective-permute-start.36
  (101 other events, 193.2 us)

commit v3 on v2

--- a/solution.py
+++ b/solution.py
@@ -75,8 +75,16 @@
             )
         )
     stacked = jnp.concatenate(grads, axis=0).reshape((lag_blocks + 1) * atoms_here, block_width * block_width)
-    bands = jnp.dot(stacked, skew.astype(jnp.float32).T, precision=highest)
-    bands = bands.reshape(lag_blocks + 1, atoms_here, 2 * block_width)
+    pieces = []
+    rest = stacked
+    for _ in range(3):
+        piece = rest.astype(jnp.bfloat16)
+        pieces.append(piece)
+        rest = rest - piece.astype(jnp.float32)
+    split = jnp.concatenate(pieces, axis=0)
+    bands = jnp.dot(split, skew.T, preferred_element_type=jnp.float32)
+    bands = bands.reshape(3, (lag_blocks + 1) * atoms_here, 2 * block_width)
+    bands = (bands[0] + bands[1] + bands[2]).reshape(lag_blocks + 1, atoms_here, 2 * block_width)
     total = jnp.zeros((atoms_here, tap_count + 3 * block_width), jnp.float32)
     for offset in range(lag_blocks + 1):
         start = offset * block_width + 1
@@ -110,7 +118,7 @@
     for offset, matrix in enumerate(matrices):
         window = extended[:, offset : offset + block_count]
         summed = summed + jnp.einsum(
-            "kbi,kmi->kbm", window, matrix, preferred_element_type=jnp.float32, precision=highest
+            "kbi,kim->kbm", window, matrix, preferred_element_type=jnp.float32, precision=highest
         )
     return summed.reshape(atoms_here, seg_len)
 
@@ -154,24 +162,28 @@
             return jnp.dot(own_gram, rebuilt_part, precision=highest)
 
         matrices = toeplitz(kernel_b, block_width, skew)
+        flipped = [jnp.swapaxes(matrix, 1, 2) for matrix in matrices]
         step_col = step_sizes[:, None]
         limit_col = (step_sizes * thresholds)[:, None]
 
         projected_wide = widened(projected, ghost)
 
-        def shrink_step(iteration, current):
-            rebuilt = convolve_blocks(matrices, current.astype(jnp.bfloat16), zero_rim, block_width)
+        def shrink_step(iteration, carried):
+            current, current_b = carried
+            rebuilt = convolve_blocks(matrices, current_b, zero_rim, block_width)
             residual = (projected_wide - mix_atoms(rebuilt)) * inside[None, :]
-            descent = correlate_blocks(matrices, residual.astype(jnp.bfloat16), zero_rim, block_width)
+            descent = correlate_blocks(flipped, residual.astype(jnp.bfloat16), zero_rim, block_width)
             stepped = current + step_col * descent
-            return (
+            shrunk = (
                 allowed_wide[None, :]
                 * jnp.sign(stepped)
                 * jnp.maximum(jnp.abs(stepped) - limit_col, 0.0)
             )
+            return (shrunk, shrunk.astype(jnp.bfloat16))
 
         for chunk in range(ITERS // CHUNK):
-            wide = lax.fori_loop(0, CHUNK, shrink_step, widened(latent, ghost))
+            wide = widened(latent, ghost)
+            wide, _ = lax.fori_loop(0, CHUNK, shrink_step, (wide, wide.astype(jnp.bfloat16)))
             latent = wide[:, ghost : ghost + seg_len]
         rebuilt, before, latent_b = reconstruct(matrices, latent, block_width, tap_count)
         rebuilt_b = rebuilt.astype(jnp.bfloat16)

time: 758 us -> 769 us (1.015)
  local copies, waits for them, and re-layouts: 88.4 us -> 212 us
  matrix products: 300 us -> 238 us
  other arithmetic: 112 us -> 71.9 us
  waiting for transfers between devices: 163 us -> 146 us
    unnamed x68 -> x86, local copies, waits for them, and re-layouts: 21 us -> 96.5 us
    dot_general x62, matrix products: 164 us -> 101 us  [the longest x60 77 us: correlate_blocks(): jnp.einsum('kbi,kim->kbm', window, matrix, preferred_element_type=jnp.flo...]
    mul x20 -> x0, other arithmetic: 59.4 us -> none  [shrink_step(): allowed_wide[None, :] * jnp.sign(stepped)]
    while x200 -> x280, local copies, waits for them, and re-layouts: 29.2 us -> 76.4 us
    convert_element_type x20 -> x26, other arithmetic: 26.6 us -> 43.8 us  [the longest x20 20.4 us: shrink_step(): return (shrunk, shrunk.astype(jnp.bfloat16))]
    ppermute x23, waiting for transfers between devices: 140 us -> 128 us  [butterfly_sum(): lax.ppermute(value, axis, [(i, i ^ distance) for i in range(count)])]
  transfers between devices with their start and end apart: 37 -> 37, of which waited for: 30 -> 29; matrix products, arithmetic and copies ran while one was open for 5% -> 9% of each run, Pallas kernels for 0% -> 0%
where the time goes in v3:
time: 769 us; the launch traced here: 758 us
  matrix products  238 us (31%)
  local copies, waits for them, and re-layouts  212 us (28%)
  waiting for transfers between devices  146 us (19%)
  starting transfers between devices  85 us (11%)
  other arithmetic  71.9 us (9%)
    ppermute x23, waiting for transfers between devices, butterfly_sum(): lax.ppermute(value, axis, [(i, i ^ distance) for i in range(count)])  128 us
    unnamed x86, local copies, waits for them, and re-layouts  96.5 us
    dot_general x66, matrix products, convolve_blocks(): jnp.einsum('kbm,kmi->kbi', window, matrix, preferred_element_type=jnp.flo...  84.4 us
    dot_general x60, matrix products, correlate_blocks(): jnp.einsum('kbi,kim->kbm', window, matrix, preferred_element_type=jnp.flo...  77 us
    while x280, local copies, waits for them, and re-layouts  76.4 us
    ppermute x14, starting transfers between devices, passed_along(): lax.ppermute(value, axis, [(source, source + steps) for source in range(l...  60.1 us
    dot_general x20, matrix products, mix_atoms(): return jnp.dot(own_gram, rebuilt_part, precision=highest)  27.7 us
    ppermute x23, starting transfers between devices, butterfly_sum(): lax.ppermute(value, axis, [(i, i ^ distance) for i in range(count)])  24.9 us
  transfers between devices with their start and end apart: 37, of which 29 were waited for; matrix products, arithmetic and copies ran while one was open for 9% of the time, Pallas kernels for 0%

profile of v3, /device:TPU:4, one launch (start us, length us, event | category | flops | bytes accessed | tf_op | source)
XLA Modules:
  0.0 758.4 jit_solution(11675259244500090505)
XLA Ops:
  7.2 7.3 collective-permute-start.1
  21.3 3.2 collective-permute-start.4
  30.9 6.5 collective-permute-done.5
  39.7 9.8 %collective-permute-done.6 = f32[64,2048]{1,0:T(8,128)S(1)} collective-permute-done((f32[64,2048]{1,0:T(8,128)S(1)}, f32[64,2048]{1,0:T(8,128)S(1)}, u32[]{:S(2)}, u32[]{:S(2)}) %collective-permute-start.6) | collective-permute-done | bytes 524320 | tf_op jit(solution)/shard_map/ppermute | solution.py:33
  49.6 4.8 collective-permute-start.7
  60.1 4.1 copy.70
  64.1 4.1 copy.71
  68.2 4.1 copy.72
  76.6 7.8 %collective-permute-start.9 = (f32[64,1280]{1,0:T(8,128)S(1)}, f32[64,1280]{1,0:T(8,128)S(1)}, u32[]{:S(2)}, u32[]{:S(2)}) collective-permute-start(f32[64,1280]{1,0:T(8,128)S(1)} %get-tuple-element.857), channel_id=1, source_target_pairs={{8,0},{16,8},{24,16},{32,24},{40,32},{48,40},{56,48},{64,56},{72,6... | collective-permute-start | bytes 983048 | tf_op jit(solution)/shard_map/ppermute | solution.py:19
  89.6 74.5 %while.58 = (s32[]{:T(128)}, f32[64,4608]{1,0:T(8,128)}, bf16[64,4608]{1,0:T(8,128)(2,1)S(1)}, f32[4608]{0:T(1024)S(1)}, f32[64,1]{0,1:T(1,128)S(1)}, /*index=5*...) while((s32[]{:T(128)}, f32[64,4608]{1,0:T(8,128)}, ...), condition=%wide.region_3.4_spmd.clone, body=%wide.region_2.3_spmd.clone.sunk | while | flops 684218880 | bytes 87890792 | solution.py:186
  90.0 2.4 fusion.356
  104.9 2.4 fusion.356
  134.7 2.4 fusion.356
  149.6 2.4 fusion.356
  167.8 7.6 %collective-permute-start.11 = (f32[64,1280]{1,0:T(8,128)S(1)}, f32[64,1280]{1,0:T(8,128)}, u32[]{:S(2)}, u32[]{:S(2)}) collective-permute-start(f32[64,1280]{1,0:T(8,128)S(1)} %get-tuple-element.853), channel_id=1, source_target_pairs={{8,0},{16,8},{24,16},{32,24},{40,32},{48,40},{56,48},{64,56},{72,6... | collective-permute-start | bytes 983048 | tf_op jit(solution)/shard_map/ppermute | solution.py:19
  183.2 74.5 %while.59 = (s32[]{:T(128)}, f32[64,4608]{1,0:T(8,128)}, bf16[64,4608]{1,0:T(8,128)(2,1)S(1)}, f32[4608]{0:T(1024)S(1)}, f32[64,1]{0,1:T(1,128)S(1)}, /*index=5*...) while((s32[]{:T(128)}, f32[64,4608]{1,0:T(8,128)}, ...), condition=%wide.region_5.6_spmd.clone, body=%wide.region_4.5_spmd.clone.sunk | while | flops 684218880 | bytes 87890792 | solution.py:186
  183.6 2.4 fusion.375
  198.5 2.4 fusion.375
  213.4 2.4 fusion.375
  243.2 2.4 fusion.375
  263.7 4.2 collective-permute-done.14
  282.1 4.6 copy-done.25
  286.7 10.1 %fusion.104 = (bf16[192,16384]{1,0:T(8,128)(2,1)}, bf16[192,16384]{1,0:T(8,128)(2,1)}) fusion(f32[24,8,128,128]{3,2,1,0:T(8,128)S(1)} %bitcast.363), kind=kLoop, calls=%fused_computation.151 | loop fusion | flops 22020096 | bytes 25165824 | tf_op jit(solution)/shard_map/convert_element_type | solution.py:81
  296.8 18.1 %copy.203 = bf16[24,8,128,128]{3,1,2,0:T(8,128)(2,1)} copy(f32[24,8,128,128]{3,2,1,0:T(8,128)} %bitcast.364) | data formatting | bytes 18874368
  316.5 11.7 %fusion.80 = f32[576,256]{0,1:T(8,128)S(1)} fusion(bf16[192,16384]{1,0:T(8,128)(2,1)} %get-tuple-element.841, bf16[192,16384]{1,0:T(8,128)(2,1)} %get-tuple-element.840, bf16[192,16384]{1,0:T(8,128)(2,1)} %bitcast.377, s32[16384]{0:T(1024)S(1)} %copy-done.53), kind=kOutput, calls=%fused_computation.117 | convolution fusion | flops 4901044224 | bytes 19529728 | tf_op jit(solution)/shard_map/dot_general | solution.py:85
  334.3 11.8 %collective-permute-done.16 = f32[832,64]{1,0:T(8,128)S(1)} collective-permute-done((f32[832,64]{1,0:T(8,128)S(1)}, f32[832,64]{1,0:T(8,128)S(1)}, u32[]{:S(2)}, u32[]{:S(2)}) %collective-permute-start.16) | collective-permute-done | bytes 213024 | tf_op jit(solution)/shard_map/ppermute | solution.py:33
  346.3 12.5 %collective-permute-done.17 = f32[832,64]{1,0:T(8,128)S(1)} collective-permute-done((f32[832,64]{1,0:T(8,128)S(1)}, f32[832,64]{1,0:T(8,128)S(1)}, u32[]{:S(2)}, u32[]{:S(2)}) %collective-permute-start.17) | collective-permute-done | bytes 213024 | tf_op jit(solution)/shard_map/ppermute | solution.py:33
  361.8 7.3 collective-permute-start.13
  375.4 3.1 collective-permute-done.19
  385.0 2.7 collective-permute-done.21
  391.2 7.1 collective-permute-done.22
  400.5 11.0 %collective-permute-done.23 = f32[64,2048]{1,0:T(8,128)S(1)} collective-permute-done((f32[64,2048]{1,0:T(8,128)S(1)}, f32[64,2048]{1,0:T(8,128)S(1)}, u32[]{:S(2)}, u32[]{:S(2)}) %collective-permute-start.23) | collective-permute-done | bytes 524320 | tf_op jit(solution)/shard_map/ppermute | solution.py:33
  414.1 8.2 %collective-permute-done.24 = f32[64,2048]{1,0:T(8,128)S(1)} collective-permute-done((f32[64,2048]{1,0:T(8,128)S(1)}, f32[64,2048]{1,0:T(8,128)S(1)}, u32[]{:S(2)}, u32[]{:S(2)}) %collective-permute-start.24) | collective-permute-done | bytes 524320 | tf_op jit(solution)/shard_map/ppermute | solution.py:33
  425.3 7.3 collective-permute-start.26
  432.5 2.6 slice_bitcast_fusion
  437.0 4.3 copy.84
  441.3 3.5 copy.125
  444.8 4.0 copy.85
  448.9 3.5 copy.126
  452.4 4.1 copy.86
  458.8 74.5 %while.60 = (s32[]{:T(128)}, f32[64,4608]{1,0:T(8,128)}, bf16[64,4608]{1,0:T(8,128)(2,1)S(1)}, f32[4608]{0:T(1024)S(1)}, f32[64,1]{0,1:T(1,128)S(1)}, /*index=5*...) while((s32[]{:T(128)}, f32[64,4608]{1,0:T(8,128)}, ...), condition=%wide.region_11.12_spmd.clone, body=%wide.region_10.11_spmd.clone.sunk | while | flops 684218880 | bytes 87890792 | solution.py:186
  459.2 2.4 fusion.394
  474.1 2.4 fusion.394
  489.0 2.4 fusion.394
  503.9 2.4 fusion.394
  518.8 2.4 fusion.394
  537.0 7.3 collective-permute-start.28
  552.1 74.9 %while.61 = (s32[]{:T(128)}, f32[64,4608]{1,0:T(8,128)}, bf16[64,4608]{1,0:T(8,128)(2,1)S(1)}, f32[4608]{0:T(1024)S(1)}, f32[64,1]{0,1:T(1,128)S(1)}, /*index=5*...) while((s32[]{:T(128)}, f32[64,4608]{1,0:T(8,128)}, ...), condition=%wide.region_13.14_spmd.clone, body=%wide.region_12.13_spmd.clone.sunk | while | flops 684218880 | bytes 87890792 | solution.py:186
  553.0 2.4 fusion.413
  567.9 2.4 fusion.413
  582.8 2.4 fusion.413
  597.6 2.4 fusion.413
  612.5 2.4 fusion.413
  631.8 6.2 collective-permute-done.29
  652.2 4.6 copy-done.26
  656.8 9.9 %fusion.105 = (bf16[192,16384]{1,0:T(8,128)(2,1)}, bf16[192,16384]{1,0:T(8,128)(2,1)}) fusion(f32[24,8,128,128]{3,2,1,0:T(8,128)S(1)} %bitcast.365), kind=kLoop, calls=%fused_computation.152 | loop fusion | flops 22020096 | bytes 25165824 | tf_op jit(solution)/shard_map/convert_element_type | solution.py:81
  666.7 18.1 %copy.202 = bf16[24,8,128,128]{3,1,2,0:T(8,128)(2,1)} copy(f32[24,8,128,128]{3,2,1,0:T(8,128)} %bitcast.366) | data formatting | bytes 18874368
  684.8 12.0 %fusion.86 = f32[576,256]{0,1:T(8,128)S(1)} fusion(bf16[192,16384]{1,0:T(8,128)(2,1)} %get-tuple-element.839, bf16[192,16384]{1,0:T(8,128)(2,1)} %get-tuple-element.838, bf16[192,16384]{1,0:T(8,128)(2,1)} %bitcast.378, s32[16384]{0:T(1024)S(1)} %copy-done.54), kind=kOutput, calls=%fused_computation.123 | convolution fusion | flops 4901044224 | bytes 19529728 | tf_op jit(solution)/shard_map/dot_general | solution.py:85
  704.3 11.8 %collective-permute-done.31 = f32[832,64]{1,0:T(8,128)S(1)} collective-permute-done((f32[832,64]{1,0:T(8,128)S(1)}, f32[832,64]{1,0:T(8,128)S(1)}, u32[]{:S(2)}, u32[]{:S(2)}) %collective-permute-start.31) | collective-permute-done | bytes 213024 | tf_op jit(solution)/shard_map/ppermute | solution.py:33
  716.3 12.5 %collective-permute-done.32 = f32[832,64]{1,0:T(8,128)S(1)} collective-permute-done((f32[832,64]{1,0:T(8,128)S(1)}, f32[832,64]{1,0:T(8,128)S(1)}, u32[]{:S(2)}, u32[]{:S(2)}) %collective-permute-start.32) | collective-permute-done | bytes 213024 | tf_op jit(solution)/shard_map/ppermute | solution.py:33
  729.0 11.6 %collective-permute-done.33 = f32[832,64]{1,0:T(8,128)S(1)} collective-permute-done((f32[832,64]{1,0:T(8,128)S(1)}, f32[832,64]{1,0:T(8,128)S(1)}, u32[]{:S(2)}, u32[]{:S(2)}) %collective-permute-start.33) | collective-permute-done | bytes 213024 | tf_op jit(solution)/shard_map/ppermute | solution.py:33
  743.5 3.0 collective-permute-done.34
  746.5 2.5 collective-permute-start.35
  752.2 4.1 collective-permute-done.36
  (776 shorter events, 405.2 us)
Async XLA Ops:
  0.6 26.9 %copy-start = (bf16[512,2048]{1,0:T(8,128)(2,1)S(1)}, bf16[512,2048]{1,0:T(8,128)(2,1)}, u32[]{:S(2)}) copy-start(bf16[512,2048]{1,0:T(8,128)(2,1)} %param.27) | copy-start | bytes 6291460
  0.6 26.9 %copy-start.45 = (f32[512,64]{0,1:T(8,128)S(1)}, f32[512,64]{0,1:T(8,128)}, u32[]{:S(2)}) copy-start(f32[512,64]{0,1:T(8,128)} %param.28) | copy-start | bytes 393220
  2.0 15.2 %collective-permute-start.2 = (f32[64,64]{1,0:T(8,128)S(1)}, f32[64,64]{1,0:T(8,128)S(1)}, u32[]{:S(2)}, u32[]{:S(2)}) collective-permute-start(f32[64,64]{1,0:T(8,128)S(1)} %fusion.213), channel_id=1, source_target_pairs={{0,1},{1,0},{2,3},{3,2},{4,5},{5,4},{6,7},{7,6},{8,9},{9,8},{10,11... | collective-permute-start | bytes 49160 | tf_op jit(solution)/shard_map/ppermute | solution.py:33
  5.3 67.0 %collective-permute-start = (f32[64,1280]{1,0:T(8,128)}, f32[64,1280]{1,0:T(8,128)}, u32[]{:S(2)}, u32[]{:S(2)}) collective-permute-start(f32[64,1280]{1,0:T(8,128)} %get-tuple-element.859), channel_id=1, source_target_pairs={{0,8},{8,16},{16,24},{24,32},{32,40},{40,48},{48,56},{56,64},{64,7... | collective-permute-start | bytes 983048 | tf_op jit(solution)/shard_map/ppermute | solution.py:19
  7.2 77.2 %collective-permute-start.1 = (f32[64,1280]{1,0:T(8,128)}, f32[64,1280]{1,0:T(8,128)}, u32[]{:S(2)}, u32[]{:S(2)}) collective-permute-start(f32[64,1280]{1,0:T(8,128)} %get-tuple-element.858), channel_id=1, source_target_pairs={{8,0},{16,8},{24,16},{32,24},{40,32},{48,40},{56,48},{64,56},{72,6... | collective-permute-start | bytes 983048 | tf_op jit(solution)/shard_map/ppermute | solution.py:19
  14.5 16.3 %copy-start.52 = (s32[16384]{0:T(1024)}, s32[16384]{0:T(1024)S(1)}, u32[]{:S(2)}) copy-start(s32[16384]{0:T(1024)S(1)} %add_bitcast_fusion) | copy-start | bytes 196612
  17.3 4.0 collective-permute-start.3
  21.3 5.4 collective-permute-start.4
  27.5 44.7 %copy-start.55 = (f32[64]{0:T(128)}, f32[64]{0:T(128)S(1)}, u32[]{:S(2)}) copy-start(f32[64]{0:T(128)S(1)} %add_rsqrt_fusion.2) | copy-start | bytes 772
  28.1 9.3 %collective-permute-start.5 = (f32[64,2048]{1,0:T(8,128)S(1)}, f32[64,2048]{1,0:T(8,128)S(1)}, u32[]{:S(2)}, u32[]{:S(2)}) collective-permute-start(f32[64,2048]{1,0:T(8,128)S(1)} %fusion.155), channel_id=1, source_target_pairs={{0,1},{1,0},{2,3},{3,2},{4,5},{5,4},{6,7},{7,6},{8,9},{9,8},{10,11... | collective-permute-start | bytes 1572872 | tf_op jit(solution)/shard_map/ppermute | solution.py:33
  37.4 12.1 %collective-permute-start.6 = (f32[64,2048]{1,0:T(8,128)S(1)}, f32[64,2048]{1,0:T(8,128)S(1)}, u32[]{:S(2)}, u32[]{:S(2)}) collective-permute-start(f32[64,2048]{1,0:T(8,128)S(1)} %add.362), channel_id=1, source_target_pairs={{0,2},{1,3},{2,0},{3,1},{4,6},{5,7},{6,4},{7,5},{8,10},{9,11},{10,... | collective-permute-start | bytes 1572872 | tf_op jit(solution)/shard_map/ppermute | solution.py:33
  39.1 15.3 %copy-start.51 = (f32[64]{0:T(128)S(1)}, f32[64]{0:T(128)}, u32[]{:S(2)}) copy-start(f32[64]{0:T(128)} %param.32) | copy-start | bytes 772
  39.1 15.3 %copy-start.59 = (f32[64]{0:T(128)S(1)}, f32[64]{0:T(128)}, u32[]{:S(2)}) copy-start(f32[64]{0:T(128)} %param.31) | copy-start | bytes 772
  49.6 6.7 copy-start.44
  49.6 23.8 %collective-permute-start.7 = (f32[64,2048]{1,0:T(8,128)S(1)}, f32[64,2048]{1,0:T(8,128)}, u32[]{:S(2)}, u32[]{:S(2)}) collective-permute-start(f32[64,2048]{1,0:T(8,128)S(1)} %add.363), channel_id=1, source_target_pairs={{0,4},{1,5},{2,6},{3,7},{4,0},{5,1},{6,2},{7,3},{8,12},{9,13},{10,... | collective-permute-start | bytes 1572872 | tf_op jit(solution)/shard_map/ppermute | solution.py:33
  72.2 12.2 %copy-start.43 = (f32[64,2048]{1,0:T(8,128)S(1)}, f32[64,2048]{1,0:T(8,128)}, u32[]{:S(2)}) copy-start(f32[64,2048]{1,0:T(8,128)} %param.30) | copy-start | bytes 1572868
  74.6 13.8 %copy-start.39 = (f32[64,2048]{1,0:T(8,128)}, f32[64,2048]{1,0:T(8,128)S(1)}, u32[]{:S(2)}) copy-start(f32[64,2048]{1,0:T(8,128)S(1)} %add.364) | copy-start | bytes 1572868
  74.7 12.0 %collective-permute-start.8 = (f32[64,1280]{1,0:T(8,128)S(1)}, f32[64,1280]{1,0:T(8,128)S(1)}, u32[]{:S(2)}, u32[]{:S(2)}) collective-permute-start(f32[64,1280]{1,0:T(8,128)S(1)} %get-tuple-element.856), channel_id=1, source_target_pairs={{0,8},{8,16},{16,24},{24,32},{32,40},{40,48},{48,56},{56,64},{64,7... | collective-permute-start | bytes 983048 | tf_op jit(solution)/shard_map/ppermute | solution.py:19
  76.6 11.8 %collective-permute-start.9 = (f32[64,1280]{1,0:T(8,128)S(1)}, f32[64,1280]{1,0:T(8,128)S(1)}, u32[]{:S(2)}, u32[]{:S(2)}) collective-permute-start(f32[64,1280]{1,0:T(8,128)S(1)} %get-tuple-element.857), channel_id=1, source_target_pairs={{8,0},{16,8},{24,16},{32,24},{40,32},{48,40},{56,48},{64,56},{72,6... | collective-permute-start | bytes 983048 | tf_op jit(solution)/shard_map/ppermute | solution.py:19
  134.7 2.4 copy-start.6
  165.9 12.4 %collective-permute-start.10 = (f32[64,1280]{1,0:T(8,128)}, f32[64,1280]{1,0:T(8,128)S(1)}, u32[]{:S(2)}, u32[]{:S(2)}) collective-permute-start(f32[64,1280]{1,0:T(8,128)} %get-tuple-element.852), channel_id=1, source_target_pairs={{0,8},{8,16},{16,24},{24,32},{32,40},{40,48},{48,56},{56,64},{64,7... | collective-permute-start | bytes 983048 | tf_op jit(solution)/shard_map/ppermute | solution.py:19
  167.8 12.0 %collective-permute-start.11 = (f32[64,1280]{1,0:T(8,128)S(1)}, f32[64,1280]{1,0:T(8,128)}, u32[]{:S(2)}, u32[]{:S(2)}) collective-permute-start(f32[64,1280]{1,0:T(8,128)S(1)} %get-tuple-element.853), channel_id=1, source_target_pairs={{8,0},{16,8},{24,16},{32,24},{40,32},{48,40},{56,48},{64,56},{72,6... | collective-permute-start | bytes 983048 | tf_op jit(solution)/shard_map/ppermute | solution.py:19
  183.6 2.4 copy-start.7
  198.5 2.4 copy-start.7
  243.2 2.4 copy-start.7
  258.8 9.1 %collective-permute-start.14 = (bf16[64,256]{1,0:T(8,128)(2,1)S(1)}, bf16[64,256]{1,0:T(8,128)(2,1)S(1)}, u32[]{:S(2)}, u32[]{:S(2)}) collective-permute-start(bf16[64,256]{1,0:T(8,128)(2,1)S(1)} %slice.511), channel_id=1, source_target_pairs={{0,8},{8,16},{16,24},{24,32},{32,40},{40,48},{48,56},{56,64},{64,7... | collective-permute-start | bytes 98312 | tf_op jit(solution)/shard_map/ppermute | solution.py:19
  282.1 4.6 copy-start.25
  332.3 26.7 %copy-start.32 = (f32[64,4608]{1,0:T(8,128)S(1)}, f32[64,4608]{1,0:T(8,128)}, u32[]{:S(2)}) copy-start(f32[64,4608]{1,0:T(8,128)} %get-tuple-element.384) | copy-start | bytes 3538948
  332.3 1.8 collective-permute-start.15
  334.2 11.9 %collective-permute-start.16 = (f32[832,64]{1,0:T(8,128)S(1)}, f32[832,64]{1,0:T(8,128)S(1)}, u32[]{:S(2)}, u32[]{:S(2)}) collective-permute-start(f32[832,64]{1,0:T(8,128)S(1)} %fusion.198), channel_id=1, source_target_pairs={{0,16},{8,24},{16,0},{24,8},{32,48},{40,56},{48,32},{56,40},{64,80... | collective-permute-start | bytes 638984 | tf_op jit(solution)/shard_map/ppermute | solution.py:33
  346.2 26.0 %copy-start.46 = (f32[512,64]{0,1:T(8,128)S(1)}, f32[512,64]{0,1:T(8,128)}, u32[]{:S(2)}) copy-start(f32[512,64]{0,1:T(8,128)} %param.28) | copy-start | bytes 393220
  346.2 26.0 %copy-start.56 = (f32[64]{0:T(128)S(1)}, f32[64]{0:T(128)}, u32[]{:S(2)}) copy-start(f32[64]{0:T(128)} %copy-done.55) | copy-start | bytes 772
  346.2 12.6 %collective-permute-start.17 = (f32[832,64]{1,0:T(8,128)S(1)}, f32[832,64]{1,0:T(8,128)S(1)}, u32[]{:S(2)}, u32[]{:S(2)}) collective-permute-start(f32[832,64]{1,0:T(8,128)S(1)} %add.372), channel_id=1, source_target_pairs={{0,32},{8,40},{16,48},{24,56},{32,0},{40,8},{48,16},{56,24},{64,96... | collective-permute-start | bytes 638984 | tf_op jit(solution)/shard_map/ppermute | solution.py:33
  358.9 11.7 %collective-permute-start.18 = (f32[832,64]{1,0:T(8,128)S(1)}, f32[832,64]{1,0:T(8,128)S(1)}, u32[]{:S(2)}, u32[]{:S(2)}) collective-permute-start(f32[832,64]{1,0:T(8,128)S(1)} %add.373), channel_id=1, source_target_pairs={{0,64},{8,72},{16,80},{24,88},{32,96},{40,104},{48,112},{56,120},{... | collective-permute-start | bytes 638984 | tf_op jit(solution)/shard_map/ppermute | solution.py:33
  359.9 23.0 %collective-permute-start.12 = (f32[64,1280]{1,0:T(8,128)}, f32[64,1280]{1,0:T(8,128)}, u32[]{:S(2)}, u32[]{:S(2)}) collective-permute-start(f32[64,1280]{1,0:T(8,128)} %get-tuple-element.850), channel_id=1, source_target_pairs={{0,8},{8,16},{16,24},{24,32},{32,40},{40,48},{48,56},{56,64},{64,7... | collective-permute-start | bytes 983048 | tf_op jit(solution)/shard_map/ppermute | solution.py:19
  361.8 21.1 %collective-permute-start.13 = (f32[64,1280]{1,0:T(8,128)}, f32[64,1280]{1,0:T(8,128)}, u32[]{:S(2)}, u32[]{:S(2)}) collective-permute-start(f32[64,1280]{1,0:T(8,128)} %get-tuple-element.851), channel_id=1, source_target_pairs={{8,0},{16,8},{24,16},{32,24},{40,32},{48,40},{56,48},{64,56},{72,6... | collective-permute-start | bytes 983048 | tf_op jit(solution)/shard_map/ppermute | solution.py:19
  373.8 14.8 %copy-start.41 = (f32[512,64]{1,0:T(8,128)}, f32[512,64]{1,0:T(8,128)S(1)}, u32[]{:S(2)}) copy-start(f32[512,64]{1,0:T(8,128)S(1)} %slice_subtract_fusion.1) | copy-start | bytes 393220
  374.4 4.0 collective-permute-start.19
  378.4 3.9 collective-permute-start.20
  382.4 5.4 collective-permute-start.21
  388.6 67.9 %copy-start.57 = (f32[64]{0:T(128)}, f32[64]{0:T(128)S(1)}, u32[]{:S(2)}) copy-start(f32[64]{0:T(128)S(1)} %add_rsqrt_fusion.1) | copy-start | bytes 772
  388.6 2.6 copy-start.48
  389.1 9.3 %collective-permute-start.22 = (f32[64,2048]{1,0:T(8,128)S(1)}, f32[64,2048]{1,0:T(8,128)S(1)}, u32[]{:S(2)}, u32[]{:S(2)}) collective-permute-start(f32[64,2048]{1,0:T(8,128)S(1)} %fusion.138), channel_id=1, source_target_pairs={{0,1},{1,0},{2,3},{3,2},{4,5},{5,4},{6,7},{7,6},{8,9},{9,8},{10,11... | collective-permute-start | bytes 1572872 | tf_op jit(solution)/shard_map/ppermute | solution.py:33
  398.5 13.0 %collective-permute-start.23 = (f32[64,2048]{1,0:T(8,128)S(1)}, f32[64,2048]{1,0:T(8,128)S(1)}, u32[]{:S(2)}, u32[]{:S(2)}) collective-permute-start(f32[64,2048]{1,0:T(8,128)S(1)} %add.380), channel_id=1, source_target_pairs={{0,2},{1,3},{2,0},{3,1},{4,6},{5,7},{6,4},{7,5},{8,10},{9,11},{10,... | collective-permute-start | bytes 1572872 | tf_op jit(solution)/shard_map/ppermute | solution.py:33
  411.6 10.8 %collective-permute-start.24 = (f32[64,2048]{1,0:T(8,128)S(1)}, f32[64,2048]{1,0:T(8,128)S(1)}, u32[]{:S(2)}, u32[]{:S(2)}) collective-permute-start(f32[64,2048]{1,0:T(8,128)S(1)} %add.381), channel_id=1, source_target_pairs={{0,4},{1,5},{2,6},{3,7},{4,0},{5,1},{6,2},{7,3},{8,12},{9,13},{10,... | collective-permute-start | bytes 1572872 | tf_op jit(solution)/shard_map/ppermute | solution.py:33
  422.4 34.2 %copy-start.37 = (f32[64,2048]{1,0:T(8,128)}, f32[64,2048]{1,0:T(8,128)S(1)}, u32[]{:S(2)}) copy-start(f32[64,2048]{1,0:T(8,128)S(1)} %add.382) | copy-start | bytes 1572868
  423.4 33.2 %collective-permute-start.25 = (f32[64,1280]{1,0:T(8,128)}, f32[64,1280]{1,0:T(8,128)}, u32[]{:S(2)}, u32[]{:S(2)}) collective-permute-start(f32[64,1280]{1,0:T(8,128)} %get-tuple-element.854), channel_id=1, source_target_pairs={{0,8},{8,16},{16,24},{24,32},{32,40},{40,48},{48,56},{56,64},{64,7... | collective-permute-start | bytes 983048 | tf_op jit(solution)/shard_map/ppermute | solution.py:19
  425.3 31.3 %collective-permute-start.26 = (f32[64,1280]{1,0:T(8,128)}, f32[64,1280]{1,0:T(8,128)}, u32[]{:S(2)}, u32[]{:S(2)}) collective-permute-start(f32[64,1280]{1,0:T(8,128)} %get-tuple-element.855), channel_id=1, source_target_pairs={{8,0},{16,8},{24,16},{32,24},{40,32},{48,40},{56,48},{64,56},{72,6... | collective-permute-start | bytes 983048 | tf_op jit(solution)/shard_map/ppermute | solution.py:19
  503.9 2.4 copy-start.11
  535.1 12.2 %collective-permute-start.27 = (f32[64,1280]{1,0:T(8,128)}, f32[64,1280]{1,0:T(8,128)S(1)}, u32[]{:S(2)}, u32[]{:S(2)}) collective-permute-start(f32[64,1280]{1,0:T(8,128)} %get-tuple-element.848), channel_id=1, source_target_pairs={{0,8},{8,16},{16,24},{24,32},{32,40},{40,48},{48,56},{56,64},{64,7... | collective-permute-start | bytes 983048 | tf_op jit(solution)/shard_map/ppermute | solution.py:19
  537.0 11.8 %collective-permute-start.28 = (f32[64,1280]{1,0:T(8,128)S(1)}, f32[64,1280]{1,0:T(8,128)}, u32[]{:S(2)}, u32[]{:S(2)}) collective-permute-start(f32[64,1280]{1,0:T(8,128)S(1)} %get-tuple-element.849), channel_id=1, source_target_pairs={{8,0},{16,8},{24,16},{32,24},{40,32},{48,40},{56,48},{64,56},{72,6... | collective-permute-start | bytes 983048 | tf_op jit(solution)/shard_map/ppermute | solution.py:19
  567.9 2.4 copy-start.12
  628.9 9.1 %collective-permute-start.29 = (bf16[64,256]{1,0:T(8,128)(2,1)S(1)}, bf16[64,256]{1,0:T(8,128)(2,1)S(1)}, u32[]{:S(2)}, u32[]{:S(2)}) collective-permute-start(bf16[64,256]{1,0:T(8,128)(2,1)S(1)} %slice.531), channel_id=1, source_target_pairs={{0,8},{8,16},{16,24},{24,32},{32,40},{40,48},{48,56},{56,64},{64,7... | collective-permute-start | bytes 98312 | tf_op jit(solution)/shard_map/ppermute | solution.py:19
  652.2 4.6 copy-start.26
  666.7 18.1 %copy-start.54 = (s32[16384]{0:T(1024)S(1)}, s32[16384]{0:T(1024)}, u32[]{:S(2)}) copy-start(s32[16384]{0:T(1024)} %copy-done.52) | copy-start | bytes 196612
  702.3 1.8 collective-permute-start.30
  704.2 37.2 %copy-start.42 = (f32[512,64]{1,0:T(8,128)S(1)}, f32[512,64]{1,0:T(8,128)}, u32[]{:S(2)}) copy-start(f32[512,64]{1,0:T(8,128)} %copy-done.41) | copy-start | bytes 393220
  704.2 37.2 %copy-start.58 = (f32[64]{0:T(128)S(1)}, f32[64]{0:T(128)}, u32[]{:S(2)}) copy-start(f32[64]{0:T(128)} %copy-done.57) | copy-start | bytes 772
  704.2 11.9 %collective-permute-start.31 = (f32[832,64]{1,0:T(8,128)S(1)}, f32[832,64]{1,0:T(8,128)S(1)}, u32[]{:S(2)}, u32[]{:S(2)}) collective-permute-start(f32[832,64]{1,0:T(8,128)S(1)} %fusion.197), channel_id=1, source_target_pairs={{0,16},{8,24},{16,0},{24,8},{32,48},{40,56},{48,32},{56,40},{64,80... | collective-permute-start | bytes 638984 | tf_op jit(solution)/shard_map/ppermute | solution.py:33
  716.2 12.6 %collective-permute-start.32 = (f32[832,64]{1,0:T(8,128)S(1)}, f32[832,64]{1,0:T(8,128)S(1)}, u32[]{:S(2)}, u32[]{:S(2)}) collective-permute-start(f32[832,64]{1,0:T(8,128)S(1)} %add.390), channel_id=1, source_target_pairs={{0,32},{8,40},{16,48},{24,56},{32,0},{40,8},{48,16},{56,24},{64,96... | collective-permute-start | bytes 638984 | tf_op jit(solution)/shard_map/ppermute | solution.py:33
  728.9 11.7 %collective-permute-start.33 = (f32[832,64]{1,0:T(8,128)S(1)}, f32[832,64]{1,0:T(8,128)S(1)}, u32[]{:S(2)}, u32[]{:S(2)}) collective-permute-start(f32[832,64]{1,0:T(8,128)S(1)} %add.391), channel_id=1, source_target_pairs={{0,64},{8,72},{16,80},{24,88},{32,96},{40,104},{48,112},{56,120},{... | collective-permute-start | bytes 638984 | tf_op jit(solution)/shard_map/ppermute | solution.py:33
  742.5 4.0 collective-permute-start.34
  746.5 4.4 collective-permute-start.35
  750.9 5.4 collective-permute-start.36
  (145 other events, 232.7 us)

commit v4 on v3

--- a/solution.py
+++ b/solution.py
@@ -36,13 +36,22 @@
     return value
 
 
-def one_hot_skew(block_width, tap_span):
+def one_hot_skew(block_width, tap_span, transposed=False):
     shape = (tap_span, block_width, block_width)
     d = lax.broadcasted_iota(jnp.int32, shape, 0)
-    m = lax.broadcasted_iota(jnp.int32, shape, 1)
-    i = lax.broadcasted_iota(jnp.int32, shape, 2)
+    m = lax.broadcasted_iota(jnp.int32, shape, 2 if transposed else 1)
+    i = lax.broadcasted_iota(jnp.int32, shape, 1 if transposed else 2)
     hit = d == i - m + (block_width - 1)
     return jnp.where(hit, 1.0, 0.0).astype(jnp.bfloat16).reshape(tap_span, block_width * block_width)
+
+
+def band_sums_matrix(block_width, tap_span):
+    shape = (block_width, block_width, tap_span)
+    m = lax.broadcasted_iota(jnp.int32, shape, 0)
+    i = lax.broadcasted_iota(jnp.int32, shape, 1)
+    d = lax.broadcasted_iota(jnp.int32, shape, 2)
+    hit = d == i - m + (block_width - 1)
+    return jnp.where(hit, 1.0, 0.0).reshape(block_width * block_width, tap_span)
 
 
 def toeplitz(kernel_taps, block_width, skew):
@@ -60,7 +69,7 @@
     return [flat[off] for off in range(lag_blocks + 1)]
 
 
-def lag_sums(code_ext, others, block_width, tap_count, skew):
+def lag_sums(code_ext, others, block_width, tap_count):
     atoms_here, seg_len = others.shape
     block_count = seg_len // block_width
     lag_blocks = tap_count // block_width
@@ -75,16 +84,8 @@
             )
         )
     stacked = jnp.concatenate(grads, axis=0).reshape((lag_blocks + 1) * atoms_here, block_width * block_width)
-    pieces = []
-    rest = stacked
-    for _ in range(3):
-        piece = rest.astype(jnp.bfloat16)
-        pieces.append(piece)
-        rest = rest - piece.astype(jnp.float32)
-    split = jnp.concatenate(pieces, axis=0)
-    bands = jnp.dot(split, skew.T, preferred_element_type=jnp.float32)
-    bands = bands.reshape(3, (lag_blocks + 1) * atoms_here, 2 * block_width)
-    bands = (bands[0] + bands[1] + bands[2]).reshape(lag_blocks + 1, atoms_here, 2 * block_width)
+    bands = jnp.dot(stacked, band_sums_matrix(block_width, 2 * block_width), precision=lax.Precision.HIGH)
+    bands = bands.reshape(lag_blocks + 1, atoms_here, 2 * block_width)
     total = jnp.zeros((atoms_here, tap_count + 3 * block_width), jnp.float32)
     for offset in range(lag_blocks + 1):
         start = offset * block_width + 1
@@ -134,6 +135,7 @@
     atoms_all, tap_count = temporal.shape
     block_width = 128
     skew = one_hot_skew(block_width, 2 * block_width)
+    skew_flipped = one_hot_skew(block_width, 2 * block_width, transposed=True)
     ghost = GHOST_BLOCKS * block_width
     wide_positions = lax.axis_index("seg") * seg_len - ghost + lax.iota(jnp.int32, seg_len + 2 * ghost)
     wide_crosses = (wide_positions[None, :] < breaks[:, None]) & (
@@ -162,7 +164,7 @@
             return jnp.dot(own_gram, rebuilt_part, precision=highest)
 
         matrices = toeplitz(kernel_b, block_width, skew)
-        flipped = [jnp.swapaxes(matrix, 1, 2) for matrix in matrices]
+        flipped = toeplitz(kernel_b, block_width, skew_flipped)
         step_col = step_sizes[:, None]
         limit_col = (step_sizes * thresholds)[:, None]
 
@@ -192,7 +194,7 @@
             gram_matrix - jnp.diag(jnp.diag(gram_matrix)), rebuilt, precision=highest
         )
         code_ext = jnp.concatenate([before, latent_b], axis=1)
-        taps_part = lag_sums(code_ext, others, block_width, tap_count, skew)
+        taps_part = lag_sums(code_ext, others, block_width, tap_count)
         cross_part = jnp.dot(rebuilt, rebuilt.T, precision=highest)
         joined = butterfly_sum(jnp.concatenate([row_part, cross_part, taps_part.T], axis=0), "seg")
         stats_rows = joined[:chan_rows]

time: 769 us -> 716 us (0.931)
  local copies, waits for them, and re-layouts: 212 us -> 153 us
  matrix products: 238 us -> 258 us
  other arithmetic: 71.9 us -> 57.1 us
    unnamed x86, local copies, waits for them, and re-layouts: 96.5 us -> 36.5 us
    convert_element_type x2 -> x0, other arithmetic: 19.9 us -> none  [lag_sums(): piece = rest.astype(jnp.bfloat16)]
    dot_general x2, matrix products: 23.7 us -> 40.3 us  [lag_sums(): jnp.dot(stacked, band_sums_matrix(block_width, 2 * block_width), precisio...]
where the time goes in v4:
time: 716 us; the launch traced here: 705 us
  matrix products  258 us (36%)
  local copies, waits for them, and re-layouts  153 us (21%)
  waiting for transfers between devices  145 us (20%)
  starting transfers between devices  86.6 us (12%)
  other arithmetic  57.1 us (8%)
    ppermute x23, waiting for transfers between devices, butterfly_sum(): lax.ppermute(value, axis, [(i, i ^ distance) for i in range(count)])  128 us
    dot_general x66, matrix products, convolve_blocks(): jnp.einsum('kbm,kmi->kbi', window, matrix, preferred_element_type=jnp.flo...  84.4 us
    dot_general x60, matrix products, correlate_blocks(): jnp.einsum('kbi,kim->kbm', window, matrix, preferred_element_type=jnp.flo...  77 us
    while x280, local copies, waits for them, and re-layouts  77 us
    ppermute x14, starting transfers between devices, passed_along(): lax.ppermute(value, axis, [(source, source + steps) for source in range(l...  65.3 us
    dot_general x2, matrix products, lag_sums(): jnp.dot(stacked, band_sums_matrix(block_width, 2 * block_width), precisio...  40.3 us
    unnamed x86, local copies, waits for them, and re-layouts  36.5 us
    dot_general x20, matrix products, mix_atoms(): return jnp.dot(own_gram, rebuilt_part, precision=highest)  27.7 us
  transfers between devices with their start and end apart: 37, of which 29 were waited for; matrix products, arithmetic and copies ran while one was open for 9% of the time, Pallas kernels for 0%

profile of v4, /device:TPU:4, one launch (start us, length us, event | category | flops | bytes accessed | tf_op | source)
XLA Modules:
  0.0 704.7 jit_solution(16138346492060101356)
XLA Ops:
  7.2 7.3 %collective-permute-start.1 = (f32[64,1280]{1,0:T(8,128)}, f32[64,1280]{1,0:T(8,128)}, u32[]{:S(2)}, u32[]{:S(2)}) collective-permute-start(f32[64,1280]{1,0:T(8,128)} %get-tuple-element.680), channel_id=1, source_target_pairs={{8,0},{16,8},{24,16},{32,24},{40,32},{48,40},{56,48},{64,56},{72,6... | collective-permute-start | bytes 983048 | tf_op jit(solution)/shard_map/ppermute | solution.py:19
  16.8 2.7 slice_bitcast_fusion.9
  23.5 3.2 collective-permute-start.4
  33.1 6.5 collective-permute-done.5
  42.2 9.9 %collective-permute-done.6 = f32[64,2048]{1,0:T(8,128)S(1)} collective-permute-done((f32[64,2048]{1,0:T(8,128)S(1)}, f32[64,2048]{1,0:T(8,128)S(1)}, u32[]{:S(2)}, u32[]{:S(2)}) %collective-permute-start.6) | collective-permute-done | bytes 524320 | tf_op jit(solution)/shard_map/ppermute | solution.py:33
  52.2 4.7 collective-permute-start.7
  72.8 7.4 %collective-permute-start.9 = (f32[64,1280]{1,0:T(8,128)S(1)}, f32[64,1280]{1,0:T(8,128)S(1)}, u32[]{:S(2)}, u32[]{:S(2)}) collective-permute-start(f32[64,1280]{1,0:T(8,128)S(1)} %get-tuple-element.679), channel_id=1, source_target_pairs={{8,0},{16,8},{24,16},{32,24},{40,32},{48,40},{56,48},{64,56},{72,6... | collective-permute-start | bytes 983048 | tf_op jit(solution)/shard_map/ppermute | solution.py:19
  85.7 74.6 %while.58 = (s32[]{:T(128)}, f32[64,4608]{1,0:T(8,128)}, bf16[64,4608]{1,0:T(8,128)(2,1)S(1)}, f32[4608]{0:T(1024)S(1)}, f32[64,1]{0,1:T(1,128)S(1)}, /*index=5*...) while((s32[]{:T(128)}, f32[64,4608]{1,0:T(8,128)}, ...), condition=%wide.region_3.4_spmd.clone, body=%wide.region_2.3_spmd.clone.sunk | while | flops 684218880 | bytes 87890792 | solution.py:188
  86.2 2.4 fusion.360
  101.1 2.4 fusion.360
  108.2 2.4 fusion.363
  116.0 2.4 fusion.360
  130.9 2.4 fusion.360
  138.1 2.4 fusion.363
  145.9 2.4 fusion.360
  164.1 7.6 %collective-permute-start.11 = (f32[64,1280]{1,0:T(8,128)S(1)}, f32[64,1280]{1,0:T(8,128)}, u32[]{:S(2)}, u32[]{:S(2)}) collective-permute-start(f32[64,1280]{1,0:T(8,128)S(1)} %get-tuple-element.675), channel_id=1, source_target_pairs={{8,0},{16,8},{24,16},{32,24},{40,32},{48,40},{56,48},{64,56},{72,6... | collective-permute-start | bytes 983048 | tf_op jit(solution)/shard_map/ppermute | solution.py:19
  179.4 74.6 %while.59 = (s32[]{:T(128)}, f32[64,4608]{1,0:T(8,128)}, bf16[64,4608]{1,0:T(8,128)(2,1)S(1)}, f32[4608]{0:T(1024)S(1)}, f32[64,1]{0,1:T(1,128)S(1)}, /*index=5*...) while((s32[]{:T(128)}, f32[64,4608]{1,0:T(8,128)}, ...), condition=%wide.region_5.6_spmd.clone, body=%wide.region_4.5_spmd.clone.sunk | while | flops 684218880 | bytes 87890792 | solution.py:188
  179.9 2.4 fusion.379
  187.0 2.4 fusion.382
  194.8 2.4 fusion.379
  201.9 2.4 fusion.382
  209.7 2.4 fusion.379
  224.7 2.4 fusion.379
  231.8 2.4 fusion.382
  239.6 2.4 fusion.379
  260.4 3.9 collective-permute-done.14
  277.4 5.6 pad_maximum_fusion
  283.0 20.2 %fusion.106 = f32[192,256]{0,1:T(8,128)S(1)} fusion(f32[192,128,128]{2,1,0:T(8,128)} %pad_maximum_fusion), kind=kOutput, calls=%fused_computation.177 | convolution fusion | flops 4848615424 | bytes 12779520 | tf_op jit(solution)/shard_map/dot_general | solution.py:87
  309.2 11.8 %collective-permute-done.16 = f32[832,64]{1,0:T(8,128)S(1)} collective-permute-done((f32[832,64]{1,0:T(8,128)S(1)}, f32[832,64]{1,0:T(8,128)S(1)}, u32[]{:S(2)}, u32[]{:S(2)}) %collective-permute-start.16) | collective-permute-done | bytes 213024 | tf_op jit(solution)/shard_map/ppermute | solution.py:33
  321.2 12.5 %collective-permute-done.17 = f32[832,64]{1,0:T(8,128)S(1)} collective-permute-done((f32[832,64]{1,0:T(8,128)S(1)}, f32[832,64]{1,0:T(8,128)S(1)}, u32[]{:S(2)}, u32[]{:S(2)}) %collective-permute-start.17) | collective-permute-done | bytes 213024 | tf_op jit(solution)/shard_map/ppermute | solution.py:33
  338.9 7.3 %collective-permute-start.13 = (f32[64,1280]{1,0:T(8,128)}, f32[64,1280]{1,0:T(8,128)}, u32[]{:S(2)}, u32[]{:S(2)}) collective-permute-start(f32[64,1280]{1,0:T(8,128)} %get-tuple-element.673), channel_id=1, source_target_pairs={{8,0},{16,8},{24,16},{32,24},{40,32},{48,40},{56,48},{64,56},{72,6... | collective-permute-start | bytes 983048 | tf_op jit(solution)/shard_map/ppermute | solution.py:19
  358.9 4.4 collective-permute-done.21
  366.6 7.4 %collective-permute-done.22 = f32[64,2048]{1,0:T(8,128)S(1)} collective-permute-done((f32[64,2048]{1,0:T(8,128)S(1)}, f32[64,2048]{1,0:T(8,128)S(1)}, u32[]{:S(2)}, u32[]{:S(2)}) %collective-permute-start.22) | collective-permute-done | bytes 524320 | tf_op jit(solution)/shard_map/ppermute | solution.py:33
  378.1 10.0 %collective-permute-done.23 = f32[64,2048]{1,0:T(8,128)S(1)} collective-permute-done((f32[64,2048]{1,0:T(8,128)S(1)}, f32[64,2048]{1,0:T(8,128)S(1)}, u32[]{:S(2)}, u32[]{:S(2)}) %collective-permute-start.23) | collective-permute-done | bytes 524320 | tf_op jit(solution)/shard_map/ppermute | solution.py:33
  390.6 8.7 %collective-permute-done.24 = f32[64,2048]{1,0:T(8,128)S(1)} collective-permute-done((f32[64,2048]{1,0:T(8,128)S(1)}, f32[64,2048]{1,0:T(8,128)S(1)}, u32[]{:S(2)}, u32[]{:S(2)}) %collective-permute-start.24) | collective-permute-done | bytes 524320 | tf_op jit(solution)/shard_map/ppermute | solution.py:33
  401.4 12.3 %collective-permute-start.26 = (f32[64,1280]{1,0:T(8,128)S(1)}, f32[64,1280]{1,0:T(8,128)S(1)}, u32[]{:S(2)}, u32[]{:S(2)}) collective-permute-start(f32[64,1280]{1,0:T(8,128)S(1)} %get-tuple-element.677), channel_id=1, source_target_pairs={{8,0},{16,8},{24,16},{32,24},{40,32},{48,40},{56,48},{64,56},{72,6... | collective-permute-start | bytes 983048 | tf_op jit(solution)/shard_map/ppermute | solution.py:19
  427.1 74.6 %while.60 = (s32[]{:T(128)}, f32[64,4608]{1,0:T(8,128)}, bf16[64,4608]{1,0:T(8,128)(2,1)S(1)}, f32[4608]{0:T(1024)S(1)}, f32[64,1]{0,1:T(1,128)S(1)}, /*index=5*...) while((s32[]{:T(128)}, f32[64,4608]{1,0:T(8,128)}, ...), condition=%wide.region_11.12_spmd.clone, body=%wide.region_10.11_spmd.clone.sunk | while | flops 684218880 | bytes 87890792 | solution.py:188
  427.6 2.4 fusion.398
  434.7 2.4 fusion.401
  442.5 2.4 fusion.398
  449.6 2.4 fusion.401
  457.4 2.4 fusion.398
  464.5 2.4 fusion.401
  472.3 2.4 fusion.398
  487.3 2.4 fusion.398
  494.4 2.4 fusion.401
  505.5 7.4 %collective-permute-start.28 = (f32[64,1280]{1,0:T(8,128)S(1)}, f32[64,1280]{1,0:T(8,128)}, u32[]{:S(2)}, u32[]{:S(2)}) collective-permute-start(f32[64,1280]{1,0:T(8,128)S(1)} %get-tuple-element.671), channel_id=1, source_target_pairs={{8,0},{16,8},{24,16},{32,24},{40,32},{48,40},{56,48},{64,56},{72,6... | collective-permute-start | bytes 983048 | tf_op jit(solution)/shard_map/ppermute | solution.py:19
  520.7 74.6 %while.61 = (s32[]{:T(128)}, f32[64,4608]{1,0:T(8,128)}, bf16[64,4608]{1,0:T(8,128)(2,1)S(1)}, f32[4608]{0:T(1024)S(1)}, f32[64,1]{0,1:T(1,128)S(1)}, /*index=5*...) while((s32[]{:T(128)}, f32[64,4608]{1,0:T(8,128)}, ...), condition=%wide.region_13.14_spmd.clone, body=%wide.region_12.13_spmd.clone.sunk | while | flops 684218880 | bytes 87890792 | solution.py:188
  521.1 2.4 fusion.417
  536.0 2.4 fusion.417
  543.1 2.4 fusion.420
  550.9 2.4 fusion.417
  565.9 2.4 fusion.417
  573.0 2.4 fusion.420
  580.8 2.4 fusion.417
  600.1 6.2 collective-permute-done.29
  618.0 5.8 pad_maximum_fusion.1
  623.8 20.1 %fusion.111 = f32[192,256]{0,1:T(8,128)S(1)} fusion(f32[192,128,128]{2,1,0:T(8,128)} %pad_maximum_fusion.1), kind=kOutput, calls=%fused_computation.178 | convolution fusion | flops 4848615424 | bytes 12779520 | tf_op jit(solution)/shard_map/dot_general | solution.py:87
  651.4 11.8 %collective-permute-done.31 = f32[832,64]{1,0:T(8,128)S(1)} collective-permute-done((f32[832,64]{1,0:T(8,128)S(1)}, f32[832,64]{1,0:T(8,128)S(1)}, u32[]{:S(2)}, u32[]{:S(2)}) %collective-permute-start.31) | collective-permute-done | bytes 213024 | tf_op jit(solution)/shard_map/ppermute | solution.py:33
  663.4 12.5 %collective-permute-done.32 = f32[832,64]{1,0:T(8,128)S(1)} collective-permute-done((f32[832,64]{1,0:T(8,128)S(1)}, f32[832,64]{1,0:T(8,128)S(1)}, u32[]{:S(2)}, u32[]{:S(2)}) %collective-permute-start.32) | collective-permute-done | bytes 213024 | tf_op jit(solution)/shard_map/ppermute | solution.py:33
  676.1 11.6 %collective-permute-done.33 = f32[832,64]{1,0:T(8,128)S(1)} collective-permute-done((f32[832,64]{1,0:T(8,128)S(1)}, f32[832,64]{1,0:T(8,128)S(1)}, u32[]{:S(2)}, u32[]{:S(2)}) %collective-permute-start.33) | collective-permute-done | bytes 213024 | tf_op jit(solution)/shard_map/ppermute | solution.py:33
  690.4 3.2 collective-permute-done.34
  694.3 3.2 collective-permute-done.35
  698.7 4.3 collective-permute-done.36
  (775 shorter events, 385.7 us)
Async XLA Ops:
  0.6 29.1 %copy-start = (bf16[512,2048]{1,0:T(8,128)(2,1)S(1)}, bf16[512,2048]{1,0:T(8,128)(2,1)}, u32[]{:S(2)}) copy-start(bf16[512,2048]{1,0:T(8,128)(2,1)} %param.27) | copy-start | bytes 6291460
  0.6 13.9 %copy-start.52 = (f32[64,256]{1,0:T(8,128)S(1)}, f32[64,256]{1,0:T(8,128)}, u32[]{:S(2)}) copy-start(f32[64,256]{1,0:T(8,128)} %param.29) | copy-start | bytes 196612
  2.0 17.4 %collective-permute-start.2 = (f32[64,64]{1,0:T(8,128)S(1)}, f32[64,64]{1,0:T(8,128)S(1)}, u32[]{:S(2)}, u32[]{:S(2)}) collective-permute-start(f32[64,64]{1,0:T(8,128)S(1)} %fusion.217), channel_id=1, source_target_pairs={{0,1},{1,0},{2,3},{3,2},{4,5},{5,4},{6,7},{7,6},{8,9},{9,8},{10,11... | collective-permute-start | bytes 49160 | tf_op jit(solution)/shard_map/ppermute | solution.py:33
  5.3 63.3 %collective-permute-start = (f32[64,1280]{1,0:T(8,128)}, f32[64,1280]{1,0:T(8,128)}, u32[]{:S(2)}, u32[]{:S(2)}) collective-permute-start(f32[64,1280]{1,0:T(8,128)} %get-tuple-element.681), channel_id=1, source_target_pairs={{0,8},{8,16},{16,24},{24,32},{32,40},{40,48},{48,56},{56,64},{64,7... | collective-permute-start | bytes 983048 | tf_op jit(solution)/shard_map/ppermute | solution.py:19
  7.2 73.1 %collective-permute-start.1 = (f32[64,1280]{1,0:T(8,128)}, f32[64,1280]{1,0:T(8,128)}, u32[]{:S(2)}, u32[]{:S(2)}) collective-permute-start(f32[64,1280]{1,0:T(8,128)} %get-tuple-element.680), channel_id=1, source_target_pairs={{8,0},{16,8},{24,16},{32,24},{40,32},{48,40},{56,48},{64,56},{72,6... | collective-permute-start | bytes 983048 | tf_op jit(solution)/shard_map/ppermute | solution.py:19
  14.5 16.7 %copy-start.56 = (s32[16384]{0:T(1024)}, s32[16384]{0:T(1024)S(1)}, u32[]{:S(2)}) copy-start(s32[16384]{0:T(1024)S(1)} %add_bitcast_fusion) | copy-start | bytes 196612
  16.7 4.4 copy-start.58
  16.7 13.0 %copy-start.45 = (f32[512,64]{0,1:T(8,128)S(1)}, f32[512,64]{0,1:T(8,128)}, u32[]{:S(2)}) copy-start(f32[512,64]{0,1:T(8,128)} %param.28) | copy-start | bytes 393220
  19.5 4.0 collective-permute-start.3
  23.5 5.4 collective-permute-start.4
  30.3 9.3 %collective-permute-start.5 = (f32[64,2048]{1,0:T(8,128)S(1)}, f32[64,2048]{1,0:T(8,128)S(1)}, u32[]{:S(2)}, u32[]{:S(2)}) collective-permute-start(f32[64,2048]{1,0:T(8,128)S(1)} %fusion.153), channel_id=1, source_target_pairs={{0,1},{1,0},{2,3},{3,2},{4,5},{5,4},{6,7},{7,6},{8,9},{9,8},{10,11... | collective-permute-start | bytes 1572872 | tf_op jit(solution)/shard_map/ppermute | solution.py:33
  39.6 12.5 %collective-permute-start.6 = (f32[64,2048]{1,0:T(8,128)S(1)}, f32[64,2048]{1,0:T(8,128)S(1)}, u32[]{:S(2)}, u32[]{:S(2)}) collective-permute-start(f32[64,2048]{1,0:T(8,128)S(1)} %add.356), channel_id=1, source_target_pairs={{0,2},{1,3},{2,0},{3,1},{4,6},{5,7},{6,4},{7,5},{8,10},{9,11},{10,... | collective-permute-start | bytes 1572872 | tf_op jit(solution)/shard_map/ppermute | solution.py:33
  41.5 15.4 %copy-start.40 = (bf16[8,8,128,128]{3,1,2,0:T(8,128)(2,1)S(1)}, bf16[8,8,128,128]{3,1,2,0:T(8,128)(2,1)}, u32[]{:S(2)}) copy-start(bf16[8,8,128,128]{3,1,2,0:T(8,128)(2,1)} %get-tuple-element.669) | copy-start | bytes 6291460
  42.1 14.7 %copy-start.53 = (f32[64]{0:T(128)S(1)}, f32[64]{0:T(128)}, u32[]{:S(2)}) copy-start(f32[64]{0:T(128)} %param.32) | copy-start | bytes 772
  42.1 14.7 %copy-start.59 = (f32[64]{0:T(128)S(1)}, f32[64]{0:T(128)}, u32[]{:S(2)}) copy-start(f32[64]{0:T(128)} %param.31) | copy-start | bytes 772
  52.2 17.5 %collective-permute-start.7 = (f32[64,2048]{1,0:T(8,128)S(1)}, f32[64,2048]{1,0:T(8,128)}, u32[]{:S(2)}, u32[]{:S(2)}) collective-permute-start(f32[64,2048]{1,0:T(8,128)S(1)} %add.357), channel_id=1, source_target_pairs={{0,4},{1,5},{2,6},{3,7},{4,0},{5,1},{6,2},{7,3},{8,12},{9,13},{10,... | collective-permute-start | bytes 1572872 | tf_op jit(solution)/shard_map/ppermute | solution.py:33
  69.6 10.6 %copy-start.44 = (f32[64,2048]{1,0:T(8,128)S(1)}, f32[64,2048]{1,0:T(8,128)}, u32[]{:S(2)}) copy-start(f32[64,2048]{1,0:T(8,128)} %param.30) | copy-start | bytes 1572868
  70.8 13.8 %copy-start.36 = (f32[64,2048]{1,0:T(8,128)}, f32[64,2048]{1,0:T(8,128)S(1)}, u32[]{:S(2)}) copy-start(f32[64,2048]{1,0:T(8,128)S(1)} %add.358) | copy-start | bytes 1572868
  70.9 12.0 %collective-permute-start.8 = (f32[64,1280]{1,0:T(8,128)S(1)}, f32[64,1280]{1,0:T(8,128)S(1)}, u32[]{:S(2)}, u32[]{:S(2)}) collective-permute-start(f32[64,1280]{1,0:T(8,128)S(1)} %get-tuple-element.678), channel_id=1, source_target_pairs={{0,8},{8,16},{16,24},{24,32},{32,40},{40,48},{48,56},{56,64},{64,7... | collective-permute-start | bytes 983048 | tf_op jit(solution)/shard_map/ppermute | solution.py:19
  72.8 11.8 %collective-permute-start.9 = (f32[64,1280]{1,0:T(8,128)S(1)}, f32[64,1280]{1,0:T(8,128)S(1)}, u32[]{:S(2)}, u32[]{:S(2)}) collective-permute-start(f32[64,1280]{1,0:T(8,128)S(1)} %get-tuple-element.679), channel_id=1, source_target_pairs={{8,0},{16,8},{24,16},{32,24},{40,32},{48,40},{56,48},{64,56},{72,6... | collective-permute-start | bytes 983048 | tf_op jit(solution)/shard_map/ppermute | solution.py:19
  86.2 2.4 copy-start.6
  116.0 2.4 copy-start.6
  145.9 2.4 copy-start.6
  162.2 12.4 %collective-permute-start.10 = (f32[64,1280]{1,0:T(8,128)}, f32[64,1280]{1,0:T(8,128)S(1)}, u32[]{:S(2)}, u32[]{:S(2)}) collective-permute-start(f32[64,1280]{1,0:T(8,128)} %get-tuple-element.674), channel_id=1, source_target_pairs={{0,8},{8,16},{16,24},{24,32},{32,40},{40,48},{48,56},{56,64},{64,7... | collective-permute-start | bytes 983048 | tf_op jit(solution)/shard_map/ppermute | solution.py:19
  164.1 12.0 %collective-permute-start.11 = (f32[64,1280]{1,0:T(8,128)S(1)}, f32[64,1280]{1,0:T(8,128)}, u32[]{:S(2)}, u32[]{:S(2)}) collective-permute-start(f32[64,1280]{1,0:T(8,128)S(1)} %get-tuple-element.675), channel_id=1, source_target_pairs={{8,0},{16,8},{24,16},{32,24},{40,32},{48,40},{56,48},{64,56},{72,6... | collective-permute-start | bytes 983048 | tf_op jit(solution)/shard_map/ppermute | solution.py:19
  179.9 2.4 copy-start.7
  209.7 2.4 copy-start.7
  239.6 2.4 copy-start.7
  255.2 9.1 %collective-permute-start.14 = (bf16[64,256]{1,0:T(8,128)(2,1)S(1)}, bf16[64,256]{1,0:T(8,128)(2,1)S(1)}, u32[]{:S(2)}, u32[]{:S(2)}) collective-permute-start(bf16[64,256]{1,0:T(8,128)(2,1)S(1)} %slice.520), channel_id=1, source_target_pairs={{0,8},{8,16},{16,24},{24,32},{32,40},{40,48},{48,56},{56,64},{64,7... | collective-permute-start | bytes 98312 | tf_op jit(solution)/shard_map/ppermute | solution.py:19
  307.2 1.8 collective-permute-start.15
  309.1 11.9 %collective-permute-start.16 = (f32[832,64]{1,0:T(8,128)S(1)}, f32[832,64]{1,0:T(8,128)S(1)}, u32[]{:S(2)}, u32[]{:S(2)}) collective-permute-start(f32[832,64]{1,0:T(8,128)S(1)} %fusion.202), channel_id=1, source_target_pairs={{0,16},{8,24},{16,0},{24,8},{32,48},{40,56},{48,32},{56,40},{64,80... | collective-permute-start | bytes 638984 | tf_op jit(solution)/shard_map/ppermute | solution.py:33
  321.1 12.6 %collective-permute-start.17 = (f32[832,64]{1,0:T(8,128)S(1)}, f32[832,64]{1,0:T(8,128)S(1)}, u32[]{:S(2)}, u32[]{:S(2)}) collective-permute-start(f32[832,64]{1,0:T(8,128)S(1)} %add.367), channel_id=1, source_target_pairs={{0,32},{8,40},{16,48},{24,56},{32,0},{40,8},{48,16},{56,24},{64,96... | collective-permute-start | bytes 638984 | tf_op jit(solution)/shard_map/ppermute | solution.py:33
  333.8 12.4 %collective-permute-start.18 = (f32[832,64]{1,0:T(8,128)S(1)}, f32[832,64]{1,0:T(8,128)S(1)}, u32[]{:S(2)}, u32[]{:S(2)}) collective-permute-start(f32[832,64]{1,0:T(8,128)S(1)} %add.368), channel_id=1, source_target_pairs={{0,64},{8,72},{16,80},{24,88},{32,96},{40,104},{48,112},{56,120},{... | collective-permute-start | bytes 638984 | tf_op jit(solution)/shard_map/ppermute | solution.py:33
  335.8 12.0 %copy-start.46 = (f32[512,64]{0,1:T(8,128)S(1)}, f32[512,64]{0,1:T(8,128)}, u32[]{:S(2)}) copy-start(f32[512,64]{0,1:T(8,128)} %param.28) | copy-start | bytes 393220
  336.9 14.4 %copy-start.43 = (f32[64,2048]{1,0:T(8,128)}, f32[64,2048]{1,0:T(8,128)S(1)}, u32[]{:S(2)}) copy-start(f32[64,2048]{1,0:T(8,128)S(1)} %slice.407) | copy-start | bytes 1572868
  336.9 14.0 %collective-permute-start.12 = (f32[64,1280]{1,0:T(8,128)}, f32[64,1280]{1,0:T(8,128)}, u32[]{:S(2)}, u32[]{:S(2)}) collective-permute-start(f32[64,1280]{1,0:T(8,128)} %get-tuple-element.672), channel_id=1, source_target_pairs={{0,8},{8,16},{16,24},{24,32},{32,40},{40,48},{48,56},{56,64},{64,7... | collective-permute-start | bytes 983048 | tf_op jit(solution)/shard_map/ppermute | solution.py:19
  338.9 12.5 %collective-permute-start.13 = (f32[64,1280]{1,0:T(8,128)}, f32[64,1280]{1,0:T(8,128)}, u32[]{:S(2)}, u32[]{:S(2)}) collective-permute-start(f32[64,1280]{1,0:T(8,128)} %get-tuple-element.673), channel_id=1, source_target_pairs={{8,0},{16,8},{24,16},{32,24},{40,32},{48,40},{56,48},{64,56},{72,6... | collective-permute-start | bytes 983048 | tf_op jit(solution)/shard_map/ppermute | solution.py:19
  349.4 14.8 %copy-start.41 = (f32[512,64]{1,0:T(8,128)}, f32[512,64]{1,0:T(8,128)S(1)}, u32[]{:S(2)}) copy-start(f32[512,64]{1,0:T(8,128)S(1)} %slice_subtract_fusion.1) | copy-start | bytes 393220
  350.0 4.0 collective-permute-start.19
  354.0 3.9 collective-permute-start.20
  357.9 5.4 collective-permute-start.21
  364.7 10.8 %copy-start.57 = (s32[16384]{0:T(1024)S(1)}, s32[16384]{0:T(1024)}, u32[]{:S(2)}) copy-start(s32[16384]{0:T(1024)} %copy-done.56) | copy-start | bytes 196612
  364.7 9.3 %collective-permute-start.22 = (f32[64,2048]{1,0:T(8,128)S(1)}, f32[64,2048]{1,0:T(8,128)S(1)}, u32[]{:S(2)}, u32[]{:S(2)}) collective-permute-start(f32[64,2048]{1,0:T(8,128)S(1)} %fusion.146), channel_id=1, source_target_pairs={{0,1},{1,0},{2,3},{3,2},{4,5},{5,4},{6,7},{7,6},{8,9},{9,8},{10,11... | collective-permute-start | bytes 1572872 | tf_op jit(solution)/shard_map/ppermute | solution.py:33
  374.1 14.0 %collective-permute-start.23 = (f32[64,2048]{1,0:T(8,128)S(1)}, f32[64,2048]{1,0:T(8,128)S(1)}, u32[]{:S(2)}, u32[]{:S(2)}) collective-permute-start(f32[64,2048]{1,0:T(8,128)S(1)} %add.375), channel_id=1, source_target_pairs={{0,2},{1,3},{2,0},{3,1},{4,6},{5,7},{6,4},{7,5},{8,10},{9,11},{10,... | collective-permute-start | bytes 1572872 | tf_op jit(solution)/shard_map/ppermute | solution.py:33
  378.1 10.6 %copy-start.55 = (s32[16384]{0:T(1024)S(1)}, s32[16384]{0:T(1024)}, u32[]{:S(2)}) copy-start(s32[16384]{0:T(1024)} %copy-done.54) | copy-start | bytes 196612
  388.1 11.2 %collective-permute-start.24 = (f32[64,2048]{1,0:T(8,128)S(1)}, f32[64,2048]{1,0:T(8,128)S(1)}, u32[]{:S(2)}, u32[]{:S(2)}) collective-permute-start(f32[64,2048]{1,0:T(8,128)S(1)} %add.376), channel_id=1, source_target_pairs={{0,4},{1,5},{2,6},{3,7},{4,0},{5,1},{6,2},{7,3},{8,12},{9,13},{10,... | collective-permute-start | bytes 1572872 | tf_op jit(solution)/shard_map/ppermute | solution.py:33
  399.4 26.7 %copy-start.34 = (f32[64,2048]{1,0:T(8,128)}, f32[64,2048]{1,0:T(8,128)S(1)}, u32[]{:S(2)}) copy-start(f32[64,2048]{1,0:T(8,128)S(1)} %add.377) | copy-start | bytes 1572868
  399.4 26.6 %collective-permute-start.25 = (f32[64,1280]{1,0:T(8,128)S(1)}, f32[64,1280]{1,0:T(8,128)S(1)}, u32[]{:S(2)}, u32[]{:S(2)}) collective-permute-start(f32[64,1280]{1,0:T(8,128)S(1)} %get-tuple-element.676), channel_id=1, source_target_pairs={{0,8},{8,16},{16,24},{24,32},{32,40},{40,48},{48,56},{56,64},{64,7... | collective-permute-start | bytes 983048 | tf_op jit(solution)/shard_map/ppermute | solution.py:19
  401.4 24.7 %collective-permute-start.26 = (f32[64,1280]{1,0:T(8,128)S(1)}, f32[64,1280]{1,0:T(8,128)S(1)}, u32[]{:S(2)}, u32[]{:S(2)}) collective-permute-start(f32[64,1280]{1,0:T(8,128)S(1)} %get-tuple-element.677), channel_id=1, source_target_pairs={{8,0},{16,8},{24,16},{32,24},{40,32},{48,40},{56,48},{64,56},{72,6... | collective-permute-start | bytes 983048 | tf_op jit(solution)/shard_map/ppermute | solution.py:19
  442.5 2.4 copy-start.11
  472.3 2.4 copy-start.11
  503.6 12.2 %collective-permute-start.27 = (f32[64,1280]{1,0:T(8,128)}, f32[64,1280]{1,0:T(8,128)S(1)}, u32[]{:S(2)}, u32[]{:S(2)}) collective-permute-start(f32[64,1280]{1,0:T(8,128)} %get-tuple-element.670), channel_id=1, source_target_pairs={{0,8},{8,16},{16,24},{24,32},{32,40},{40,48},{48,56},{56,64},{64,7... | collective-permute-start | bytes 983048 | tf_op jit(solution)/shard_map/ppermute | solution.py:19
  505.5 11.8 %collective-permute-start.28 = (f32[64,1280]{1,0:T(8,128)S(1)}, f32[64,1280]{1,0:T(8,128)}, u32[]{:S(2)}, u32[]{:S(2)}) collective-permute-start(f32[64,1280]{1,0:T(8,128)S(1)} %get-tuple-element.671), channel_id=1, source_target_pairs={{8,0},{16,8},{24,16},{32,24},{40,32},{48,40},{56,48},{64,56},{72,6... | collective-permute-start | bytes 983048 | tf_op jit(solution)/shard_map/ppermute | solution.py:19
  521.1 2.4 copy-start.12
  550.9 2.4 copy-start.12
  597.2 9.1 %collective-permute-start.29 = (bf16[64,256]{1,0:T(8,128)(2,1)S(1)}, bf16[64,256]{1,0:T(8,128)(2,1)S(1)}, u32[]{:S(2)}, u32[]{:S(2)}) collective-permute-start(bf16[64,256]{1,0:T(8,128)(2,1)S(1)} %slice.540), channel_id=1, source_target_pairs={{0,8},{8,16},{16,24},{24,32},{32,40},{40,48},{48,56},{56,64},{64,7... | collective-permute-start | bytes 98312 | tf_op jit(solution)/shard_map/ppermute | solution.py:19
  649.4 1.8 collective-permute-start.30
  651.3 11.9 %collective-permute-start.31 = (f32[832,64]{1,0:T(8,128)S(1)}, f32[832,64]{1,0:T(8,128)S(1)}, u32[]{:S(2)}, u32[]{:S(2)}) collective-permute-start(f32[832,64]{1,0:T(8,128)S(1)} %fusion.201), channel_id=1, source_target_pairs={{0,16},{8,24},{16,0},{24,8},{32,48},{40,56},{48,32},{56,40},{64,80... | collective-permute-start | bytes 638984 | tf_op jit(solution)/shard_map/ppermute | solution.py:33
  663.3 25.2 %copy-start.42 = (f32[512,64]{1,0:T(8,128)S(1)}, f32[512,64]{1,0:T(8,128)}, u32[]{:S(2)}) copy-start(f32[512,64]{1,0:T(8,128)} %copy-done.41) | copy-start | bytes 393220
  663.3 12.6 %collective-permute-start.32 = (f32[832,64]{1,0:T(8,128)S(1)}, f32[832,64]{1,0:T(8,128)S(1)}, u32[]{:S(2)}, u32[]{:S(2)}) collective-permute-start(f32[832,64]{1,0:T(8,128)S(1)} %add.383), channel_id=1, source_target_pairs={{0,32},{8,40},{16,48},{24,56},{32,0},{40,8},{48,16},{56,24},{64,96... | collective-permute-start | bytes 638984 | tf_op jit(solution)/shard_map/ppermute | solution.py:33
  676.0 11.7 %collective-permute-start.33 = (f32[832,64]{1,0:T(8,128)S(1)}, f32[832,64]{1,0:T(8,128)S(1)}, u32[]{:S(2)}, u32[]{:S(2)}) collective-permute-start(f32[832,64]{1,0:T(8,128)S(1)} %add.384), channel_id=1, source_target_pairs={{0,64},{8,72},{16,80},{24,88},{32,96},{40,104},{48,112},{56,120},{... | collective-permute-start | bytes 638984 | tf_op jit(solution)/shard_map/ppermute | solution.py:33
  689.6 4.0 collective-permute-start.34
  693.6 3.9 collective-permute-start.35
  697.5 5.4 collective-permute-start.36
  (145 other events, 230.4 us)

commit v5 on v4

--- a/solution.py
+++ b/solution.py
@@ -51,7 +51,7 @@
     i = lax.broadcasted_iota(jnp.int32, shape, 1)
     d = lax.broadcasted_iota(jnp.int32, shape, 2)
     hit = d == i - m + (block_width - 1)
-    return jnp.where(hit, 1.0, 0.0).reshape(block_width * block_width, tap_span)
+    return jnp.where(hit, 1.0, 0.0).astype(jnp.bfloat16).reshape(block_width * block_width, tap_span)
 
 
 def toeplitz(kernel_taps, block_width, skew):
@@ -69,7 +69,7 @@
     return [flat[off] for off in range(lag_blocks + 1)]
 
 
-def lag_sums(code_ext, others, block_width, tap_count):
+def lag_sums(code_ext, others, block_width, tap_count, band_sums):
     atoms_here, seg_len = others.shape
     block_count = seg_len // block_width
     lag_blocks = tap_count // block_width
@@ -84,7 +84,7 @@
             )
         )
     stacked = jnp.concatenate(grads, axis=0).reshape((lag_blocks + 1) * atoms_here, block_width * block_width)
-    bands = jnp.dot(stacked, band_sums_matrix(block_width, 2 * block_width), precision=lax.Precision.HIGH)
+    bands = jnp.dot(stacked, band_sums.astype(jnp.float32), precision=lax.Precision.HIGH)
     bands = bands.reshape(lag_blocks + 1, atoms_here, 2 * block_width)
     total = jnp.zeros((atoms_here, tap_count + 3 * block_width), jnp.float32)
     for offset in range(lag_blocks + 1):
@@ -136,6 +136,7 @@
     block_width = 128
     skew = one_hot_skew(block_width, 2 * block_width)
     skew_flipped = one_hot_skew(block_width, 2 * block_width, transposed=True)
+    band_sums = lax.optimization_barrier(band_sums_matrix(block_width, 2 * block_width))
     ghost = GHOST_BLOCKS * block_width
     wide_positions = lax.axis_index("seg") * seg_len - ghost + lax.iota(jnp.int32, seg_len + 2 * ghost)
     wide_crosses = (wide_positions[None, :] < breaks[:, None]) & (
@@ -194,7 +195,7 @@
             gram_matrix - jnp.diag(jnp.diag(gram_matrix)), rebuilt, precision=highest
         )
         code_ext = jnp.concatenate([before, latent_b], axis=1)
-        taps_part = lag_sums(code_ext, others, block_width, tap_count)
+        taps_part = lag_sums(code_ext, others, block_width, tap_count, band_sums)
         cross_part = jnp.dot(rebuilt, rebuilt.T, precision=highest)
         joined = butterfly_sum(jnp.concatenate([row_part, cross_part, taps_part.T], axis=0), "seg")
         stats_rows = joined[:chan_rows]

time: 716 us -> 733 us (1.024)
  matrix products: 258 us -> 267 us
  other arithmetic: 57.1 us -> 65.6 us
  waiting for transfers between devices: 145 us -> 137 us
    dot_general x2, matrix products: 40.3 us -> 49.7 us  [lag_sums(): jnp.dot(stacked, band_sums.astype(jnp.float32), precision=lax.Precision.H...]
    convert_element_type x0 -> x1, other arithmetic: none -> 8.89 us  [band_sums_matrix(): jnp.where(hit, 1.0, 0.0).astype(jnp.bfloat16)]
    unnamed x86 -> x90, local copies, waits for them, and re-layouts: 36.5 us -> 40.4 us
  transfers between devices with their start and end apart: 37 -> 37, of which waited for: 29 -> 27; matrix products, arithmetic and copies ran while one was open for 9% -> 10% of each run, Pallas kernels for 0% -> 0%
where the time goes in v5:
time: 733 us; the launch traced here: 722 us
  matrix products  267 us (36%)
  local copies, waits for them, and re-layouts  157 us (21%)
  waiting for transfers between devices  137 us (19%)
  starting transfers between devices  90.3 us (12%)
  other arithmetic  65.6 us (9%)
    ppermute x23, waiting for transfers between devices, butterfly_sum(): lax.ppermute(value, axis, [(i, i ^ distance) for i in range(count)])  124 us
    dot_general x66, matrix products, convolve_blocks(): jnp.einsum('kbm,kmi->kbi', window, matrix, preferred_element_type=jnp.flo...  84.4 us
    dot_general x60, matrix products, correlate_blocks(): jnp.einsum('kbi,kim->kbm', window, matrix, preferred_element_type=jnp.flo...  77 us
    while x280, local copies, waits for them, and re-layouts  77 us
    ppermute x14, starting transfers between devices, passed_along(): lax.ppermute(value, axis, [(source, source + steps) for source in range(l...  64.6 us
    dot_general x2, matrix products, lag_sums(): jnp.dot(stacked, band_sums.astype(jnp.float32), precision=lax.Precision.H...  49.7 us
    unnamed x90, local copies, waits for them, and re-layouts  40.4 us
    dot_general x20, matrix products, mix_atoms(): return jnp.dot(own_gram, rebuilt_part, precision=highest)  27.6 us
  transfers between devices with their start and end apart: 37, of which 27 were waited for; matrix products, arithmetic and copies ran while one was open for 10% of the time, Pallas kernels for 0%

profile of v5, /device:TPU:4, one launch (start us, length us, event | category | flops | bytes accessed | tf_op | source)
XLA Modules:
  0.0 722.1 jit_solution(17316880196703946589)
XLA Ops:
  5.3 5.3 collective-permute-start.1
  14.8 2.7 slice_bitcast_fusion.6
  21.6 3.2 collective-permute-start.4
  31.4 7.1 collective-permute-done.5
  40.3 2.9 slice_bitcast_fusion.9
  43.3 5.8 collective-permute-done.6
  49.2 4.9 collective-permute-start.7
  54.1 3.6 copy.87
  71.7 9.3 %collective-permute-start.9 = (f32[64,1280]{1,0:T(8,128)S(1)}, f32[64,1280]{1,0:T(8,128)S(1)}, u32[]{:S(2)}, u32[]{:S(2)}) collective-permute-start(f32[64,1280]{1,0:T(8,128)S(1)} %get-tuple-element.679), channel_id=1, source_target_pairs={{8,0},{16,8},{24,16},{32,24},{40,32},{48,40},{56,48},{64,56},{72,6... | collective-permute-start | bytes 983048 | tf_op jit(solution)/shard_map/ppermute | solution.py:19
  86.4 74.6 %while.58 = (s32[]{:T(128)}, f32[64,4608]{1,0:T(8,128)}, bf16[64,4608]{1,0:T(8,128)(2,1)S(1)}, f32[4608]{0:T(1024)S(1)}, f32[64,1]{0,1:T(1,128)S(1)}, /*index=5*...) while((s32[]{:T(128)}, f32[64,4608]{1,0:T(8,128)}, ...), condition=%wide.region_3.4_spmd.clone, body=%wide.region_2.3_spmd.clone.sunk | while | flops 684218880 | bytes 87890792 | solution.py:189
  86.8 2.4 fusion.340
  94.0 2.4 fusion.343
  101.8 2.4 fusion.340
  108.9 2.4 fusion.343
  116.7 2.4 fusion.340
  131.6 2.4 fusion.340
  146.5 2.4 fusion.340
  164.8 7.7 %collective-permute-start.11 = (f32[64,1280]{1,0:T(8,128)S(1)}, f32[64,1280]{1,0:T(8,128)}, u32[]{:S(2)}, u32[]{:S(2)}) collective-permute-start(f32[64,1280]{1,0:T(8,128)S(1)} %get-tuple-element.675), channel_id=1, source_target_pairs={{8,0},{16,8},{24,16},{32,24},{40,32},{48,40},{56,48},{64,56},{72,6... | collective-permute-start | bytes 983048 | tf_op jit(solution)/shard_map/ppermute | solution.py:19
  180.1 74.6 %while.59 = (s32[]{:T(128)}, f32[64,4608]{1,0:T(8,128)}, bf16[64,4608]{1,0:T(8,128)(2,1)S(1)}, f32[4608]{0:T(1024)S(1)}, f32[64,1]{0,1:T(1,128)S(1)}, /*index=5*...) while((s32[]{:T(128)}, f32[64,4608]{1,0:T(8,128)}, ...), condition=%wide.region_5.6_spmd.clone, body=%wide.region_4.5_spmd.clone.sunk | while | flops 684218880 | bytes 87890792 | solution.py:189
  180.5 2.4 fusion.359
  195.4 2.4 fusion.359
  210.4 2.4 fusion.359
  225.3 2.4 fusion.359
  240.2 2.4 fusion.359
  258.2 8.9 %select_convert_fusion = bf16[16384,256]{1,0:T(8,128)(2,1)} fusion(s32[16384]{0:T(1024)S(1)} %add_bitcast_fusion.1), kind=kLoop, calls=%fused_computation.119 | loop fusion | flops 12582912 | bytes 8454144 | tf_op jit(solution)/shard_map/convert_element_type | solution.py:54
  283.0 5.4 pad_maximum_fusion
  288.4 24.9 %fusion.83 = f32[192,256]{0,1:T(8,128)S(1)} fusion(bf16[16384,256]{1,0:T(8,128)(2,1)} %select_convert_fusion, f32[24,8,128,128]{3,2,1,0:T(8,128)} %bitcast.352), kind=kOutput, calls=%fused_computation.128 | convolution fusion | flops 4831838208 | bytes 21168128 | tf_op jit(solution)/shard_map/dot_general | solution.py:87
  319.4 11.8 %collective-permute-done.16 = f32[832,64]{1,0:T(8,128)S(1)} collective-permute-done((f32[832,64]{1,0:T(8,128)S(1)}, f32[832,64]{1,0:T(8,128)S(1)}, u32[]{:S(2)}, u32[]{:S(2)}) %collective-permute-start.16) | collective-permute-done | bytes 213024 | tf_op jit(solution)/shard_map/ppermute | solution.py:33
  331.4 12.5 %collective-permute-done.17 = f32[832,64]{1,0:T(8,128)S(1)} collective-permute-done((f32[832,64]{1,0:T(8,128)S(1)}, f32[832,64]{1,0:T(8,128)S(1)}, u32[]{:S(2)}, u32[]{:S(2)}) %collective-permute-start.17) | collective-permute-done | bytes 213024 | tf_op jit(solution)/shard_map/ppermute | solution.py:33
  344.0 3.4 collective-permute-start.18
  352.4 7.5 %collective-permute-start.13 = (f32[64,1280]{1,0:T(8,128)}, f32[64,1280]{1,0:T(8,128)}, u32[]{:S(2)}, u32[]{:S(2)}) collective-permute-start(f32[64,1280]{1,0:T(8,128)} %get-tuple-element.673), channel_id=1, source_target_pairs={{8,0},{16,8},{24,16},{32,24},{40,32},{48,40},{56,48},{64,56},{72,6... | collective-permute-start | bytes 983048 | tf_op jit(solution)/shard_map/ppermute | solution.py:19
  373.2 4.0 collective-permute-done.21
  380.7 7.1 collective-permute-done.22
  391.2 10.8 %collective-permute-done.23 = f32[64,2048]{1,0:T(8,128)S(1)} collective-permute-done((f32[64,2048]{1,0:T(8,128)S(1)}, f32[64,2048]{1,0:T(8,128)S(1)}, u32[]{:S(2)}, u32[]{:S(2)}) %collective-permute-start.23) | collective-permute-done | bytes 524320 | tf_op jit(solution)/shard_map/ppermute | solution.py:33
  404.1 8.7 %collective-permute-done.24 = f32[64,2048]{1,0:T(8,128)S(1)} collective-permute-done((f32[64,2048]{1,0:T(8,128)S(1)}, f32[64,2048]{1,0:T(8,128)S(1)}, u32[]{:S(2)}, u32[]{:S(2)}) %collective-permute-start.24) | collective-permute-done | bytes 524320 | tf_op jit(solution)/shard_map/ppermute | solution.py:33
  414.9 11.4 %collective-permute-start.26 = (f32[64,1280]{1,0:T(8,128)S(1)}, f32[64,1280]{1,0:T(8,128)S(1)}, u32[]{:S(2)}, u32[]{:S(2)}) collective-permute-start(f32[64,1280]{1,0:T(8,128)S(1)} %get-tuple-element.677), channel_id=1, source_target_pairs={{8,0},{16,8},{24,16},{32,24},{40,32},{48,40},{56,48},{64,56},{72,6... | collective-permute-start | bytes 983048 | tf_op jit(solution)/shard_map/ppermute | solution.py:19
  439.7 74.5 %while.60 = (s32[]{:T(128)}, f32[64,4608]{1,0:T(8,128)}, bf16[64,4608]{1,0:T(8,128)(2,1)S(1)}, f32[4608]{0:T(1024)S(1)}, f32[64,1]{0,1:T(1,128)S(1)}, /*index=5*...) while((s32[]{:T(128)}, f32[64,4608]{1,0:T(8,128)}, ...), condition=%wide.region_11.12_spmd.clone, body=%wide.region_10.11_spmd.clone.sunk | while | flops 684218880 | bytes 87890792 | solution.py:189
  440.2 2.4 fusion.378
  447.3 2.4 fusion.381
  455.1 2.4 fusion.378
  470.0 2.4 fusion.378
  477.1 2.4 fusion.381
  484.9 2.4 fusion.378
  492.0 2.4 fusion.381
  499.8 2.4 fusion.378
  518.0 7.4 %collective-permute-start.28 = (f32[64,1280]{1,0:T(8,128)S(1)}, f32[64,1280]{1,0:T(8,128)}, u32[]{:S(2)}, u32[]{:S(2)}) collective-permute-start(f32[64,1280]{1,0:T(8,128)S(1)} %get-tuple-element.671), channel_id=1, source_target_pairs={{8,0},{16,8},{24,16},{32,24},{40,32},{48,40},{56,48},{64,56},{72,6... | collective-permute-start | bytes 983048 | tf_op jit(solution)/shard_map/ppermute | solution.py:19
  533.1 74.5 %while.61 = (s32[]{:T(128)}, f32[64,4608]{1,0:T(8,128)}, bf16[64,4608]{1,0:T(8,128)(2,1)S(1)}, f32[4608]{0:T(1024)S(1)}, f32[64,1]{0,1:T(1,128)S(1)}, /*index=5*...) while((s32[]{:T(128)}, f32[64,4608]{1,0:T(8,128)}, ...), condition=%wide.region_13.14_spmd.clone, body=%wide.region_12.13_spmd.clone.sunk | while | flops 684218880 | bytes 87890792 | solution.py:189
  533.5 2.4 fusion.397
  548.4 2.4 fusion.397
  555.6 2.4 fusion.400
  563.3 2.4 fusion.397
  578.2 2.4 fusion.397
  585.4 2.4 fusion.400
  593.1 2.4 fusion.397
  600.3 2.4 fusion.400
  612.4 6.2 collective-permute-done.29
  631.7 5.7 pad_maximum_fusion.1
  637.4 24.8 %fusion.80 = f32[192,256]{0,1:T(8,128)S(1)} fusion(bf16[16384,256]{1,0:T(8,128)(2,1)} %select_convert_fusion, f32[24,8,128,128]{3,2,1,0:T(8,128)} %bitcast.351), kind=kOutput, calls=%fused_computation.125 | convolution fusion | flops 4831838208 | bytes 21168128 | tf_op jit(solution)/shard_map/dot_general | solution.py:87
  668.2 11.8 %collective-permute-done.31 = f32[832,64]{1,0:T(8,128)S(1)} collective-permute-done((f32[832,64]{1,0:T(8,128)S(1)}, f32[832,64]{1,0:T(8,128)S(1)}, u32[]{:S(2)}, u32[]{:S(2)}) %collective-permute-start.31) | collective-permute-done | bytes 213024 | tf_op jit(solution)/shard_map/ppermute | solution.py:33
  680.2 12.5 %collective-permute-done.32 = f32[832,64]{1,0:T(8,128)S(1)} collective-permute-done((f32[832,64]{1,0:T(8,128)S(1)}, f32[832,64]{1,0:T(8,128)S(1)}, u32[]{:S(2)}, u32[]{:S(2)}) %collective-permute-start.32) | collective-permute-done | bytes 213024 | tf_op jit(solution)/shard_map/ppermute | solution.py:33
  693.1 11.6 %collective-permute-done.33 = f32[832,64]{1,0:T(8,128)S(1)} collective-permute-done((f32[832,64]{1,0:T(8,128)S(1)}, f32[832,64]{1,0:T(8,128)S(1)}, u32[]{:S(2)}, u32[]{:S(2)}) %collective-permute-start.33) | collective-permute-done | bytes 213024 | tf_op jit(solution)/shard_map/ppermute | solution.py:33
  707.7 2.9 collective-permute-done.34
  711.3 3.2 collective-permute-done.35
  716.7 3.3 collective-permute-done.36
  (780 shorter events, 391.1 us)
Async XLA Ops:
  0.6 27.2 %copy-start = (bf16[512,2048]{1,0:T(8,128)(2,1)S(1)}, bf16[512,2048]{1,0:T(8,128)(2,1)}, u32[]{:S(2)}) copy-start(bf16[512,2048]{1,0:T(8,128)(2,1)} %param.27) | copy-start | bytes 6291460
  0.6 12.0 %copy-start.54 = (f32[64,256]{1,0:T(8,128)S(1)}, f32[64,256]{1,0:T(8,128)}, u32[]{:S(2)}) copy-start(f32[64,256]{1,0:T(8,128)} %param.29) | copy-start | bytes 196612
  2.1 15.5 %collective-permute-start.2 = (f32[64,64]{1,0:T(8,128)S(1)}, f32[64,64]{1,0:T(8,128)S(1)}, u32[]{:S(2)}, u32[]{:S(2)}) collective-permute-start(f32[64,64]{1,0:T(8,128)S(1)} %fusion.195), channel_id=1, source_target_pairs={{0,1},{1,0},{2,3},{3,2},{4,5},{5,4},{6,7},{7,6},{8,9},{9,8},{10,11... | collective-permute-start | bytes 49160 | tf_op jit(solution)/shard_map/ppermute | solution.py:33
  5.3 75.7 %collective-permute-start.1 = (f32[64,1280]{1,0:T(8,128)}, f32[64,1280]{1,0:T(8,128)}, u32[]{:S(2)}, u32[]{:S(2)}) collective-permute-start(f32[64,1280]{1,0:T(8,128)} %get-tuple-element.680), channel_id=1, source_target_pairs={{8,0},{16,8},{24,16},{32,24},{40,32},{48,40},{56,48},{64,56},{72,6... | collective-permute-start | bytes 983048 | tf_op jit(solution)/shard_map/ppermute | solution.py:19
  10.6 56.9 %collective-permute-start = (f32[64,1280]{1,0:T(8,128)}, f32[64,1280]{1,0:T(8,128)}, u32[]{:S(2)}, u32[]{:S(2)}) collective-permute-start(f32[64,1280]{1,0:T(8,128)} %get-tuple-element.681), channel_id=1, source_target_pairs={{0,8},{8,16},{16,24},{24,32},{32,40},{40,48},{48,56},{56,64},{64,7... | collective-permute-start | bytes 983048 | tf_op jit(solution)/shard_map/ppermute | solution.py:19
  14.8 4.4 copy-start.60
  14.8 13.0 %copy-start.47 = (f32[512,64]{0,1:T(8,128)S(1)}, f32[512,64]{0,1:T(8,128)}, u32[]{:S(2)}) copy-start(f32[512,64]{0,1:T(8,128)} %param.28) | copy-start | bytes 393220
  17.6 4.0 collective-permute-start.3
  21.6 5.4 collective-permute-start.4
  27.8 39.6 %copy-start.58 = (f32[64]{0:T(128)}, f32[64]{0:T(128)S(1)}, u32[]{:S(2)}) copy-start(f32[64]{0:T(128)S(1)} %add_rsqrt_fusion.2) | copy-start | bytes 772
  28.4 10.2 %collective-permute-start.5 = (f32[64,2048]{1,0:T(8,128)S(1)}, f32[64,2048]{1,0:T(8,128)S(1)}, u32[]{:S(2)}, u32[]{:S(2)}) collective-permute-start(f32[64,2048]{1,0:T(8,128)S(1)} %fusion.137), channel_id=1, source_target_pairs={{0,1},{1,0},{2,3},{3,2},{4,5},{5,4},{6,7},{7,6},{8,9},{9,8},{10,11... | collective-permute-start | bytes 1572872 | tf_op jit(solution)/shard_map/ppermute | solution.py:33
  38.7 10.4 %collective-permute-start.6 = (f32[64,2048]{1,0:T(8,128)S(1)}, f32[64,2048]{1,0:T(8,128)S(1)}, u32[]{:S(2)}, u32[]{:S(2)}) collective-permute-start(f32[64,2048]{1,0:T(8,128)S(1)} %add.358), channel_id=1, source_target_pairs={{0,2},{1,3},{2,0},{3,1},{4,6},{5,7},{6,4},{7,5},{8,10},{9,11},{10,... | collective-permute-start | bytes 1572872 | tf_op jit(solution)/shard_map/ppermute | solution.py:33
  43.3 10.8 %copy-start.55 = (f32[64]{0:T(128)S(1)}, f32[64]{0:T(128)}, u32[]{:S(2)}) copy-start(f32[64]{0:T(128)} %param.32) | copy-start | bytes 772
  43.3 10.8 %copy-start.61 = (f32[64]{0:T(128)S(1)}, f32[64]{0:T(128)}, u32[]{:S(2)}) copy-start(f32[64]{0:T(128)} %param.31) | copy-start | bytes 772
  49.2 19.3 %collective-permute-start.7 = (f32[64,2048]{1,0:T(8,128)S(1)}, f32[64,2048]{1,0:T(8,128)}, u32[]{:S(2)}, u32[]{:S(2)}) collective-permute-start(f32[64,2048]{1,0:T(8,128)S(1)} %add.359), channel_id=1, source_target_pairs={{0,4},{1,5},{2,6},{3,7},{4,0},{5,1},{6,2},{7,3},{8,12},{9,13},{10,... | collective-permute-start | bytes 1572872 | tf_op jit(solution)/shard_map/ppermute | solution.py:33
  54.0 3.6 copy-start.39
  68.5 12.5 %copy-start.46 = (f32[64,2048]{1,0:T(8,128)S(1)}, f32[64,2048]{1,0:T(8,128)}, u32[]{:S(2)}) copy-start(f32[64,2048]{1,0:T(8,128)} %param.30) | copy-start | bytes 1572868
  69.7 15.6 %copy-start.36 = (f32[64,2048]{1,0:T(8,128)}, f32[64,2048]{1,0:T(8,128)S(1)}, u32[]{:S(2)}) copy-start(f32[64,2048]{1,0:T(8,128)S(1)} %add.360) | copy-start | bytes 1572868
  69.7 13.8 %collective-permute-start.8 = (f32[64,1280]{1,0:T(8,128)S(1)}, f32[64,1280]{1,0:T(8,128)S(1)}, u32[]{:S(2)}, u32[]{:S(2)}) collective-permute-start(f32[64,1280]{1,0:T(8,128)S(1)} %get-tuple-element.678), channel_id=1, source_target_pairs={{0,8},{8,16},{16,24},{24,32},{32,40},{40,48},{48,56},{56,64},{64,7... | collective-permute-start | bytes 983048 | tf_op jit(solution)/shard_map/ppermute | solution.py:19
  71.7 13.6 %collective-permute-start.9 = (f32[64,1280]{1,0:T(8,128)S(1)}, f32[64,1280]{1,0:T(8,128)S(1)}, u32[]{:S(2)}, u32[]{:S(2)}) collective-permute-start(f32[64,1280]{1,0:T(8,128)S(1)} %get-tuple-element.679), channel_id=1, source_target_pairs={{8,0},{16,8},{24,16},{32,24},{40,32},{48,40},{56,48},{64,56},{72,6... | collective-permute-start | bytes 983048 | tf_op jit(solution)/shard_map/ppermute | solution.py:19
  101.8 2.4 copy-start.6
  116.7 2.4 copy-start.6
  131.6 2.4 copy-start.6
  146.5 2.4 copy-start.6
  162.9 12.4 %collective-permute-start.10 = (f32[64,1280]{1,0:T(8,128)}, f32[64,1280]{1,0:T(8,128)S(1)}, u32[]{:S(2)}, u32[]{:S(2)}) collective-permute-start(f32[64,1280]{1,0:T(8,128)} %get-tuple-element.674), channel_id=1, source_target_pairs={{0,8},{8,16},{16,24},{24,32},{32,40},{40,48},{48,56},{56,64},{64,7... | collective-permute-start | bytes 983048 | tf_op jit(solution)/shard_map/ppermute | solution.py:19
  164.8 12.0 %collective-permute-start.11 = (f32[64,1280]{1,0:T(8,128)S(1)}, f32[64,1280]{1,0:T(8,128)}, u32[]{:S(2)}, u32[]{:S(2)}) collective-permute-start(f32[64,1280]{1,0:T(8,128)S(1)} %get-tuple-element.675), channel_id=1, source_target_pairs={{8,0},{16,8},{24,16},{32,24},{40,32},{48,40},{56,48},{64,56},{72,6... | collective-permute-start | bytes 983048 | tf_op jit(solution)/shard_map/ppermute | solution.py:19
  180.5 2.4 copy-start.7
  195.4 2.4 copy-start.7
  210.4 2.4 copy-start.7
  225.3 2.4 copy-start.7
  240.2 2.4 copy-start.7
  255.8 14.2 %collective-permute-start.14 = (bf16[64,256]{1,0:T(8,128)(2,1)S(1)}, bf16[64,256]{1,0:T(8,128)(2,1)S(1)}, u32[]{:S(2)}, u32[]{:S(2)}) collective-permute-start(bf16[64,256]{1,0:T(8,128)(2,1)S(1)} %slice.520), channel_id=1, source_target_pairs={{0,8},{8,16},{16,24},{24,32},{32,40},{40,48},{48,56},{56,64},{64,7... | collective-permute-start | bytes 98312 | tf_op jit(solution)/shard_map/ppermute | solution.py:19
  317.4 1.8 collective-permute-start.15
  319.3 11.9 %collective-permute-start.16 = (f32[832,64]{1,0:T(8,128)S(1)}, f32[832,64]{1,0:T(8,128)S(1)}, u32[]{:S(2)}, u32[]{:S(2)}) collective-permute-start(f32[832,64]{1,0:T(8,128)S(1)} %fusion.180), channel_id=1, source_target_pairs={{0,16},{8,24},{16,0},{24,8},{32,48},{40,56},{48,32},{56,40},{64,80... | collective-permute-start | bytes 638984 | tf_op jit(solution)/shard_map/ppermute | solution.py:33
  331.3 12.6 %collective-permute-start.17 = (f32[832,64]{1,0:T(8,128)S(1)}, f32[832,64]{1,0:T(8,128)S(1)}, u32[]{:S(2)}, u32[]{:S(2)}) collective-permute-start(f32[832,64]{1,0:T(8,128)S(1)} %add.368), channel_id=1, source_target_pairs={{0,32},{8,40},{16,48},{24,56},{32,0},{40,8},{48,16},{56,24},{64,96... | collective-permute-start | bytes 638984 | tf_op jit(solution)/shard_map/ppermute | solution.py:33
  344.0 16.0 %collective-permute-start.18 = (f32[832,64]{1,0:T(8,128)S(1)}, f32[832,64]{1,0:T(8,128)S(1)}, u32[]{:S(2)}, u32[]{:S(2)}) collective-permute-start(f32[832,64]{1,0:T(8,128)S(1)} %add.369), channel_id=1, source_target_pairs={{0,64},{8,72},{16,80},{24,88},{32,96},{40,104},{48,112},{56,120},{... | collective-permute-start | bytes 638984 | tf_op jit(solution)/shard_map/ppermute | solution.py:33
  349.4 12.2 %copy-start.48 = (f32[512,64]{0,1:T(8,128)S(1)}, f32[512,64]{0,1:T(8,128)}, u32[]{:S(2)}) copy-start(f32[512,64]{0,1:T(8,128)} %param.28) | copy-start | bytes 393220
  349.4 12.2 %copy-start.59 = (f32[64]{0:T(128)S(1)}, f32[64]{0:T(128)}, u32[]{:S(2)}) copy-start(f32[64]{0:T(128)} %copy-done.58) | copy-start | bytes 772
  350.5 14.5 %copy-start.45 = (f32[64,2048]{1,0:T(8,128)}, f32[64,2048]{1,0:T(8,128)S(1)}, u32[]{:S(2)}) copy-start(f32[64,2048]{1,0:T(8,128)S(1)} %slice.407) | copy-start | bytes 1572868
  350.5 14.5 %collective-permute-start.12 = (f32[64,1280]{1,0:T(8,128)}, f32[64,1280]{1,0:T(8,128)}, u32[]{:S(2)}, u32[]{:S(2)}) collective-permute-start(f32[64,1280]{1,0:T(8,128)} %get-tuple-element.672), channel_id=1, source_target_pairs={{0,8},{8,16},{16,24},{24,32},{32,40},{40,48},{48,56},{56,64},{64,7... | collective-permute-start | bytes 983048 | tf_op jit(solution)/shard_map/ppermute | solution.py:19
  352.4 12.6 %collective-permute-start.13 = (f32[64,1280]{1,0:T(8,128)}, f32[64,1280]{1,0:T(8,128)}, u32[]{:S(2)}, u32[]{:S(2)}) collective-permute-start(f32[64,1280]{1,0:T(8,128)} %get-tuple-element.673), channel_id=1, source_target_pairs={{8,0},{16,8},{24,16},{32,24},{40,32},{48,40},{56,48},{64,56},{72,6... | collective-permute-start | bytes 983048 | tf_op jit(solution)/shard_map/ppermute | solution.py:19
  363.2 14.8 %copy-start.43 = (f32[512,64]{1,0:T(8,128)}, f32[512,64]{1,0:T(8,128)S(1)}, u32[]{:S(2)}) copy-start(f32[512,64]{1,0:T(8,128)S(1)} %slice_subtract_fusion.1) | copy-start | bytes 393220
  363.8 4.0 collective-permute-start.19
  367.8 3.9 collective-permute-start.20
  371.7 5.4 collective-permute-start.21
  378.5 10.1 %copy-start.57 = (s32[16384]{0:T(1024)S(1)}, s32[16384]{0:T(1024)}, u32[]{:S(2)}) copy-start(s32[16384]{0:T(1024)} %copy-done.56) | copy-start | bytes 196612
  378.5 9.3 %collective-permute-start.22 = (f32[64,2048]{1,0:T(8,128)S(1)}, f32[64,2048]{1,0:T(8,128)S(1)}, u32[]{:S(2)}, u32[]{:S(2)}) collective-permute-start(f32[64,2048]{1,0:T(8,128)S(1)} %fusion.130), channel_id=1, source_target_pairs={{0,1},{1,0},{2,3},{3,2},{4,5},{5,4},{6,7},{7,6},{8,9},{9,8},{10,11... | collective-permute-start | bytes 1572872 | tf_op jit(solution)/shard_map/ppermute | solution.py:33
  387.8 14.1 %collective-permute-start.23 = (f32[64,2048]{1,0:T(8,128)S(1)}, f32[64,2048]{1,0:T(8,128)S(1)}, u32[]{:S(2)}, u32[]{:S(2)}) collective-permute-start(f32[64,2048]{1,0:T(8,128)S(1)} %add.376), channel_id=1, source_target_pairs={{0,2},{1,3},{2,0},{3,1},{4,6},{5,7},{6,4},{7,5},{8,10},{9,11},{10,... | collective-permute-start | bytes 1572872 | tf_op jit(solution)/shard_map/ppermute | solution.py:33
  402.1 10.8 %collective-permute-start.24 = (f32[64,2048]{1,0:T(8,128)S(1)}, f32[64,2048]{1,0:T(8,128)S(1)}, u32[]{:S(2)}, u32[]{:S(2)}) collective-permute-start(f32[64,2048]{1,0:T(8,128)S(1)} %add.377), channel_id=1, source_target_pairs={{0,4},{1,5},{2,6},{3,7},{4,0},{5,1},{6,2},{7,3},{8,12},{9,13},{10,... | collective-permute-start | bytes 1572872 | tf_op jit(solution)/shard_map/ppermute | solution.py:33
  412.9 25.7 %copy-start.34 = (f32[64,2048]{1,0:T(8,128)}, f32[64,2048]{1,0:T(8,128)S(1)}, u32[]{:S(2)}) copy-start(f32[64,2048]{1,0:T(8,128)S(1)} %add.378) | copy-start | bytes 1572868
  413.0 25.6 %collective-permute-start.25 = (f32[64,1280]{1,0:T(8,128)S(1)}, f32[64,1280]{1,0:T(8,128)S(1)}, u32[]{:S(2)}, u32[]{:S(2)}) collective-permute-start(f32[64,1280]{1,0:T(8,128)S(1)} %get-tuple-element.676), channel_id=1, source_target_pairs={{0,8},{8,16},{16,24},{24,32},{32,40},{40,48},{48,56},{56,64},{64,7... | collective-permute-start | bytes 983048 | tf_op jit(solution)/shard_map/ppermute | solution.py:19
  414.9 23.7 %collective-permute-start.26 = (f32[64,1280]{1,0:T(8,128)S(1)}, f32[64,1280]{1,0:T(8,128)S(1)}, u32[]{:S(2)}, u32[]{:S(2)}) collective-permute-start(f32[64,1280]{1,0:T(8,128)S(1)} %get-tuple-element.677), channel_id=1, source_target_pairs={{8,0},{16,8},{24,16},{32,24},{40,32},{48,40},{56,48},{64,56},{72,6... | collective-permute-start | bytes 983048 | tf_op jit(solution)/shard_map/ppermute | solution.py:19
  516.1 12.2 %collective-permute-start.27 = (f32[64,1280]{1,0:T(8,128)}, f32[64,1280]{1,0:T(8,128)S(1)}, u32[]{:S(2)}, u32[]{:S(2)}) collective-permute-start(f32[64,1280]{1,0:T(8,128)} %get-tuple-element.670), channel_id=1, source_target_pairs={{0,8},{8,16},{16,24},{24,32},{32,40},{40,48},{48,56},{56,64},{64,7... | collective-permute-start | bytes 983048 | tf_op jit(solution)/shard_map/ppermute | solution.py:19
  518.0 11.8 %collective-permute-start.28 = (f32[64,1280]{1,0:T(8,128)S(1)}, f32[64,1280]{1,0:T(8,128)}, u32[]{:S(2)}, u32[]{:S(2)}) collective-permute-start(f32[64,1280]{1,0:T(8,128)S(1)} %get-tuple-element.671), channel_id=1, source_target_pairs={{8,0},{16,8},{24,16},{32,24},{40,32},{48,40},{56,48},{64,56},{72,6... | collective-permute-start | bytes 983048 | tf_op jit(solution)/shard_map/ppermute | solution.py:19
  533.5 2.4 copy-start.12
  609.5 9.1 %collective-permute-start.29 = (bf16[64,256]{1,0:T(8,128)(2,1)S(1)}, bf16[64,256]{1,0:T(8,128)(2,1)S(1)}, u32[]{:S(2)}, u32[]{:S(2)}) collective-permute-start(bf16[64,256]{1,0:T(8,128)(2,1)S(1)} %slice.540), channel_id=1, source_target_pairs={{0,8},{8,16},{16,24},{24,32},{32,40},{40,48},{48,56},{56,64},{64,7... | collective-permute-start | bytes 98312 | tf_op jit(solution)/shard_map/ppermute | solution.py:19
  666.2 1.8 collective-permute-start.30
  668.1 11.9 %collective-permute-start.31 = (f32[832,64]{1,0:T(8,128)S(1)}, f32[832,64]{1,0:T(8,128)S(1)}, u32[]{:S(2)}, u32[]{:S(2)}) collective-permute-start(f32[832,64]{1,0:T(8,128)S(1)} %fusion.179), channel_id=1, source_target_pairs={{0,16},{8,24},{16,0},{24,8},{32,48},{40,56},{48,32},{56,40},{64,80... | collective-permute-start | bytes 638984 | tf_op jit(solution)/shard_map/ppermute | solution.py:33
  680.1 25.5 %copy-start.44 = (f32[512,64]{1,0:T(8,128)S(1)}, f32[512,64]{1,0:T(8,128)}, u32[]{:S(2)}) copy-start(f32[512,64]{1,0:T(8,128)} %copy-done.43) | copy-start | bytes 393220
  680.1 12.6 %collective-permute-start.32 = (f32[832,64]{1,0:T(8,128)S(1)}, f32[832,64]{1,0:T(8,128)S(1)}, u32[]{:S(2)}, u32[]{:S(2)}) collective-permute-start(f32[832,64]{1,0:T(8,128)S(1)} %add.384), channel_id=1, source_target_pairs={{0,32},{8,40},{16,48},{24,56},{32,0},{40,8},{48,16},{56,24},{64,96... | collective-permute-start | bytes 638984 | tf_op jit(solution)/shard_map/ppermute | solution.py:33
  692.7 12.0 %collective-permute-start.33 = (f32[832,64]{1,0:T(8,128)S(1)}, f32[832,64]{1,0:T(8,128)S(1)}, u32[]{:S(2)}, u32[]{:S(2)}) collective-permute-start(f32[832,64]{1,0:T(8,128)S(1)} %add.385), channel_id=1, source_target_pairs={{0,64},{8,72},{16,80},{24,88},{32,96},{40,104},{48,112},{56,120},{... | collective-permute-start | bytes 638984 | tf_op jit(solution)/shard_map/ppermute | solution.py:33
  706.6 4.0 collective-permute-start.34
  710.6 3.9 collective-permute-start.35
  714.5 5.4 collective-permute-start.36
  (147 other events, 233.9 us)

commit v6 on v4

--- a/solution.py
+++ b/solution.py
@@ -45,13 +45,13 @@
     return jnp.where(hit, 1.0, 0.0).astype(jnp.bfloat16).reshape(tap_span, block_width * block_width)
 
 
-def band_sums_matrix(block_width, tap_span):
-    shape = (block_width, block_width, tap_span)
+def band_sums_matrix(block_width, tap_count, offset):
+    shape = (block_width, block_width, tap_count)
     m = lax.broadcasted_iota(jnp.int32, shape, 0)
     i = lax.broadcasted_iota(jnp.int32, shape, 1)
-    d = lax.broadcasted_iota(jnp.int32, shape, 2)
-    hit = d == i - m + (block_width - 1)
-    return jnp.where(hit, 1.0, 0.0).reshape(block_width * block_width, tap_span)
+    tau = lax.broadcasted_iota(jnp.int32, shape, 2)
+    hit = tau == i - m + block_width * offset
+    return jnp.where(hit, 1.0, 0.0).reshape(block_width * block_width, tap_count)
 
 
 def toeplitz(kernel_taps, block_width, skew):
@@ -75,22 +75,14 @@
     lag_blocks = tap_count // block_width
     extended = code_ext.reshape(atoms_here, block_count + lag_blocks, block_width)
     others_blocks = others.reshape(atoms_here, block_count, block_width)
-    grads = []
+    total = jnp.zeros((atoms_here, tap_count), jnp.float32)
     for offset in range(lag_blocks + 1):
         window = extended[:, lag_blocks - offset : lag_blocks - offset + block_count]
-        grads.append(
-            jnp.einsum(
-                "kbm,kbi->kmi", window, others_blocks, preferred_element_type=jnp.float32, precision=highest
-            )
-        )
-    stacked = jnp.concatenate(grads, axis=0).reshape((lag_blocks + 1) * atoms_here, block_width * block_width)
-    bands = jnp.dot(stacked, band_sums_matrix(block_width, 2 * block_width), precision=lax.Precision.HIGH)
-    bands = bands.reshape(lag_blocks + 1, atoms_here, 2 * block_width)
-    total = jnp.zeros((atoms_here, tap_count + 3 * block_width), jnp.float32)
-    for offset in range(lag_blocks + 1):
-        start = offset * block_width + 1
-        total = total.at[:, start : start + 2 * block_width].add(bands[offset])
-    return total[:, block_width : block_width + tap_count]
+        grad = jnp.einsum(
+            "kbm,kbi->kmi", window, others_blocks, preferred_element_type=jnp.float32, precision=highest
+        ).reshape(atoms_here, block_width * block_width)
+        total = total + jnp.dot(grad, band_sums_matrix(block_width, tap_count, offset), precision=highest)
+    return total
 
 
 def convolve_blocks(matrices, code_rows, before, block_width):

time: 716 us -> 715 us (level)
  matrix products: 258 us -> 276 us
  other arithmetic: 57.1 us -> 39.2 us
  starting transfers between devices: 86.6 us -> 97.5 us
    dot_general x2 -> x6, matrix products: 40.3 us -> 58 us  [lag_sums(): jnp.dot(grad, band_sums_matrix(block_width, tap_count, offset), precision...]
    concatenate x2 -> x0, other arithmetic: 11.3 us -> none  [lag_sums(): jnp.concatenate(grads, axis=0)]
    ppermute x14, starting transfers between devices: 65.3 us -> 72.7 us  [passed_along(): lax.ppermute(value, axis, [(source, source + steps) for source in range(l...]
    unnamed x86 -> x84, local copies, waits for them, and re-layouts: 36.5 us -> 35.7 us
  transfers between devices with their start and end apart: 37 -> 37, of which waited for: 29 -> 28; matrix products, arithmetic and copies ran while one was open for 9% -> 9% of each run, Pallas kernels for 0% -> 0%
where the time goes in v6:
time: 715 us; the launch traced here: 708 us
  matrix products  276 us (39%)
  local copies, waits for them, and re-layouts  148 us (21%)
  waiting for transfers between devices  142 us (20%)
  starting transfers between devices  97.5 us (14%)
  other arithmetic  39.2 us (5%)
    ppermute x23, waiting for transfers between devices, butterfly_sum(): lax.ppermute(value, axis, [(i, i ^ distance) for i in range(count)])  128 us
    dot_general x66, matrix products, convolve_blocks(): jnp.einsum('kbm,kmi->kbi', window, matrix, preferred_element_type=jnp.flo...  84.4 us
    while x280, local copies, waits for them, and re-layouts  77.4 us
    dot_general x60, matrix products, correlate_blocks(): jnp.einsum('kbi,kim->kbm', window, matrix, preferred_element_type=jnp.flo...  77 us
    ppermute x14, starting transfers between devices, passed_along(): lax.ppermute(value, axis, [(source, source + steps) for source in range(l...  72.7 us
    dot_general x6, matrix products, lag_sums(): jnp.dot(grad, band_sums_matrix(block_width, tap_count, offset), precision...  58 us
    unnamed x84, local copies, waits for them, and re-layouts  35.7 us
    dot_general x20, matrix products, mix_atoms(): return jnp.dot(own_gram, rebuilt_part, precision=highest)  27.7 us
  transfers between devices with their start and end apart: 37, of which 28 were waited for; matrix products, arithmetic and copies ran while one was open for 9% of the time, Pallas kernels for 0%

profile of v6, /device:TPU:4, one launch (start us, length us, event | category | flops | bytes accessed | tf_op | source)
XLA Modules:
  0.0 707.5 jit_solution(16656370706751355252)
XLA Ops:
  7.2 7.3 %collective-permute-start.1 = (f32[64,1280]{1,0:T(8,128)}, f32[64,1280]{1,0:T(8,128)}, u32[]{:S(2)}, u32[]{:S(2)}) collective-permute-start(f32[64,1280]{1,0:T(8,128)} %get-tuple-element.611), channel_id=1, source_target_pairs={{8,0},{16,8},{24,16},{32,24},{40,32},{48,40},{56,48},{64,56},{72,6... | collective-permute-start | bytes 983048 | tf_op jit(solution)/shard_map/ppermute | solution.py:19
  18.4 2.7 slice_bitcast_fusion.9
  25.2 3.2 collective-permute-start.4
  34.8 6.5 collective-permute-done.5
  43.9 9.9 %collective-permute-done.6 = f32[64,2048]{1,0:T(8,128)S(1)} collective-permute-done((f32[64,2048]{1,0:T(8,128)S(1)}, f32[64,2048]{1,0:T(8,128)S(1)}, u32[]{:S(2)}, u32[]{:S(2)}) %collective-permute-start.6) | collective-permute-done | bytes 524320 | tf_op jit(solution)/shard_map/ppermute | solution.py:33
  53.9 4.7 collective-permute-start.7
  74.5 7.5 %collective-permute-start.9 = (f32[64,1280]{1,0:T(8,128)S(1)}, f32[64,1280]{1,0:T(8,128)S(1)}, u32[]{:S(2)}, u32[]{:S(2)}) collective-permute-start(f32[64,1280]{1,0:T(8,128)S(1)} %get-tuple-element.610), channel_id=1, source_target_pairs={{8,0},{16,8},{24,16},{32,24},{40,32},{48,40},{56,48},{64,56},{72,6... | collective-permute-start | bytes 983048 | tf_op jit(solution)/shard_map/ppermute | solution.py:19
  87.5 74.7 %while.52 = (s32[]{:T(128)}, f32[64,4608]{1,0:T(8,128)}, bf16[64,4608]{1,0:T(8,128)(2,1)S(1)}, f32[4608]{0:T(1024)S(1)}, f32[64,1]{0,1:T(1,128)S(1)}, /*index=5*...) while((s32[]{:T(128)}, f32[64,4608]{1,0:T(8,128)}, ...), condition=%wide.region_3.4_spmd.clone, body=%wide.region_2.3_spmd.clone.sunk | while | flops 684218880 | bytes 87890792 | solution.py:180
  87.9 2.4 fusion.435
  95.0 2.4 fusion.438
  102.9 2.4 fusion.435
  110.0 2.4 fusion.438
  117.8 2.4 fusion.435
  132.8 2.4 fusion.435
  147.7 2.4 fusion.435
  154.8 2.4 fusion.438
  166.0 7.4 %collective-permute-start.11 = (f32[64,1280]{1,0:T(8,128)S(1)}, f32[64,1280]{1,0:T(8,128)}, u32[]{:S(2)}, u32[]{:S(2)}) collective-permute-start(f32[64,1280]{1,0:T(8,128)S(1)} %get-tuple-element.606), channel_id=1, source_target_pairs={{8,0},{16,8},{24,16},{32,24},{40,32},{48,40},{56,48},{64,56},{72,6... | collective-permute-start | bytes 983048 | tf_op jit(solution)/shard_map/ppermute | solution.py:19
  181.3 74.7 %while.53 = (s32[]{:T(128)}, f32[64,4608]{1,0:T(8,128)}, bf16[64,4608]{1,0:T(8,128)(2,1)S(1)}, f32[4608]{0:T(1024)S(1)}, f32[64,1]{0,1:T(1,128)S(1)}, /*index=5*...) while((s32[]{:T(128)}, f32[64,4608]{1,0:T(8,128)}, ...), condition=%wide.region_5.6_spmd.clone, body=%wide.region_4.5_spmd.clone.sunk | while | flops 684218880 | bytes 87890792 | solution.py:180
  181.8 2.4 fusion.454
  196.7 2.4 fusion.454
  203.8 2.4 fusion.457
  211.7 2.4 fusion.454
  218.8 2.4 fusion.457
  226.6 2.4 fusion.454
  241.5 2.4 fusion.454
  257.2 10.7 %collective-permute-start.14 = (bf16[64,256]{1,0:T(8,128)(2,1)S(1)}, bf16[64,256]{1,0:T(8,128)(2,1)S(1)}, u32[]{:S(2)}, u32[]{:S(2)}) collective-permute-start(bf16[64,256]{1,0:T(8,128)(2,1)S(1)} %slice.370), channel_id=1, source_target_pairs={{0,8},{8,16},{16,24},{24,32},{32,40},{40,48},{48,56},{56,64},{64,7... | collective-permute-start | bytes 98312 | tf_op jit(solution)/shard_map/ppermute | solution.py:19
  281.9 7.1 %fusion.131 = f32[256,64]{0,1:T(8,128)S(1)} fusion(f32[64,128,128]{2,1,0:T(8,128)S(1)} %fusion.208), kind=kOutput, calls=%fused_computation.200 | convolution fusion | flops 3233808384 | bytes 4259840 | tf_op jit(solution)/shard_map/dot_general | solution.py:84
  289.0 13.8 %fusion.176 = f32[256,64]{0,1:T(8,128)S(1)} fusion(f32[256,64]{0,1:T(8,128)S(1)} %fusion.131, f32[64,128,128]{2,1,0:T(8,128)S(1)} %fusion.204), kind=kOutput, calls=%fused_computation.209 | convolution fusion | flops 3238019072 | bytes 4325376 | tf_op jit(solution)/shard_map/dot_general | solution.py:84
  302.8 8.2 %fusion.166 = f32[256,64]{0,1:T(8,128)S(1)} fusion(f32[256,64]{0,1:T(8,128)S(1)} %fusion.176, f32[64,128,128]{2,1,0:T(8,128)S(1)} %fusion.201), kind=kOutput, calls=%fused_computation.207 | convolution fusion | flops 3238019072 | bytes 4325376 | tf_op jit(solution)/shard_map/dot_general | solution.py:84
  313.2 11.8 %collective-permute-done.16 = f32[832,64]{1,0:T(8,128)S(1)} collective-permute-done((f32[832,64]{1,0:T(8,128)S(1)}, f32[832,64]{1,0:T(8,128)S(1)}, u32[]{:S(2)}, u32[]{:S(2)}) %collective-permute-start.16) | collective-permute-done | bytes 213024 | tf_op jit(solution)/shard_map/ppermute | solution.py:33
  325.1 12.5 %collective-permute-done.17 = f32[832,64]{1,0:T(8,128)S(1)} collective-permute-done((f32[832,64]{1,0:T(8,128)S(1)}, f32[832,64]{1,0:T(8,128)S(1)}, u32[]{:S(2)}, u32[]{:S(2)}) %collective-permute-start.17) | collective-permute-done | bytes 213024 | tf_op jit(solution)/shard_map/ppermute | solution.py:33
  337.7 3.5 collective-permute-start.18
  346.2 7.3 %collective-permute-start.13 = (f32[64,1280]{1,0:T(8,128)}, f32[64,1280]{1,0:T(8,128)}, u32[]{:S(2)}, u32[]{:S(2)}) collective-permute-start(f32[64,1280]{1,0:T(8,128)} %get-tuple-element.604), channel_id=1, source_target_pairs={{8,0},{16,8},{24,16},{32,24},{40,32},{48,40},{56,48},{64,56},{72,6... | collective-permute-start | bytes 983048 | tf_op jit(solution)/shard_map/ppermute | solution.py:19
  366.4 4.4 collective-permute-done.21
  374.1 7.4 %collective-permute-done.22 = f32[64,2048]{1,0:T(8,128)S(1)} collective-permute-done((f32[64,2048]{1,0:T(8,128)S(1)}, f32[64,2048]{1,0:T(8,128)S(1)}, u32[]{:S(2)}, u32[]{:S(2)}) %collective-permute-start.22) | collective-permute-done | bytes 524320 | tf_op jit(solution)/shard_map/ppermute | solution.py:33
  385.5 10.4 %collective-permute-done.23 = f32[64,2048]{1,0:T(8,128)S(1)} collective-permute-done((f32[64,2048]{1,0:T(8,128)S(1)}, f32[64,2048]{1,0:T(8,128)S(1)}, u32[]{:S(2)}, u32[]{:S(2)}) %collective-permute-start.23) | collective-permute-done | bytes 524320 | tf_op jit(solution)/shard_map/ppermute | solution.py:33
  398.1 8.7 %collective-permute-done.24 = f32[64,2048]{1,0:T(8,128)S(1)} collective-permute-done((f32[64,2048]{1,0:T(8,128)S(1)}, f32[64,2048]{1,0:T(8,128)S(1)}, u32[]{:S(2)}, u32[]{:S(2)}) %collective-permute-start.24) | collective-permute-done | bytes 524320 | tf_op jit(solution)/shard_map/ppermute | solution.py:33
  408.8 11.2 %collective-permute-start.26 = (f32[64,1280]{1,0:T(8,128)S(1)}, f32[64,1280]{1,0:T(8,128)S(1)}, u32[]{:S(2)}, u32[]{:S(2)}) collective-permute-start(f32[64,1280]{1,0:T(8,128)S(1)} %get-tuple-element.608), channel_id=1, source_target_pairs={{8,0},{16,8},{24,16},{32,24},{40,32},{48,40},{56,48},{64,56},{72,6... | collective-permute-start | bytes 983048 | tf_op jit(solution)/shard_map/ppermute | solution.py:19
  433.4 74.7 %while.54 = (s32[]{:T(128)}, f32[64,4608]{1,0:T(8,128)}, bf16[64,4608]{1,0:T(8,128)(2,1)S(1)}, f32[4608]{0:T(1024)S(1)}, f32[64,1]{0,1:T(1,128)S(1)}, /*index=5*...) while((s32[]{:T(128)}, f32[64,4608]{1,0:T(8,128)}, ...), condition=%wide.region_8.9_spmd.clone, body=%wide.region_7.8_spmd.clone.sunk | while | flops 684218880 | bytes 87890792 | solution.py:180
  433.8 2.4 fusion.473
  448.8 2.4 fusion.473
  455.9 2.4 fusion.476
  463.7 2.4 fusion.473
  478.7 2.4 fusion.473
  493.6 2.4 fusion.473
  500.7 2.4 fusion.476
  511.2 7.5 %collective-permute-start.28 = (f32[64,1280]{1,0:T(8,128)S(1)}, f32[64,1280]{1,0:T(8,128)S(1)}, u32[]{:S(2)}, u32[]{:S(2)}) collective-permute-start(f32[64,1280]{1,0:T(8,128)S(1)} %get-tuple-element.602), channel_id=1, source_target_pairs={{8,0},{16,8},{24,16},{32,24},{40,32},{48,40},{56,48},{64,56},{72,6... | collective-permute-start | bytes 983048 | tf_op jit(solution)/shard_map/ppermute | solution.py:19
  524.2 74.7 %while.55 = (s32[]{:T(128)}, f32[64,4608]{1,0:T(8,128)}, bf16[64,4608]{1,0:T(8,128)(2,1)S(1)}, f32[4608]{0:T(1024)S(1)}, f32[64,1]{0,1:T(1,128)S(1)}, /*index=5*...) while((s32[]{:T(128)}, f32[64,4608]{1,0:T(8,128)}, ...), condition=%wide.region_10.11_spmd.clone, body=%wide.region_9.10_spmd.clone.sunk | while | flops 684218880 | bytes 87890792 | solution.py:180
  524.7 2.4 fusion.492
  539.6 2.4 fusion.492
  554.5 2.4 fusion.492
  561.7 2.4 fusion.495
  569.5 2.4 fusion.492
  584.4 2.4 fusion.492
  604.0 5.8 collective-permute-done.29
  623.1 7.1 %fusion.136 = f32[256,64]{0,1:T(8,128)S(1)} fusion(f32[64,128,128]{2,1,0:T(8,128)S(1)} %fusion.198), kind=kOutput, calls=%fused_computation.201 | convolution fusion | flops 3233808384 | bytes 4259840 | tf_op jit(solution)/shard_map/dot_general | solution.py:84
  630.2 13.6 %fusion.171 = f32[256,64]{0,1:T(8,128)S(1)} fusion(f32[256,64]{0,1:T(8,128)S(1)} %fusion.136, f32[64,128,128]{2,1,0:T(8,128)S(1)} %fusion.194), kind=kOutput, calls=%fused_computation.208 | convolution fusion | flops 3238019072 | bytes 4325376 | tf_op jit(solution)/shard_map/dot_general | solution.py:84
  643.8 8.2 %fusion.161 = f32[256,64]{0,1:T(8,128)S(1)} fusion(f32[256,64]{0,1:T(8,128)S(1)} %fusion.171, f32[64,128,128]{2,1,0:T(8,128)S(1)} %fusion.191), kind=kOutput, calls=%fused_computation.206 | convolution fusion | flops 3238019072 | bytes 4325376 | tf_op jit(solution)/shard_map/dot_general | solution.py:84
  654.2 11.8 %collective-permute-done.31 = f32[832,64]{1,0:T(8,128)S(1)} collective-permute-done((f32[832,64]{1,0:T(8,128)S(1)}, f32[832,64]{1,0:T(8,128)S(1)}, u32[]{:S(2)}, u32[]{:S(2)}) %collective-permute-start.31) | collective-permute-done | bytes 213024 | tf_op jit(solution)/shard_map/ppermute | solution.py:33
  666.2 12.5 %collective-permute-done.32 = f32[832,64]{1,0:T(8,128)S(1)} collective-permute-done((f32[832,64]{1,0:T(8,128)S(1)}, f32[832,64]{1,0:T(8,128)S(1)}, u32[]{:S(2)}, u32[]{:S(2)}) %collective-permute-start.32) | collective-permute-done | bytes 213024 | tf_op jit(solution)/shard_map/ppermute | solution.py:33
  678.8 11.6 %collective-permute-done.33 = f32[832,64]{1,0:T(8,128)S(1)} collective-permute-done((f32[832,64]{1,0:T(8,128)S(1)}, f32[832,64]{1,0:T(8,128)S(1)}, u32[]{:S(2)}, u32[]{:S(2)}) %collective-permute-start.33) | collective-permute-done | bytes 213024 | tf_op jit(solution)/shard_map/ppermute | solution.py:33
  692.9 3.4 collective-permute-done.34
  697.6 2.6 collective-permute-done.35
  701.5 4.1 collective-permute-done.36
  (760 shorter events, 380.7 us)
Async XLA Ops:
  0.6 30.8 %copy-start = (bf16[512,2048]{1,0:T(8,128)(2,1)S(1)}, bf16[512,2048]{1,0:T(8,128)(2,1)}, u32[]{:S(2)}) copy-start(bf16[512,2048]{1,0:T(8,128)(2,1)} %param.15) | copy-start | bytes 6291460
  2.0 19.1 %collective-permute-start.2 = (f32[64,64]{1,0:T(8,128)S(1)}, f32[64,64]{1,0:T(8,128)S(1)}, u32[]{:S(2)}, u32[]{:S(2)}) collective-permute-start(f32[64,64]{1,0:T(8,128)S(1)} %fusion.292), channel_id=1, source_target_pairs={{0,1},{1,0},{2,3},{3,2},{4,5},{5,4},{6,7},{7,6},{8,9},{9,8},{10,11... | collective-permute-start | bytes 49160 | tf_op jit(solution)/shard_map/ppermute | solution.py:33
  5.3 65.0 %collective-permute-start = (f32[64,1280]{1,0:T(8,128)}, f32[64,1280]{1,0:T(8,128)}, u32[]{:S(2)}, u32[]{:S(2)}) collective-permute-start(f32[64,1280]{1,0:T(8,128)} %get-tuple-element.612), channel_id=1, source_target_pairs={{0,8},{8,16},{16,24},{24,32},{32,40},{40,48},{48,56},{56,64},{64,7... | collective-permute-start | bytes 983048 | tf_op jit(solution)/shard_map/ppermute | solution.py:19
  7.2 74.9 %collective-permute-start.1 = (f32[64,1280]{1,0:T(8,128)}, f32[64,1280]{1,0:T(8,128)}, u32[]{:S(2)}, u32[]{:S(2)}) collective-permute-start(f32[64,1280]{1,0:T(8,128)} %get-tuple-element.611), channel_id=1, source_target_pairs={{8,0},{16,8},{24,16},{32,24},{40,32},{48,40},{56,48},{64,56},{72,6... | collective-permute-start | bytes 983048 | tf_op jit(solution)/shard_map/ppermute | solution.py:19
  14.5 18.4 %copy-start.53 = (s32[16384]{0:T(1024)}, s32[16384]{0:T(1024)S(1)}, u32[]{:S(2)}) copy-start(s32[16384]{0:T(1024)S(1)} %add_bitcast_fusion) | copy-start | bytes 196612
  18.4 4.4 copy-start.57
  18.4 13.0 %copy-start.46 = (f32[512,64]{0,1:T(8,128)S(1)}, f32[512,64]{0,1:T(8,128)}, u32[]{:S(2)}) copy-start(f32[512,64]{0,1:T(8,128)} %param.16) | copy-start | bytes 393220
  21.2 4.0 collective-permute-start.3
  25.2 5.4 collective-permute-start.4
  31.5 38.7 %copy-start.55 = (f32[64]{0:T(128)}, f32[64]{0:T(128)S(1)}, u32[]{:S(2)}) copy-start(f32[64]{0:T(128)S(1)} %add_rsqrt_fusion.2) | copy-start | bytes 772
  32.0 9.3 %collective-permute-start.5 = (f32[64,2048]{1,0:T(8,128)S(1)}, f32[64,2048]{1,0:T(8,128)S(1)}, u32[]{:S(2)}, u32[]{:S(2)}) collective-permute-start(f32[64,2048]{1,0:T(8,128)S(1)} %fusion.218), channel_id=1, source_target_pairs={{0,1},{1,0},{2,3},{3,2},{4,5},{5,4},{6,7},{7,6},{8,9},{9,8},{10,11... | collective-permute-start | bytes 1572872 | tf_op jit(solution)/shard_map/ppermute | solution.py:33
  41.3 12.5 %collective-permute-start.6 = (f32[64,2048]{1,0:T(8,128)S(1)}, f32[64,2048]{1,0:T(8,128)S(1)}, u32[]{:S(2)}, u32[]{:S(2)}) collective-permute-start(f32[64,2048]{1,0:T(8,128)S(1)} %add.336), channel_id=1, source_target_pairs={{0,2},{1,3},{2,0},{3,1},{4,6},{5,7},{6,4},{7,5},{8,10},{9,11},{10,... | collective-permute-start | bytes 1572872 | tf_op jit(solution)/shard_map/ppermute | solution.py:33
  43.2 15.4 %copy-start.50 = (f32[64]{0:T(128)S(1)}, f32[64]{0:T(128)}, u32[]{:S(2)}) copy-start(f32[64]{0:T(128)} %param.20) | copy-start | bytes 772
  43.2 15.4 %copy-start.58 = (f32[64]{0:T(128)S(1)}, f32[64]{0:T(128)}, u32[]{:S(2)}) copy-start(f32[64]{0:T(128)} %param.19) | copy-start | bytes 772
  43.2 15.4 %copy-start.40 = (bf16[8,8,128,128]{3,1,2,0:T(8,128)(2,1)S(1)}, bf16[8,8,128,128]{3,1,2,0:T(8,128)(2,1)}, u32[]{:S(2)}) copy-start(bf16[8,8,128,128]{3,1,2,0:T(8,128)(2,1)} %get-tuple-element.600) | copy-start | bytes 6291460
  53.9 6.6 copy-start.45
  53.9 17.4 %collective-permute-start.7 = (f32[64,2048]{1,0:T(8,128)S(1)}, f32[64,2048]{1,0:T(8,128)}, u32[]{:S(2)}, u32[]{:S(2)}) collective-permute-start(f32[64,2048]{1,0:T(8,128)S(1)} %add.337), channel_id=1, source_target_pairs={{0,4},{1,5},{2,6},{3,7},{4,0},{5,1},{6,2},{7,3},{8,12},{9,13},{10,... | collective-permute-start | bytes 1572872 | tf_op jit(solution)/shard_map/ppermute | solution.py:33
  70.2 11.9 %copy-start.44 = (f32[64,2048]{1,0:T(8,128)S(1)}, f32[64,2048]{1,0:T(8,128)}, u32[]{:S(2)}) copy-start(f32[64,2048]{1,0:T(8,128)} %param.18) | copy-start | bytes 1572868
  72.6 13.8 %copy-start.36 = (f32[64,2048]{1,0:T(8,128)}, f32[64,2048]{1,0:T(8,128)S(1)}, u32[]{:S(2)}) copy-start(f32[64,2048]{1,0:T(8,128)S(1)} %add.338) | copy-start | bytes 1572868
  72.6 12.0 %collective-permute-start.8 = (f32[64,1280]{1,0:T(8,128)S(1)}, f32[64,1280]{1,0:T(8,128)S(1)}, u32[]{:S(2)}, u32[]{:S(2)}) collective-permute-start(f32[64,1280]{1,0:T(8,128)S(1)} %get-tuple-element.609), channel_id=1, source_target_pairs={{0,8},{8,16},{16,24},{24,32},{32,40},{40,48},{48,56},{56,64},{64,7... | collective-permute-start | bytes 983048 | tf_op jit(solution)/shard_map/ppermute | solution.py:19
  74.5 11.8 %collective-permute-start.9 = (f32[64,1280]{1,0:T(8,128)S(1)}, f32[64,1280]{1,0:T(8,128)S(1)}, u32[]{:S(2)}, u32[]{:S(2)}) collective-permute-start(f32[64,1280]{1,0:T(8,128)S(1)} %get-tuple-element.610), channel_id=1, source_target_pairs={{8,0},{16,8},{24,16},{32,24},{40,32},{48,40},{56,48},{64,56},{72,6... | collective-permute-start | bytes 983048 | tf_op jit(solution)/shard_map/ppermute | solution.py:19
  87.9 2.4 copy-start.6
  102.9 2.4 copy-start.6
  117.8 2.4 copy-start.6
  147.7 2.4 copy-start.6
  164.1 12.4 %collective-permute-start.10 = (f32[64,1280]{1,0:T(8,128)}, f32[64,1280]{1,0:T(8,128)S(1)}, u32[]{:S(2)}, u32[]{:S(2)}) collective-permute-start(f32[64,1280]{1,0:T(8,128)} %get-tuple-element.605), channel_id=1, source_target_pairs={{0,8},{8,16},{16,24},{24,32},{32,40},{40,48},{48,56},{56,64},{64,7... | collective-permute-start | bytes 983048 | tf_op jit(solution)/shard_map/ppermute | solution.py:19
  166.0 12.0 %collective-permute-start.11 = (f32[64,1280]{1,0:T(8,128)S(1)}, f32[64,1280]{1,0:T(8,128)}, u32[]{:S(2)}, u32[]{:S(2)}) collective-permute-start(f32[64,1280]{1,0:T(8,128)S(1)} %get-tuple-element.606), channel_id=1, source_target_pairs={{8,0},{16,8},{24,16},{32,24},{40,32},{48,40},{56,48},{64,56},{72,6... | collective-permute-start | bytes 983048 | tf_op jit(solution)/shard_map/ppermute | solution.py:19
  181.8 2.4 copy-start.7
  211.7 2.4 copy-start.7
  257.2 11.5 %collective-permute-start.14 = (bf16[64,256]{1,0:T(8,128)(2,1)S(1)}, bf16[64,256]{1,0:T(8,128)(2,1)S(1)}, u32[]{:S(2)}, u32[]{:S(2)}) collective-permute-start(bf16[64,256]{1,0:T(8,128)(2,1)S(1)} %slice.370), channel_id=1, source_target_pairs={{0,8},{8,16},{16,24},{24,32},{32,40},{40,48},{48,56},{56,64},{64,7... | collective-permute-start | bytes 98312 | tf_op jit(solution)/shard_map/ppermute | solution.py:19
  311.2 1.8 collective-permute-start.15
  313.1 11.9 %collective-permute-start.16 = (f32[832,64]{1,0:T(8,128)S(1)}, f32[832,64]{1,0:T(8,128)S(1)}, u32[]{:S(2)}, u32[]{:S(2)}) collective-permute-start(f32[832,64]{1,0:T(8,128)S(1)} %fusion.277), channel_id=1, source_target_pairs={{0,16},{8,24},{16,0},{24,8},{32,48},{40,56},{48,32},{56,40},{64,80... | collective-permute-start | bytes 638984 | tf_op jit(solution)/shard_map/ppermute | solution.py:33
  325.0 12.6 %collective-permute-start.17 = (f32[832,64]{1,0:T(8,128)S(1)}, f32[832,64]{1,0:T(8,128)S(1)}, u32[]{:S(2)}, u32[]{:S(2)}) collective-permute-start(f32[832,64]{1,0:T(8,128)S(1)} %add.348), channel_id=1, source_target_pairs={{0,32},{8,40},{16,48},{24,56},{32,0},{40,8},{48,16},{56,24},{64,96... | collective-permute-start | bytes 638984 | tf_op jit(solution)/shard_map/ppermute | solution.py:33
  337.7 17.4 %copy-start.47 = (f32[512,64]{0,1:T(8,128)S(1)}, f32[512,64]{0,1:T(8,128)}, u32[]{:S(2)}) copy-start(f32[512,64]{0,1:T(8,128)} %param.16) | copy-start | bytes 393220
  337.7 17.3 %copy-start.56 = (f32[64]{0:T(128)S(1)}, f32[64]{0:T(128)}, u32[]{:S(2)}) copy-start(f32[64]{0:T(128)} %copy-done.55) | copy-start | bytes 772
  337.7 15.7 %collective-permute-start.18 = (f32[832,64]{1,0:T(8,128)S(1)}, f32[832,64]{1,0:T(8,128)S(1)}, u32[]{:S(2)}, u32[]{:S(2)}) collective-permute-start(f32[832,64]{1,0:T(8,128)S(1)} %add.349), channel_id=1, source_target_pairs={{0,64},{8,72},{16,80},{24,88},{32,96},{40,104},{48,112},{56,120},{... | collective-permute-start | bytes 638984 | tf_op jit(solution)/shard_map/ppermute | solution.py:33
  344.3 16.3 %copy-start.43 = (f32[64,2048]{1,0:T(8,128)}, f32[64,2048]{1,0:T(8,128)S(1)}, u32[]{:S(2)}) copy-start(f32[64,2048]{1,0:T(8,128)S(1)} %slice.269) | copy-start | bytes 1572868
  344.3 14.0 %collective-permute-start.12 = (f32[64,1280]{1,0:T(8,128)}, f32[64,1280]{1,0:T(8,128)}, u32[]{:S(2)}, u32[]{:S(2)}) collective-permute-start(f32[64,1280]{1,0:T(8,128)} %get-tuple-element.603), channel_id=1, source_target_pairs={{0,8},{8,16},{16,24},{24,32},{32,40},{40,48},{48,56},{56,64},{64,7... | collective-permute-start | bytes 983048 | tf_op jit(solution)/shard_map/ppermute | solution.py:19
  346.2 12.2 %collective-permute-start.13 = (f32[64,1280]{1,0:T(8,128)}, f32[64,1280]{1,0:T(8,128)}, u32[]{:S(2)}, u32[]{:S(2)}) collective-permute-start(f32[64,1280]{1,0:T(8,128)} %get-tuple-element.604), channel_id=1, source_target_pairs={{8,0},{16,8},{24,16},{32,24},{40,32},{48,40},{56,48},{64,56},{72,6... | collective-permute-start | bytes 983048 | tf_op jit(solution)/shard_map/ppermute | solution.py:19
  356.7 14.9 %copy-start.41 = (f32[512,64]{1,0:T(8,128)}, f32[512,64]{1,0:T(8,128)S(1)}, u32[]{:S(2)}) copy-start(f32[512,64]{1,0:T(8,128)S(1)} %slice_subtract_fusion.1) | copy-start | bytes 393220
  357.3 4.0 collective-permute-start.19
  361.3 4.1 collective-permute-start.20
  365.4 5.4 collective-permute-start.21
  371.7 11.3 %copy-start.54 = (s32[16384]{0:T(1024)S(1)}, s32[16384]{0:T(1024)}, u32[]{:S(2)}) copy-start(s32[16384]{0:T(1024)} %copy-done.53) | copy-start | bytes 196612
  372.2 9.3 %collective-permute-start.22 = (f32[64,2048]{1,0:T(8,128)S(1)}, f32[64,2048]{1,0:T(8,128)S(1)}, u32[]{:S(2)}, u32[]{:S(2)}) collective-permute-start(f32[64,2048]{1,0:T(8,128)S(1)} %fusion.211), channel_id=1, source_target_pairs={{0,1},{1,0},{2,3},{3,2},{4,5},{5,4},{6,7},{7,6},{8,9},{9,8},{10,11... | collective-permute-start | bytes 1572872 | tf_op jit(solution)/shard_map/ppermute | solution.py:33
  381.5 14.4 %collective-permute-start.23 = (f32[64,2048]{1,0:T(8,128)S(1)}, f32[64,2048]{1,0:T(8,128)S(1)}, u32[]{:S(2)}, u32[]{:S(2)}) collective-permute-start(f32[64,2048]{1,0:T(8,128)S(1)} %add.356), channel_id=1, source_target_pairs={{0,2},{1,3},{2,0},{3,1},{4,6},{5,7},{6,4},{7,5},{8,10},{9,11},{10,... | collective-permute-start | bytes 1572872 | tf_op jit(solution)/shard_map/ppermute | solution.py:33
  384.9 11.2 %copy-start.52 = (s32[16384]{0:T(1024)S(1)}, s32[16384]{0:T(1024)}, u32[]{:S(2)}) copy-start(s32[16384]{0:T(1024)} %copy-done.51) | copy-start | bytes 196612
  396.0 10.8 %collective-permute-start.24 = (f32[64,2048]{1,0:T(8,128)S(1)}, f32[64,2048]{1,0:T(8,128)S(1)}, u32[]{:S(2)}, u32[]{:S(2)}) collective-permute-start(f32[64,2048]{1,0:T(8,128)S(1)} %add.357), channel_id=1, source_target_pairs={{0,4},{1,5},{2,6},{3,7},{4,0},{5,1},{6,2},{7,3},{8,12},{9,13},{10,... | collective-permute-start | bytes 1572872 | tf_op jit(solution)/shard_map/ppermute | solution.py:33
  406.8 25.5 %copy-start.34 = (f32[64,2048]{1,0:T(8,128)}, f32[64,2048]{1,0:T(8,128)S(1)}, u32[]{:S(2)}) copy-start(f32[64,2048]{1,0:T(8,128)S(1)} %add.358) | copy-start | bytes 1572868
  406.9 25.4 %collective-permute-start.25 = (f32[64,1280]{1,0:T(8,128)S(1)}, f32[64,1280]{1,0:T(8,128)S(1)}, u32[]{:S(2)}, u32[]{:S(2)}) collective-permute-start(f32[64,1280]{1,0:T(8,128)S(1)} %get-tuple-element.607), channel_id=1, source_target_pairs={{0,8},{8,16},{16,24},{24,32},{32,40},{40,48},{48,56},{56,64},{64,7... | collective-permute-start | bytes 983048 | tf_op jit(solution)/shard_map/ppermute | solution.py:19
  408.8 23.5 %collective-permute-start.26 = (f32[64,1280]{1,0:T(8,128)S(1)}, f32[64,1280]{1,0:T(8,128)S(1)}, u32[]{:S(2)}, u32[]{:S(2)}) collective-permute-start(f32[64,1280]{1,0:T(8,128)S(1)} %get-tuple-element.608), channel_id=1, source_target_pairs={{8,0},{16,8},{24,16},{32,24},{40,32},{48,40},{56,48},{64,56},{72,6... | collective-permute-start | bytes 983048 | tf_op jit(solution)/shard_map/ppermute | solution.py:19
  493.6 2.4 copy-start.11
  509.2 12.0 %collective-permute-start.27 = (f32[64,1280]{1,0:T(8,128)S(1)}, f32[64,1280]{1,0:T(8,128)S(1)}, u32[]{:S(2)}, u32[]{:S(2)}) collective-permute-start(f32[64,1280]{1,0:T(8,128)S(1)} %get-tuple-element.601), channel_id=1, source_target_pairs={{0,8},{8,16},{16,24},{24,32},{32,40},{40,48},{48,56},{56,64},{64,7... | collective-permute-start | bytes 983048 | tf_op jit(solution)/shard_map/ppermute | solution.py:19
  511.2 11.8 %collective-permute-start.28 = (f32[64,1280]{1,0:T(8,128)S(1)}, f32[64,1280]{1,0:T(8,128)S(1)}, u32[]{:S(2)}, u32[]{:S(2)}) collective-permute-start(f32[64,1280]{1,0:T(8,128)S(1)} %get-tuple-element.602), channel_id=1, source_target_pairs={{8,0},{16,8},{24,16},{32,24},{40,32},{48,40},{56,48},{64,56},{72,6... | collective-permute-start | bytes 983048 | tf_op jit(solution)/shard_map/ppermute | solution.py:19
  554.5 2.4 copy-start.12
  600.8 9.0 %collective-permute-start.29 = (bf16[64,256]{1,0:T(8,128)(2,1)S(1)}, bf16[64,256]{1,0:T(8,128)(2,1)S(1)}, u32[]{:S(2)}, u32[]{:S(2)}) collective-permute-start(bf16[64,256]{1,0:T(8,128)(2,1)S(1)} %slice.385), channel_id=1, source_target_pairs={{0,8},{8,16},{16,24},{24,32},{32,40},{40,48},{48,56},{56,64},{64,7... | collective-permute-start | bytes 98312 | tf_op jit(solution)/shard_map/ppermute | solution.py:19
  652.1 1.8 collective-permute-start.30
  654.0 37.2 %copy-start.42 = (f32[512,64]{1,0:T(8,128)S(1)}, f32[512,64]{1,0:T(8,128)}, u32[]{:S(2)}) copy-start(f32[512,64]{1,0:T(8,128)} %copy-done.41) | copy-start | bytes 393220
  654.1 11.9 %collective-permute-start.31 = (f32[832,64]{1,0:T(8,128)S(1)}, f32[832,64]{1,0:T(8,128)S(1)}, u32[]{:S(2)}, u32[]{:S(2)}) collective-permute-start(f32[832,64]{1,0:T(8,128)S(1)} %fusion.276), channel_id=1, source_target_pairs={{0,16},{8,24},{16,0},{24,8},{32,48},{40,56},{48,32},{56,40},{64,80... | collective-permute-start | bytes 638984 | tf_op jit(solution)/shard_map/ppermute | solution.py:33
  666.1 12.6 %collective-permute-start.32 = (f32[832,64]{1,0:T(8,128)S(1)}, f32[832,64]{1,0:T(8,128)S(1)}, u32[]{:S(2)}, u32[]{:S(2)}) collective-permute-start(f32[832,64]{1,0:T(8,128)S(1)} %add.364), channel_id=1, source_target_pairs={{0,32},{8,40},{16,48},{24,56},{32,0},{40,8},{48,16},{56,24},{64,96... | collective-permute-start | bytes 638984 | tf_op jit(solution)/shard_map/ppermute | solution.py:33
  678.7 11.7 %collective-permute-start.33 = (f32[832,64]{1,0:T(8,128)S(1)}, f32[832,64]{1,0:T(8,128)S(1)}, u32[]{:S(2)}, u32[]{:S(2)}) collective-permute-start(f32[832,64]{1,0:T(8,128)S(1)} %add.365), channel_id=1, source_target_pairs={{0,64},{8,72},{16,80},{24,88},{32,96},{40,104},{48,112},{56,120},{... | collective-permute-start | bytes 638984 | tf_op jit(solution)/shard_map/ppermute | solution.py:33
  692.3 4.0 collective-permute-start.34
  696.3 3.9 collective-permute-start.35
  700.2 5.4 collective-permute-start.36
  (144 other events, 232.4 us)

commit v7 on v6

--- a/solution.py
+++ b/solution.py
@@ -6,7 +6,7 @@
 ITERS = 10
 OUTER = 2
 CHUNK = 5
-GHOST_BLOCKS = 10
+GHOST_BLOCKS = 20
 
 
 epsilon = 1e-06
@@ -125,7 +125,7 @@
 def on_device(signal, spatial, temporal, start_codes, thresholds, step_sizes, breaks):
     chan_rows, seg_len = signal.shape
     atoms_all, tap_count = temporal.shape
-    block_width = 128
+    block_width = 64
     skew = one_hot_skew(block_width, 2 * block_width)
     skew_flipped = one_hot_skew(block_width, 2 * block_width, transposed=True)
     ghost = GHOST_BLOCKS * block_width

time: 715 us -> 1270 us (1.78); the launches traced: 708 us -> 1250 us
  local copies, waits for them, and re-layouts: 148 us -> 546 us
  matrix products: 276 us -> 384 us
  other arithmetic: 39.2 us -> 87.6 us
  starting transfers between devices: 97.5 us -> 82.4 us
    add x0 -> x42, local copies, waits for them, and re-layouts: none -> 122 us  [the longest x20 60.7 us: correlate_blocks(): summed + jnp.einsum('kbi,kim->kbm', window, matrix, preferred_element_typ...]
    reshape x0 -> x44, local copies, waits for them, and re-layouts: none -> 108 us  [the longest x22 62.4 us: convolve_blocks(): return summed.reshape(atoms_here, seg_len)]
    dot_general x66 -> x110, matrix products: 84.4 us -> 137 us  [convolve_blocks(): jnp.einsum('kbm,kmi->kbi', window, matrix, preferred_element_type=jnp.flo...]
    dot_general x60 -> x100, matrix products: 77 us -> 129 us  [correlate_blocks(): jnp.einsum('kbi,kim->kbm', window, matrix, preferred_element_type=jnp.flo...]
    squeeze x0 -> x20, local copies, waits for them, and re-layouts: none -> 48 us  [toeplitz(): return [flat[off] for off in range(lag_blocks + 1)]]
    convert_element_type x20, other arithmetic: 20.4 us -> 64.6 us  [shrink_step(): return (shrunk, shrunk.astype(jnp.bfloat16))]
    concatenate x20, local copies, waits for them, and re-layouts: 0.82 us -> 39.1 us  [convolve_blocks(): jnp.concatenate([before, code_rows], axis=1)]
    reshape x22, local copies, waits for them, and re-layouts: 7.72 us -> 41.5 us  [convolve_blocks(): jnp.concatenate([before, code_rows], axis=1)]
  transfers between devices with their start and end apart: 37 -> 37, of which waited for: 28 -> 27; matrix products, arithmetic and copies ran while one was open for 9% -> 10% of each run, Pallas kernels for 0% -> 0%
where the time goes in v7:
time: 1270 us; the launch traced here: 1250 us
  local copies, waits for them, and re-layouts  546 us (43%)
  matrix products  384 us (30%)
  waiting for transfers between devices  144 us (11%)
  other arithmetic  87.6 us (7%)
  starting transfers between devices  82.4 us (6%)
    dot_general x110, matrix products, convolve_blocks(): jnp.einsum('kbm,kmi->kbi', window, matrix, preferred_element_type=jnp.flo...  137 us
    dot_general x100, matrix products, correlate_blocks(): jnp.einsum('kbi,kim->kbm', window, matrix, preferred_element_type=jnp.flo...  129 us
    ppermute x23, waiting for transfers between devices, butterfly_sum(): lax.ppermute(value, axis, [(i, i ^ distance) for i in range(count)])  123 us
    convert_element_type x20, other arithmetic, shrink_step(): return (shrunk, shrunk.astype(jnp.bfloat16))  64.6 us
    reshape x22, local copies, waits for them, and re-layouts, convolve_blocks(): return summed.reshape(atoms_here, seg_len)  62.4 us
    add x20, local copies, waits for them, and re-layouts, correlate_blocks(): summed + jnp.einsum('kbi,kim->kbm', window, matrix, preferred_element_typ...  60.7 us
    add x20, local copies, waits for them, and re-layouts, convolve_blocks(): summed + jnp.einsum('kbm,kmi->kbi', window, matrix, preferred_element_typ...  60.7 us
    ppermute x14, starting transfers between devices, passed_along(): lax.ppermute(value, axis, [(source, source + steps) for source in range(l...  59 us
  transfers between devices with their start and end apart: 37, of which 27 were waited for; matrix products, arithmetic and copies ran while one was open for 10% of the time, Pallas kernels for 0%

profile of v7, /device:TPU:4, one launch (start us, length us, event | category | flops | bytes accessed | tf_op | source)
XLA Modules:
  0.0 1249.4 jit_solution(992274052604588813)
XLA Ops:
  7.3 7.3 collective-permute-start.1
  20.9 3.2 collective-permute-start.4
  31.4 5.7 collective-permute-done.5
  41.6 7.8 collective-permute-done.6
  50.3 4.6 collective-permute-start.7
  98.1 7.3 collective-permute-start.9
  111.1 197.2 %while.52 = (s32[]{:T(128)}, f32[64,4608]{1,0:T(8,128)}, bf16[64,4608]{1,0:T(8,128)(2,1)}, f32[4608]{0:T(1024)S(1)}, f32[64,1]{0,1:T(1,128)S(1)}, /*index=5*/bf1...) while((s32[]{:T(128)}, f32[64,4608]{1,0:T(8,128)}, ...), condition=%wide.region_3.4_spmd.clone, body=%wide.region_2.3_spmd.clone.sunk | while | flops 609901056 | bytes 92806072 | solution.py:180
  147.6 3.2 fusion.655
  162.6 3.0 copy.550
  181.9 3.0 copy.551
  186.9 3.2 fusion.655
  226.3 3.2 fusion.655
  241.4 3.0 copy.550
  260.6 3.0 copy.551
  265.6 3.2 fusion.655
  305.0 3.2 fusion.655
  311.3 7.4 collective-permute-start.11
  325.4 197.3 %while.53 = (s32[]{:T(128)}, f32[64,4608]{1,0:T(8,128)}, bf16[64,4608]{1,0:T(8,128)(2,1)}, f32[4608]{0:T(1024)S(1)}, f32[64,1]{0,1:T(1,128)S(1)}, /*index=5*/bf1...) while((s32[]{:T(128)}, f32[64,4608]{1,0:T(8,128)}, ...), condition=%wide.region_5.6_spmd.clone, body=%wide.region_4.5_spmd.clone.sunk | while | flops 609901056 | bytes 92806072 | solution.py:180
  337.4 3.0 copy.552
  356.6 3.0 copy.553
  361.6 3.2 fusion.688
  401.0 3.2 fusion.688
  416.1 3.0 copy.552
  435.3 3.0 copy.553
  440.3 3.2 fusion.688
  479.7 3.2 fusion.688
  519.0 3.2 fusion.688
  526.5 6.3 collective-permute-done.14
  558.0 3.1 fusion.169
  561.2 3.4 fusion.254
  564.6 3.2 fusion.244
  567.8 3.6 fusion.234
  571.4 3.2 fusion.224
  577.7 11.8 collective-permute-done.16
  589.7 12.5 %collective-permute-done.17 = f32[832,64]{1,0:T(8,128)S(1)} collective-permute-done((f32[832,64]{1,0:T(8,128)S(1)}, f32[832,64]{1,0:T(8,128)S(1)}, u32[]{:S(2)}, u32[]{:S(2)}) %collective-permute-start.17) | collective-permute-done | bytes 213024 | tf_op jit(solution)/shard_map/ppermute | solution.py:33
  605.2 7.3 collective-permute-start.13
  636.3 6.3 collective-permute-done.22
  645.5 10.0 collective-permute-done.23
  659.0 8.3 collective-permute-done.24
  670.3 7.3 collective-permute-start.26
  729.4 197.1 %while.54 = (s32[]{:T(128)}, f32[64,4608]{1,0:T(8,128)}, bf16[64,4608]{1,0:T(8,128)(2,1)}, f32[4608]{0:T(1024)S(1)}, f32[64,1]{0,1:T(1,128)S(1)}, /*index=5*/bf1...) while((s32[]{:T(128)}, f32[64,4608]{1,0:T(8,128)}, ...), condition=%wide.region_8.9_spmd.clone, body=%wide.region_7.8_spmd.clone.sunk | while | flops 609901056 | bytes 92806072 | solution.py:180
  766.0 3.2 fusion.721
  805.3 3.2 fusion.721
  844.7 3.2 fusion.721
  884.0 3.2 fusion.721
  923.4 3.2 fusion.721
  929.6 7.3 collective-permute-start.28
  943.6 197.3 %while.55 = (s32[]{:T(128)}, f32[64,4608]{1,0:T(8,128)}, bf16[64,4608]{1,0:T(8,128)(2,1)}, f32[4608]{0:T(1024)S(1)}, f32[64,1]{0,1:T(1,128)S(1)}, /*index=5*/bf1...) while((s32[]{:T(128)}, f32[64,4608]{1,0:T(8,128)}, ...), condition=%wide.region_10.11_spmd.clone, body=%wide.region_9.10_spmd.clone.sunk | while | flops 609901056 | bytes 92806072 | solution.py:180
  979.9 3.2 fusion.754
  1019.2 3.2 fusion.754
  1058.6 3.2 fusion.754
  1097.9 3.2 fusion.754
  1137.3 3.2 fusion.754
  1145.5 6.3 collective-permute-done.29
  1177.0 3.1 fusion.174
  1180.2 3.4 fusion.249
  1183.6 3.2 fusion.239
  1186.9 3.4 fusion.229
  1190.3 3.2 fusion.219
  1195.6 11.8 collective-permute-done.31
  1207.6 12.5 %collective-permute-done.32 = f32[832,64]{1,0:T(8,128)S(1)} collective-permute-done((f32[832,64]{1,0:T(8,128)S(1)}, f32[832,64]{1,0:T(8,128)S(1)}, u32[]{:S(2)}, u32[]{:S(2)}) %collective-permute-start.32) | collective-permute-done | bytes 213024 | tf_op jit(solution)/shard_map/ppermute | solution.py:33
  1220.3 11.6 collective-permute-done.33
  1234.7 3.1 collective-permute-done.34
  1243.4 4.1 collective-permute-done.36
  (1091 shorter events, 951.9 us)
Async XLA Ops:
  0.6 26.6 %copy-start = (bf16[512,2048]{1,0:T(8,128)(2,1)S(1)}, bf16[512,2048]{1,0:T(8,128)(2,1)}, u32[]{:S(2)}) copy-start(bf16[512,2048]{1,0:T(8,128)(2,1)} %param.15) | copy-start | bytes 6291460
  2.0 14.9 %collective-permute-start.2 = (f32[64,64]{1,0:T(8,128)S(1)}, f32[64,64]{1,0:T(8,128)S(1)}, u32[]{:S(2)}, u32[]{:S(2)}) collective-permute-start(f32[64,64]{1,0:T(8,128)S(1)} %fusion.404), channel_id=1, source_target_pairs={{0,1},{1,0},{2,3},{3,2},{4,5},{5,4},{6,7},{7,6},{8,9},{9,8},{10,11... | collective-permute-start | bytes 49160 | tf_op jit(solution)/shard_map/ppermute | solution.py:33
  5.3 88.5 %collective-permute-start = (f32[64,1280]{1,0:T(8,128)}, f32[64,1280]{1,0:T(8,128)}, u32[]{:S(2)}, u32[]{:S(2)}) collective-permute-start(f32[64,1280]{1,0:T(8,128)} %get-tuple-element.1068), channel_id=1, source_target_pairs={{0,8},{8,16},{16,24},{24,32},{32,40},{40,48},{48,56},{56,64},{64,7... | collective-permute-start | bytes 983048 | tf_op jit(solution)/shard_map/ppermute | solution.py:19
  7.3 98.2 %collective-permute-start.1 = (f32[64,1280]{1,0:T(8,128)}, f32[64,1280]{1,0:T(8,128)}, u32[]{:S(2)}, u32[]{:S(2)}) collective-permute-start(f32[64,1280]{1,0:T(8,128)} %get-tuple-element.1067), channel_id=1, source_target_pairs={{8,0},{16,8},{24,16},{32,24},{40,32},{48,40},{56,48},{64,56},{72,6... | collective-permute-start | bytes 983048 | tf_op jit(solution)/shard_map/ppermute | solution.py:19
  16.9 4.0 copy-start.78
  16.9 10.3 copy-start.70
  16.9 4.0 collective-permute-start.3
  20.9 5.5 collective-permute-start.4
  24.2 6.3 copy-start.33
  27.3 66.5 %copy-start.82 = (f32[64]{0:T(128)}, f32[64]{0:T(128)S(1)}, u32[]{:S(2)}) copy-start(f32[64]{0:T(128)S(1)} %add_rsqrt_fusion.2) | copy-start | bytes 772
  27.8 9.4 collective-permute-start.5
  38.3 16.6 %copy-start.77 = (f32[64]{0:T(128)S(1)}, f32[64]{0:T(128)}, u32[]{:S(2)}) copy-start(f32[64]{0:T(128)} %param.20) | copy-start | bytes 772
  38.3 16.5 %copy-start.87 = (f32[64]{0:T(128)S(1)}, f32[64]{0:T(128)}, u32[]{:S(2)}) copy-start(f32[64]{0:T(128)} %param.19) | copy-start | bytes 772
  38.3 11.1 collective-permute-start.6
  50.3 44.6 %collective-permute-start.7 = (f32[64,2048]{1,0:T(8,128)}, f32[64,2048]{1,0:T(8,128)}, u32[]{:S(2)}, u32[]{:S(2)}) collective-permute-start(f32[64,2048]{1,0:T(8,128)} %add.425), channel_id=1, source_target_pairs={{0,4},{1,5},{2,6},{3,7},{4,0},{5,1},{6,2},{7,3},{8,12},{9,13},{10,... | collective-permute-start | bytes 1572872 | tf_op jit(solution)/shard_map/ppermute | solution.py:33
  56.9 6.4 copy-start.45
  65.4 6.4 copy-start.47
  73.8 6.4 copy-start.50
  93.7 11.7 copy-start.65
  96.1 13.8 %copy-start.43 = (f32[64,2048]{1,0:T(8,128)}, f32[64,2048]{1,0:T(8,128)S(1)}, u32[]{:S(2)}) copy-start(f32[64,2048]{1,0:T(8,128)S(1)} %add.426) | copy-start | bytes 1572868
  96.2 12.3 collective-permute-start.8
  98.1 11.8 collective-permute-start.9
  309.3 12.2 collective-permute-start.10
  311.3 12.0 collective-permute-start.11
  325.3 200.3 %copy-start.34 = (s32[64]{0:T(128)S(1)}, s32[64]{0:T(128)}, u32[]{:S(2)}) copy-start(s32[64]{0:T(128)} %copy-done.33) | copy-start | bytes 772
  523.8 9.0 collective-permute-start.14
  538.7 3.8 copy-start.44
  555.7 19.0 %copy-start.66 = (f32[512,64]{1,0:T(8,128)}, f32[512,64]{1,0:T(8,128)S(1)}, u32[]{:S(2)}) copy-start(f32[512,64]{1,0:T(8,128)S(1)} %convolution_bitcast_fusion.5) | copy-start | bytes 393220
  574.8 27.6 %copy-start.37 = (f32[64,4608]{1,0:T(8,128)S(1)}, f32[64,4608]{1,0:T(8,128)}, u32[]{:S(2)}) copy-start(f32[64,4608]{1,0:T(8,128)} %get-tuple-element.392) | copy-start | bytes 3538948
  574.8 1.8 collective-permute-start.15
  577.6 11.9 collective-permute-start.16
  589.6 26.0 %copy-start.83 = (f32[64]{0:T(128)S(1)}, f32[64]{0:T(128)}, u32[]{:S(2)}) copy-start(f32[64]{0:T(128)} %copy-done.82) | copy-start | bytes 772
  589.6 12.6 %collective-permute-start.17 = (f32[832,64]{1,0:T(8,128)S(1)}, f32[832,64]{1,0:T(8,128)S(1)}, u32[]{:S(2)}, u32[]{:S(2)}) collective-permute-start(f32[832,64]{1,0:T(8,128)S(1)} %add.442), channel_id=1, source_target_pairs={{0,32},{8,40},{16,48},{24,56},{32,0},{40,8},{48,16},{56,24},{64,96... | collective-permute-start | bytes 638984 | tf_op jit(solution)/shard_map/ppermute | solution.py:33
  602.3 11.7 collective-permute-start.18
  603.3 23.5 %collective-permute-start.12 = (f32[64,1280]{1,0:T(8,128)}, f32[64,1280]{1,0:T(8,128)}, u32[]{:S(2)}, u32[]{:S(2)}) collective-permute-start(f32[64,1280]{1,0:T(8,128)} %get-tuple-element.1059), channel_id=1, source_target_pairs={{0,8},{8,16},{16,24},{24,32},{32,40},{40,48},{48,56},{56,64},{64,7... | collective-permute-start | bytes 983048 | tf_op jit(solution)/shard_map/ppermute | solution.py:19
  605.2 21.6 %collective-permute-start.13 = (f32[64,1280]{1,0:T(8,128)}, f32[64,1280]{1,0:T(8,128)}, u32[]{:S(2)}, u32[]{:S(2)}) collective-permute-start(f32[64,1280]{1,0:T(8,128)} %get-tuple-element.1060), channel_id=1, source_target_pairs={{8,0},{16,8},{24,16},{32,24},{40,32},{48,40},{56,48},{64,56},{72,6... | collective-permute-start | bytes 983048 | tf_op jit(solution)/shard_map/ppermute | solution.py:19
  618.6 4.0 collective-permute-start.19
  622.6 3.9 collective-permute-start.20
  624.3 4.8 copy-start.61
  624.3 8.5 copy-start.59
  626.6 5.4 collective-permute-start.21
  632.8 94.4 %copy-start.84 = (f32[64]{0:T(128)}, f32[64]{0:T(128)S(1)}, u32[]{:S(2)}) copy-start(f32[64]{0:T(128)S(1)} %add_rsqrt_fusion.1) | copy-start | bytes 772
  633.3 11.2 copy-start.81
  633.3 9.3 collective-permute-start.22
  642.7 12.8 %collective-permute-start.23 = (f32[64,2048]{1,0:T(8,128)S(1)}, f32[64,2048]{1,0:T(8,128)}, u32[]{:S(2)}, u32[]{:S(2)}) collective-permute-start(f32[64,2048]{1,0:T(8,128)S(1)} %add.450), channel_id=1, source_target_pairs={{0,2},{1,3},{2,0},{3,1},{4,6},{5,7},{6,4},{7,5},{8,10},{9,11},{10,... | collective-permute-start | bytes 1572872 | tf_op jit(solution)/shard_map/ppermute | solution.py:33
  656.6 10.8 collective-permute-start.24
  667.4 59.8 %copy-start.41 = (f32[64,2048]{1,0:T(8,128)}, f32[64,2048]{1,0:T(8,128)S(1)}, u32[]{:S(2)}) copy-start(f32[64,2048]{1,0:T(8,128)S(1)} %add.452) | copy-start | bytes 1572868
  668.4 58.9 %collective-permute-start.25 = (f32[64,1280]{1,0:T(8,128)}, f32[64,1280]{1,0:T(8,128)}, u32[]{:S(2)}, u32[]{:S(2)}) collective-permute-start(f32[64,1280]{1,0:T(8,128)} %get-tuple-element.1063), channel_id=1, source_target_pairs={{0,8},{8,16},{16,24},{24,32},{32,40},{40,48},{48,56},{56,64},{64,7... | collective-permute-start | bytes 983048 | tf_op jit(solution)/shard_map/ppermute | solution.py:19
  670.3 57.0 %collective-permute-start.26 = (f32[64,1280]{1,0:T(8,128)}, f32[64,1280]{1,0:T(8,128)}, u32[]{:S(2)}, u32[]{:S(2)}) collective-permute-start(f32[64,1280]{1,0:T(8,128)} %get-tuple-element.1064), channel_id=1, source_target_pairs={{8,0},{16,8},{24,16},{32,24},{40,32},{48,40},{56,48},{64,56},{72,6... | collective-permute-start | bytes 983048 | tf_op jit(solution)/shard_map/ppermute | solution.py:19
  708.3 5.1 copy-start.68
  717.7 5.1 copy-start.67
  927.7 12.0 collective-permute-start.27
  929.6 11.8 collective-permute-start.28
  943.6 201.1 %copy-start.35 = (s32[64]{0:T(128)S(1)}, s32[64]{0:T(128)}, u32[]{:S(2)}) copy-start(s32[64]{0:T(128)} %copy-done.33) | copy-start | bytes 772
  1142.8 9.0 collective-permute-start.29
  1193.6 1.8 collective-permute-start.30
  1195.5 37.3 %copy-start.60 = (f32[512,64]{1,0:T(8,128)S(1)}, f32[512,64]{1,0:T(8,128)}, u32[]{:S(2)}) copy-start(f32[512,64]{1,0:T(8,128)} %copy-done.58) | copy-start | bytes 393220
  1195.5 37.3 %copy-start.85 = (f32[64]{0:T(128)S(1)}, f32[64]{0:T(128)}, u32[]{:S(2)}) copy-start(f32[64]{0:T(128)} %copy-done.84) | copy-start | bytes 772
  1195.5 11.9 collective-permute-start.31
  1207.5 12.6 %collective-permute-start.32 = (f32[832,64]{1,0:T(8,128)S(1)}, f32[832,64]{1,0:T(8,128)S(1)}, u32[]{:S(2)}, u32[]{:S(2)}) collective-permute-start(f32[832,64]{1,0:T(8,128)S(1)} %add.462), channel_id=1, source_target_pairs={{0,32},{8,40},{16,48},{24,56},{32,0},{40,8},{48,16},{56,24},{64,96... | collective-permute-start | bytes 638984 | tf_op jit(solution)/shard_map/ppermute | solution.py:33
  1220.2 11.7 collective-permute-start.33
  1233.8 4.0 collective-permute-start.34
  1237.8 4.3 collective-permute-start.35
  1242.1 5.4 collective-permute-start.36
  (205 other events, 330.3 us)
